TPU v7x, 512 devices: a whole 4x4x16 slice. The times are simulated.
512 devices in a mesh: ang: 64 (over x, z_lo, y), rad: 8 (over z_hi, core).
Axes of the slice: x: 4, y: 4, z: 16 (z_hi: 4, z_lo: 4; z = z_hi * 4 + z_lo), core: 2. Of those that a mesh axis runs over, the one named last changes fastest.
Arguments:
- latent: float32 [704, 16384], P('rad', 'ang'), may hold values from -6 to 6
- stencil: float32 [704, 9], P('rad'), may hold values from 0.05 to 0.3
- bin_width: float32 [704], P('rad'), may hold values from 0.0005 to 0.005
- neighbours: int32 [9, 16384], P(None, 'ang'), may hold values from 0 to 511, as said below
- star_bin: int32 [131072], P('ang'), may hold values from 0 to 702
- star_pixels: int32 [4, 131072], P(None, 'ang'), may hold values from 0 to 255
- star_weights: float32 [4, 131072], P(None, 'ang'), may hold values from 0.05 to 1
- star_frac: float32 [131072], P('ang'), may hold values from 0 to 1
- observed: float32 [131072], P('ang'), may hold values from -8 to 8
- sigma: float32 [131072], P('ang'), may hold values from 0.2 to 1
Outputs:
- predicted: float32 [131072], P('ang')
- gradient: float32 [704, 16384], P('rad', 'ang')
Inputs may be any that keep to these rules, and one draw needn't show every extreme that they name: For pixel n at cycle r and column c of its patch, neighbours[0, n] = (r + 1) * 128 + c, and every neighbours[k, n] lies in frame cycle r, r + 1 or r + 2.
All inputs are finite; a program needn't handle non-finite values.
Results may differ from a plain program's by a relative error of at most 0.00013.
Values sent between devices are 32-bit elements; how exact they have to be, the bound alone decides.
No kernel may reach another device: no remote copies, remote signals or barrier semaphores. Data moves between devices by JAX's collectives and lax.ppermute only.
A program may use at most 64 MiB of HBM per device.

v0:
```python
import jax
import jax.numpy as jnp
from jax import lax
from jax.sharding import PartitionSpec as P

COLS = 128


def extended(cells, sides, width):
    for axis, dim in sides:
        count = lax.axis_size(axis)
        head = lax.slice_in_dim(cells, 0, width, axis=dim)
        tail = lax.slice_in_dim(cells, cells.shape[dim] - width, cells.shape[dim], axis=dim)
        cells = jnp.concatenate(
            [
                lax.ppermute(tail, axis, [(i, (i + 1) % count) for i in range(count)]),
                cells,
                lax.ppermute(head, axis, [((i + 1) % count, i) for i in range(count)]),
            ],
            axis=dim,
        )
    return cells


def prefix(value, axis, join, neutral, backward):
    count, mine = (lax.axis_size(axis), lax.axis_index(axis))
    pieces = lax.all_gather(value, axis)
    if backward:
        pieces = pieces[::-1]
        mine = count - 1 - mine
    so_far = jnp.full_like(value, 0) + jnp.asarray(neutral, value.dtype)

    def hop(position, so_far):
        longer = join(so_far, pieces[position])
        return jnp.where(position < mine, longer, so_far)

    return lax.fori_loop(0, count - 1, hop, so_far)


def add_terms(earlier, later):
    return earlier + later


def on_device(
    latent,
    stencil,
    bin_width,
    neighbours,
    star_bin,
    star_pixels,
    star_weights,
    star_frac,
    observed,
    sigma,
):
    shells, pixels = latent.shape
    cycles = pixels // COLS
    field = latent.reshape(shells, cycles, COLS)
    wide = extended(field, (("ang", 1),), 1).reshape(shells, (cycles + 2) * COLS)
    refined = jnp.zeros((shells, pixels), jnp.float32)
    for offset in range(9):
        refined = refined + stencil[:, offset : offset + 1] * jnp.take(
            wide, neighbours[offset], axis=1
        )
    density = jnp.exp(refined)
    weighted = bin_width[:, None] * density
    first_index = lax.broadcasted_iota(jnp.int32, (shells, shells), 0)
    second_index = lax.broadcasted_iota(jnp.int32, (shells, shells), 1)
    lower_ones = (first_index >= second_index).astype(jnp.float32)
    upper_ones = (first_index <= second_index).astype(jnp.float32)
    running = jnp.dot(
        lower_ones, weighted, precision=lax.Precision.HIGHEST, preferred_element_type=jnp.float32
    )
    totals = running[shells - 1]
    nearer_sum = prefix(totals, "rad", add_terms, jnp.zeros_like(totals), False)
    extinction = (running + nearer_sum[None, :]).reshape(-1)
    shell_start = lax.axis_index("rad") * shells
    corner_places = []
    corner_pixels = []
    corner_bins = []
    corner_factors = []
    for upper_bin in (0, 1):
        global_bin = star_bin + upper_bin
        local_bin = global_bin - shell_start
        inside = (local_bin >= 0) & (local_bin < shells)
        radial = star_frac if upper_bin == 1 else 1.0 - star_frac
        for corner in range(4):
            corner_places.append(jnp.clip(local_bin, 0, shells - 1) * pixels + star_pixels[corner])
            corner_pixels.append(star_pixels[corner])
            corner_bins.append(global_bin)
            corner_factors.append(jnp.where(inside, radial * star_weights[corner], 0.0))
    places = jnp.stack(corner_places)
    factors = jnp.stack(corner_factors)
    partial_value = jnp.sum(factors * jnp.take(extinction, places), axis=0)
    predicted = lax.psum(partial_value, "rad")
    weight_back = (predicted - observed) / (sigma * sigma)
    adjoint = jnp.zeros((shells * pixels,), jnp.float32)
    adjoint = adjoint.at[places.reshape(-1)].add((factors * weight_back[None, :]).reshape(-1))
    adjoint = adjoint.reshape(shells, pixels)
    trailing = jnp.dot(
        upper_ones, adjoint, precision=lax.Precision.HIGHEST, preferred_element_type=jnp.float32
    )
    farther_sum = prefix(trailing[0], "rad", add_terms, jnp.zeros_like(trailing[0]), True)
    sensitivity = (trailing + farther_sum[None, :]) * weighted
    spread = (stencil[:, :, None] * sensitivity[:, None, :]).reshape(shells, 9 * pixels)
    framed = jnp.zeros((shells, (cycles + 2) * COLS), jnp.float32)
    framed = framed.at[:, neighbours.reshape(-1)].add(spread).reshape(shells, cycles + 2, COLS)
    edges = jnp.stack([framed[:, 0], framed[:, cycles + 1]], axis=1)
    returned = extended(edges, (("ang", 1),), 1)
    inner = framed[:, 1 : cycles + 1]
    inner = inner.at[:, 0].add(returned[:, 0]).at[:, cycles - 1].add(returned[:, 3])
    gradient = inner.reshape(shells, pixels)
    return (predicted, gradient)


def solution(mesh):
    return jax.shard_map(
        on_device,
        mesh=mesh,
        in_specs=(
            P("rad", "ang"),
            P("rad", None),
            P("rad"),
            P(None, "ang"),
            P("ang"),
            P(None, "ang"),
            P(None, "ang"),
            P("ang"),
            P("ang"),
            P("ang"),
        ),
        out_specs=(P("ang"), P("rad", "ang")),
        check_vma=False,
    )
```

profile of v0, /device:TPU:1, one launch (start us, length us, event | category | flops | bytes accessed | tf_op | source)
XLA Modules:
  0.0 304.9 jit_solution(1532012230398534735)
XLA Ops:
  0.6 0.0 copy-start.1
  0.6 0.0 copy-start.2
  0.7 1.0 copy.69
  1.7 4.0 %collective-permute-start = (f32[88,1,128]{0,2,1:T(8,128)S(1)}, f32[88,1,128]{0,2,1:T(8,128)S(1)}, u32[]{:S(2)}, u32[]{:S(2)}) collective-permute-start(f32[88,1,128]{0,2,1:T(8,128)S(1)} %get-tuple-element.239), channel_id=1, source_target_pairs={{0,8},{8,16},{16,24},{24,32},{32,40},{40,48},{48,56},{56,64},{64,7... | collective-permute-start | bytes 135176 | tf_op jit(solution)/shard_map/ppermute | solution.py:16
  5.7 9.6 %collective-permute-start.1 = (f32[88,1,128]{0,2,1:T(8,128)S(1)}, f32[88,1,128]{0,2,1:T(8,128)S(1)}, u32[]{:S(2)}, u32[]{:S(2)}) collective-permute-start(f32[88,1,128]{0,2,1:T(8,128)S(1)} %get-tuple-element.240), channel_id=1, source_target_pairs={{8,0},{16,8},{24,16},{32,24},{40,32},{48,40},{56,48},{64,56},{72,6... | collective-permute-start | bytes 135176 | tf_op jit(solution)/shard_map/ppermute | solution.py:18
  15.3 1.0 fusion.31
  16.5 1.0 slice_bitcast_fusion.10
  17.5 0.7 copy.73
  18.3 0.9 fusion.29
  19.2 0.9 fusion.30
  20.2 0.7 fusion.23
  20.9 0.1 stack.89
  21.0 0.1 copy.74
  21.1 0.1 compare_select_fusion
  21.3 0.1 compare_select_fusion.1
  21.4 0.0 copy-done.1
  21.4 0.0 copy-done.2
  21.5 0.1 stack.80
  21.6 0.0 collective-permute-done
  21.6 0.0 collective-permute-done.1
  21.7 0.7 gather_fusion.9
  22.4 0.1 copy.65
  22.5 0.7 gather_fusion.8
  23.2 0.1 copy.64
  23.3 0.7 gather_fusion.7
  24.0 0.1 copy.63
  24.1 0.7 gather_fusion.6
  24.9 0.1 copy.62
  25.0 0.7 gather_fusion.5
  25.7 0.1 copy.61
  25.8 0.7 gather_fusion.4
  26.5 0.1 copy.60
  26.6 0.7 gather_fusion.3
  27.3 0.1 copy.59
  27.4 0.7 gather_fusion.2
  28.1 0.7 gather_fusion.1
  28.9 0.1 copy.57
  29.0 0.1 copy.58
  29.1 0.0 copy-done.6
  29.1 0.2 fusion.4
  29.3 0.2 fusion.16
  29.5 20.9 %all-gather = f32[8,1,256]{2,1,0:T(1,128)S(1)} all-gather(f32[1,1,256]{2,1,0:T(1,128)S(1)} %slice_bitcast_fusion.1), channel_id=1, replica_groups=mesh['ang'=64,'rad'=8] {'rad'}, dimensions={0}, use_global_device_ids=true | all-gather | bytes 9216 | tf_op jit(solution)/shard_map/all_gather | solution.py:27
  50.3 0.3 while.30
  50.8 0.0 copy-start.4
  50.8 0.0 copy-start.5
  50.8 90.5 %gather_fusion = f32[16384]{0:T(1024)S(1)} fusion(f32[22528]{0:T(1024)S(1)} %bitcast.154, s32[16384]{0:T(1024)S(1)} %broadcast_clamp_fusion), kind=kCustom, calls=%fused_computation.9 | custom fusion | bytes 196608 | tf_op jit(solution)/shard_map/jit(_take)/gather | solution.py:94
  141.3 0.0 copy-start.3
  141.4 17.6 %psum.7 = f32[2048]{0:T(1024)S(1)} all-reduce(f32[2048]{0:T(1024)S(1)} %multiply_reduce_fusion), channel_id=1, replica_groups=mesh['ang'=64,'rad'=8] {'rad'}, use_global_device_ids=true, to_apply=%region_3.5 | all-reduce | flops 2048 | bytes 16384 | tf_op jit(solution)/shard_map/psum | solution.py:95
  159.0 0.0 copy-done.4
  159.0 0.0 copy-done.5
  159.0 0.0 copy-start
  159.1 91.7 %scatter_custom_fusion = f32[22528]{0:T(1024)S(1)} fusion(s32[16384]{0:T(1024)S(1)} %bitcast.192, f32[16384]{0:T(1024)S(1)} %bitcast.193, f32[]{:T(128)} %constant.143.clone.1), kind=kCustom, calls=%fused_computation.51 | custom fusion | flops 16384 | bytes 90116 | tf_op jit(solution)/shard_map/scatter-add | solution.py:98
  250.8 0.2 fusion.17
  251.0 25.4 %all-gather.1 = f32[8,1,256]{2,1,0:T(1,128)S(1)} all-gather(f32[1,1,256]{2,1,0:T(1,128)S(1)} %slice_bitcast_fusion), channel_id=1, replica_groups=mesh['ang'=64,'rad'=8] {'rad'}, dimensions={0}, use_global_device_ids=true | all-gather | bytes 9216 | tf_op jit(solution)/shard_map/all_gather | solution.py:27
  276.4 0.4 while.31
  276.8 0.1 copy.66
  276.9 0.0 copy-done.3
  276.9 0.1 broadcast_multiply_fusion
  277.0 14.5 %scatter_custom_fusion.1 = f32[88,512]{0,1:T(8,128)S(1)} fusion(s32[2304]{0:T(1024)S(1)} %fusion.18, f32[2304,88]{1,0:T(8,128)S(1)} %bitcast.167, f32[]{:T(128)} %constant.143.clone.1), kind=kCustom, calls=%fused_computation.21 | custom fusion | flops 202752 | bytes 180228 | tf_op jit(solution)/shard_map/scatter-add | solution.py:107
  291.5 1.9 collective-permute-start.2
  293.5 9.4 %collective-permute-start.3 = (f32[88,1,128]{0,2,1:T(8,128)S(1)}, f32[88,1,128]{0,2,1:T(8,128)S(1)}, u32[]{:S(2)}, u32[]{:S(2)}) collective-permute-start(f32[88,1,128]{0,2,1:T(8,128)S(1)} %get-tuple-element.237), channel_id=1, source_target_pairs={{8,0},{16,8},{24,16},{32,24},{40,32},{48,40},{56,48},{64,56},{72,6... | collective-permute-start | bytes 135176 | tf_op jit(solution)/shard_map/ppermute | solution.py:18
  302.9 0.1 collective-permute-done.2
  303.0 1.2 collective-permute-done.3
  304.2 0.7 copy.68
  (83 shorter events, 0.9 us)
Async XLA Ops:
  0.6 20.8 %copy-start.1 = (s32[2048]{0:T(1024)S(1)}, s32[2048]{0:T(1024)}, u32[]{:S(2)}) copy-start(s32[2048]{0:T(1024)} %param.24) | copy-start | bytes 24580
  0.6 20.8 %copy-start.2 = (f32[2048]{0:T(1024)S(1)}, f32[2048]{0:T(1024)}, u32[]{:S(2)}) copy-start(f32[2048]{0:T(1024)} %param.27) | copy-start | bytes 24580
  1.7 20.0 %collective-permute-start = (f32[88,1,128]{0,2,1:T(8,128)S(1)}, f32[88,1,128]{0,2,1:T(8,128)S(1)}, u32[]{:S(2)}, u32[]{:S(2)}) collective-permute-start(f32[88,1,128]{0,2,1:T(8,128)S(1)} %get-tuple-element.239), channel_id=1, source_target_pairs={{0,8},{8,16},{16,24},{24,32},{32,40},{40,48},{48,56},{56,64},{64,7... | collective-permute-start | bytes 135176 | tf_op jit(solution)/shard_map/ppermute | solution.py:16
  5.7 15.9 %collective-permute-start.1 = (f32[88,1,128]{0,2,1:T(8,128)S(1)}, f32[88,1,128]{0,2,1:T(8,128)S(1)}, u32[]{:S(2)}, u32[]{:S(2)}) collective-permute-start(f32[88,1,128]{0,2,1:T(8,128)S(1)} %get-tuple-element.240), channel_id=1, source_target_pairs={{8,0},{16,8},{24,16},{32,24},{40,32},{48,40},{56,48},{64,56},{72,6... | collective-permute-start | bytes 135176 | tf_op jit(solution)/shard_map/ppermute | solution.py:18
  27.3 1.7 copy-start.6
  50.8 108.2 %copy-start.4 = (f32[2048]{0:T(1024)S(1)}, f32[2048]{0:T(1024)}, u32[]{:S(2)}) copy-start(f32[2048]{0:T(1024)} %param.29) | copy-start | bytes 24580
  50.8 108.2 %copy-start.5 = (f32[2048]{0:T(1024)S(1)}, f32[2048]{0:T(1024)}, u32[]{:S(2)}) copy-start(f32[2048]{0:T(1024)} %param.28) | copy-start | bytes 24580
  141.3 135.6 %copy-start.3 = (f32[88,9]{0,1:T(8,128)S(1)}, f32[88,9]{0,1:T(8,128)}, u32[]{:S(2)}) copy-start(f32[88,9]{0,1:T(8,128)} %param.21) | copy-start | bytes 9508
  159.0 118.0 %copy-start = (f32[2048]{0:T(1024)}, f32[2048]{0:T(1024)S(1)}, u32[]{:S(2)}) copy-start(f32[2048]{0:T(1024)S(1)} %psum.7) | copy-start | bytes 24580
  291.5 11.4 %collective-permute-start.2 = (f32[88,1,128]{0,2,1:T(8,128)S(1)}, f32[88,1,128]{0,2,1:T(8,128)S(1)}, u32[]{:S(2)}, u32[]{:S(2)}) collective-permute-start(f32[88,1,128]{0,2,1:T(8,128)S(1)} %get-tuple-element.238), channel_id=1, source_target_pairs={{0,8},{8,16},{16,24},{24,32},{32,40},{40,48},{48,56},{56,64},{64,7... | collective-permute-start | bytes 135176 | tf_op jit(solution)/shard_map/ppermute | solution.py:16
  293.5 10.7 %collective-permute-start.3 = (f32[88,1,128]{0,2,1:T(8,128)S(1)}, f32[88,1,128]{0,2,1:T(8,128)S(1)}, u32[]{:S(2)}, u32[]{:S(2)}) collective-permute-start(f32[88,1,128]{0,2,1:T(8,128)S(1)} %get-tuple-element.237), channel_id=1, source_target_pairs={{8,0},{16,8},{24,16},{32,24},{40,32},{48,40},{56,48},{64,56},{72,6... | collective-permute-start | bytes 135176 | tf_op jit(solution)/shard_map/ppermute | solution.py:18
where the time goes:
time: 306 us; the launch traced here: 305 us
  other arithmetic  108 us (35%)
  local copies, waits for them, and re-layouts  105 us (34%)
  blocking collectives  63.8 us (21%)
  starting transfers between devices  24.9 us (8%)
    scatter-add x1, other arithmetic, on_device(): adjoint.at[places.reshape(-1)]  91.7 us
    gather x2, local copies, waits for them, and re-layouts, on_device(): partial_value = jnp.sum(factors * jnp.take(extinction, places), axis=0)  90.6 us
    all_gather x2, blocking collectives, prefix(): pieces = lax.all_gather(value, axis)  46.2 us
    ppermute x2, starting transfers between devices, extended(): lax.ppermute(head, axis, [((i + 1) % count, i) for i in range(count)])  19 us
    psum x1, blocking collectives, on_device(): predicted = lax.psum(partial_value, 'rad')  17.6 us
    scatter-add x1, other arithmetic, on_device(): framed.at[:, neighbours.reshape(-1)].add(spread)  14.5 us
    gather x18, local copies, waits for them, and re-layouts, on_device(): jnp.take(wide, neighbours[offset], axis=1)  7.31 us
  transfers between devices with their start and end apart: 4, of which 2 were waited for; matrix products, arithmetic and copies ran while one was open for 2% of the time, Pallas kernels for 0%

commit v1 on v0

v1 whole, which is shorter than its diff:
```python
import jax
import jax.numpy as jnp
from jax import lax
from jax.sharding import PartitionSpec as P

COLS = 128
HIGHEST = lax.Precision.HIGHEST


def ring(value, axis, step):
    count = lax.axis_size(axis)
    return lax.ppermute(value, axis, [(i, (i + step) % count) for i in range(count)])


def on_device(
    latent,
    stencil,
    bin_width,
    neighbours,
    star_bin,
    star_pixels,
    star_weights,
    star_frac,
    observed,
    sigma,
):
    shells, pixels = latent.shape
    taps = neighbours.shape[0]
    frame = pixels + 2 * COLS

    above = ring(latent[:, pixels - COLS :], "ang", 1)
    below = ring(latent[:, :COLS], "ang", -1)
    wide = jnp.concatenate([above, latent, below], axis=1)

    position = lax.broadcasted_iota(jnp.int32, (frame, taps * pixels), 0)
    pick = (position == neighbours.reshape(1, taps * pixels)).astype(jnp.float32)
    picked = jnp.dot(wide, pick, precision=HIGHEST, preferred_element_type=jnp.float32)
    refined = jnp.zeros((shells, pixels), jnp.float32)
    for offset in range(taps):
        refined = refined + stencil[:, offset : offset + 1] * picked[:, offset * pixels : (offset + 1) * pixels]
    density = jnp.exp(refined)
    weighted = bin_width[:, None] * density

    nstars = star_bin.shape[0]
    pixel_id = lax.broadcasted_iota(jnp.int32, (pixels, nstars), 0)
    spread = jnp.zeros((pixels, nstars), jnp.float32)
    for corner in range(star_pixels.shape[0]):
        spread = spread + jnp.where(pixel_id == star_pixels[corner][None, :], star_weights[corner][None, :], 0.0)

    shell_start = lax.axis_index("rad") * shells
    bin_id = shell_start + lax.broadcasted_iota(jnp.int32, (shells, nstars), 0)
    lower = star_bin[None, :]
    radial = jnp.where(bin_id <= lower, 1.0, jnp.where(bin_id == lower + 1, star_frac[None, :], 0.0))

    at_stars = jnp.dot(weighted, spread, precision=HIGHEST, preferred_element_type=jnp.float32)
    partial_value = jnp.sum(radial * at_stars, axis=0)
    predicted = lax.psum(partial_value, "rad")
    weight_back = (predicted - observed) / (sigma * sigma)

    adjoint_sum = lax.dot_general(
        radial * weight_back[None, :],
        spread,
        (((1,), (1,)), ((), ())),
        precision=HIGHEST,
        preferred_element_type=jnp.float32,
    )
    sensitivity = adjoint_sum * weighted

    terms = jnp.concatenate(
        [stencil[:, offset : offset + 1] * sensitivity for offset in range(taps)], axis=1
    )
    framed = lax.dot_general(
        terms, pick, (((1,), (1,)), ((), ())), precision=HIGHEST, preferred_element_type=jnp.float32
    )
    from_before = ring(framed[:, frame - COLS :], "ang", 1)
    from_after = ring(framed[:, :COLS], "ang", -1)
    inner = framed[:, COLS : frame - COLS]
    gradient = jnp.concatenate(
        [inner[:, :COLS] + from_before, inner[:, COLS : pixels - COLS], inner[:, pixels - COLS :] + from_after],
        axis=1,
    )
    return (predicted, gradient)


def solution(mesh):
    return jax.shard_map(
        on_device,
        mesh=mesh,
        in_specs=(
            P("rad", "ang"),
            P("rad", None),
            P("rad"),
            P(None, "ang"),
            P("ang"),
            P(None, "ang"),
            P(None, "ang"),
            P("ang"),
            P("ang"),
            P("ang"),
        ),
        out_specs=(P("ang"), P("rad", "ang")),
        check_vma=False,
    )
```

time: 306 us -> 74.8 us (0.24)
  the two profiles are of different devices: /device:TPU:1 before, /device:TPU:8 now
where the time goes in v1:
time: 74.8 us; the launch traced here: 74.1 us
  blocking collectives  24 us (32%)
  starting transfers between devices  23.1 us (31%)
  matrix products  10.6 us (14%)
  waiting for transfers between devices  8.61 us (12%)
  local copies, waits for them, and re-layouts  4.93 us (7%)
  other arithmetic  2.19 us (3%)
  between operations  0.82 us (1%)
    psum x1, blocking collectives, on_device(): predicted = lax.psum(partial_value, 'rad')  24 us
    ppermute x4, starting transfers between devices, ring(): lax.ppermute(value, axis, [(i, (i + step) % count) for i in range(count)])  23.1 us
    ppermute x4, waiting for transfers between devices, ring(): lax.ppermute(value, axis, [(i, (i + step) % count) for i in range(count)])  8.61 us
    dot_general x1, matrix products, on_device(): lax.dot_general(radial * weight_back[None, :], spread, (((1,), (1,)), (()...  2.9 us
    dot_general x1, matrix products, on_device(): jnp.dot(wide, pick, precision=HIGHEST, preferred_element_type=jnp.float32)  2.73 us
    dot_general x1, matrix products, on_device(): lax.dot_general(terms, pick, (((1,), (1,)), ((), ())), precision=HIGHEST,...  2.56 us
    dot_general x1, matrix products, on_device(): jnp.dot(weighted, spread, precision=HIGHEST, preferred_element_type=jnp.f...  2.39 us
  transfers between devices with their start and end apart: 4, of which 2 were waited for; matrix products, arithmetic and copies ran while one was open for 6% of the time, Pallas kernels for 0%

profile of v1, /device:TPU:8, one launch (start us, length us, event | category | flops | bytes accessed | tf_op | source)
XLA Modules:
  0.0 74.1 jit_solution(17561463417894758028)
XLA Ops:
  0.6 0.8 %fusion.54 = (f32[88,128]{1,0:T(8,128)S(1)}, f32[88,128]{1,0:T(8,128)S(1)}) fusion(f32[88,256]{1,0:T(8,128)} %param.10), kind=kLoop, calls=%fused_computation.95 | loop fusion | bytes 180224 | tf_op jit(solution)/shard_map/slice | solution.py:31
  1.5 3.5 %collective-permute-start = (f32[88,128]{1,0:T(8,128)S(1)}, f32[88,128]{1,0:T(8,128)S(1)}, u32[]{:S(2)}, u32[]{:S(2)}) collective-permute-start(f32[88,128]{1,0:T(8,128)S(1)} %get-tuple-element.4), channel_id=1, source_target_pairs={{0,8},{8,16},{16,24},{24,32},{32,40},{40,48},{48,56},{56,64},{64,7... | collective-permute-start | bytes 135176 | tf_op jit(solution)/shard_map/ppermute | solution.py:12
  4.9 6.2 %collective-permute-start.1 = (f32[88,128]{1,0:T(8,128)S(1)}, f32[88,128]{1,0:T(8,128)S(1)}, u32[]{:S(2)}, u32[]{:S(2)}) collective-permute-start(f32[88,128]{1,0:T(8,128)S(1)} %get-tuple-element.5), channel_id=1, source_target_pairs={{0,504},{8,0},{16,8},{24,16},{32,24},{40,32},{48,40},{56,48},{64,5... | collective-permute-start | bytes 135176 | tf_op jit(solution)/shard_map/ppermute | solution.py:12
  11.1 1.0 %slice_bitcast_fusion.8 = (f32[88]{0:T(128)S(1)}, f32[88]{0:T(128)S(1)}, f32[88]{0:T(128)S(1)}, f32[88]{0:T(128)S(1)}, f32[88]{0:T(128)S(1)}, /*index=5*/f32[88]...) fusion(f32[88,9]{0,1:T(8,128)} %param.11), kind=kLoop, calls=%fused_computation.89 | loop fusion | bytes 6336 | tf_op jit(solution)/shard_map/mul | solution.py:40
  12.1 0.7 broadcast_add_fusion
  12.8 0.9 %fusion.55 = (s32[1,2048]{1,0:T(1,128)S(1)}, s32[1,2048]{1,0:T(1,128)S(1)}, s32[1,2048]{1,0:T(1,128)S(1)}, s32[1,2048]{1,0:T(1,128)S(1)}) fusion(s32[4,2048]{1,0:T(4,128)} %param.15), kind=kLoop, calls=%fused_computation.96 | loop fusion | bytes 65536 | tf_op jit(solution)/shard_map/slice | solution.py:48
  13.7 0.9 %fusion.56 = (f32[1,2048]{1,0:T(1,128)S(1)}, f32[1,2048]{1,0:T(1,128)S(1)}, f32[1,2048]{1,0:T(1,128)S(1)}, f32[1,2048]{1,0:T(1,128)S(1)}) fusion(f32[4,2048]{1,0:T(4,128)} %param.16), kind=kLoop, calls=%fused_computation.97 | loop fusion | bytes 65536 | tf_op jit(solution)/shard_map/slice | solution.py:48
  14.7 0.7 eq.60
  15.4 0.0 copy-start.4
  15.4 0.0 collective-permute-done
  15.4 0.0 collective-permute-done.1
  15.4 2.7 %fusion.1 = f32[88,2304]{1,0:T(8,128)S(1)} fusion(s32[2304]{0:T(1024)S(1)} %eq.60, f32[88,128]{1,0:T(8,128)S(1)} %collective-permute-done.1, f32[88,256]{1,0:T(8,128)} %param.10, f32[88,128]{1,0:T(8,128)S(1)} %collective-permute-done), kind=kOutput, calls=%fused_computation.2 | convolution fusion | flops 1246978048 | bytes 1000448 | tf_op jit(solution)/shard_map/dot_general | solution.py:37
  18.2 0.0 copy-start.1
  18.2 0.0 copy-start.5
  18.2 0.0 copy-done.4
  18.2 0.2 fusion.42
  18.4 0.5 copy-done.1
  18.9 0.0 copy-done.5
  18.9 0.0 copy-start.2
  18.9 0.0 copy-start.3
  18.9 2.4 %fusion.5 = f32[2048]{0:T(1024)S(1)} fusion(f32[88,256]{1,0:T(8,128)S(1)} %fusion.42, f32[2048]{0:T(1024)S(1)} %bitcast.40, s32[2048]{0:T(1024)S(1)} %bitcast.32, f32[2048]{0:T(1024)S(1)} %bitcast.42, s32[2048]{0:T(1024)S(1)} %bitcast.34, f32[2048]{0:T(1024)S(1)} %bitcast.38, s32[2048]{0:T(1024)S(1)} %bitcast.30, f32[2048]{0:T(1024)S(1)} %bitcast.36, ...), kind=kOutput, calls=%fused_computation.12 | convolution fusion | flops 560494592 | bytes 188768 | tf_op jit(solution)/shard_map/dot_general | solution.py:55
  21.3 24.0 %psum.7 = f32[2048]{0:T(1024)S(1)} all-reduce(f32[2048]{0:T(1024)S(1)} %fusion.5), channel_id=1, replica_groups=mesh['ang'=64,'rad'=8] {'rad'}, use_global_device_ids=true, to_apply=%region_1.2 | all-reduce | flops 2048 | bytes 16384 | tf_op jit(solution)/shard_map/psum | solution.py:57
  45.2 0.0 copy-done.2
  45.3 0.0 copy-done.3
  45.3 0.0 copy-start
  45.3 2.9 %multiply_dynamic-update-slice_fusion.8 = (f32[88,2304]{1,0:T(8,128)S(1)}, f32[88,256]{1,0:T(8,128)S(1)}) fusion(f32[88]{0:T(128)S(1)} %get-tuple-element.14, f32[88,256]{1,0:T(8,128)S(1)} %fusion.42, f32[2048]{0:T(1024)S(1)} %bitcast.41, s32[2048]{0:T(1024)S(1)} %bitcast.33, f32[2048]{0:T(1024)S(1)} %bitcast.43, s32[2048]{0:T(1024)S(1)} %bitcast.35, ...), kind=kOutput, calls=%fused_computation.76 | convolution fusion | flops 560361472 | bytes 369344 | tf_op jit(solution)/shard_map/dot_general | solution.py:60
  48.2 0.0 copy-done
  48.2 0.1 multiply_dynamic-update-slice_fusion.7
  48.3 0.1 multiply_dynamic-update-slice_fusion.6
  48.4 0.1 multiply_dynamic-update-slice_fusion.5
  48.5 0.1 multiply_dynamic-update-slice_fusion.4
  48.5 0.1 multiply_dynamic-update-slice_fusion.3
  48.6 0.1 multiply_dynamic-update-slice_fusion.2
  48.7 0.1 multiply_dynamic-update-slice_fusion.1
  48.8 0.1 multiply_dynamic-update-slice_fusion
  48.9 2.6 %fusion = f32[88,512]{1,0:T(8,128)S(1)} fusion(f32[88,2304]{1,0:T(8,128)S(1)} %multiply_dynamic-update-slice_fusion, s32[2304]{0:T(1024)S(1)} %eq.60), kind=kOutput, calls=%fused_computation.1 | convolution fusion | flops 1246887936 | bytes 1000448 | tf_op jit(solution)/shard_map/dot_general | solution.py:72
  51.4 3.5 %collective-permute-start.2 = (f32[88,128]{1,0:T(8,128)S(1)}, f32[88,128]{1,0:T(8,128)S(1)}, u32[]{:S(2)}, u32[]{:S(2)}) collective-permute-start(f32[88,128]{1,0:T(8,128)S(1)} %slice.150), channel_id=1, source_target_pairs={{0,8},{8,16},{16,24},{24,32},{32,40},{40,48},{48,56},{56,64},{64,7... | collective-permute-start | bytes 135176 | tf_op jit(solution)/shard_map/ppermute | solution.py:12
  54.9 6.9 %collective-permute-done.2 = f32[88,128]{1,0:T(8,128)S(1)} collective-permute-done((f32[88,128]{1,0:T(8,128)S(1)}, f32[88,128]{1,0:T(8,128)S(1)}, u32[]{:S(2)}, u32[]{:S(2)}) %collective-permute-start.2) | collective-permute-done | bytes 45088 | tf_op jit(solution)/shard_map/ppermute | solution.py:12
  61.9 9.9 %collective-permute-start.3 = (f32[88,128]{1,0:T(8,128)S(1)}, f32[88,128]{1,0:T(8,128)S(1)}, u32[]{:S(2)}, u32[]{:S(2)}) collective-permute-start(f32[88,128]{1,0:T(8,128)S(1)} %get-tuple-element.3), channel_id=1, source_target_pairs={{0,504},{8,0},{16,8},{24,16},{32,24},{40,32},{48,40},{56,48},{64,5... | collective-permute-start | bytes 135176 | tf_op jit(solution)/shard_map/ppermute | solution.py:12
  71.8 1.7 %collective-permute-done.3 = f32[88,128]{1,0:T(8,128)S(1)} collective-permute-done((f32[88,128]{1,0:T(8,128)S(1)}, f32[88,128]{1,0:T(8,128)S(1)}, u32[]{:S(2)}, u32[]{:S(2)}) %collective-permute-start.3) | collective-permute-done | bytes 45088 | tf_op jit(solution)/shard_map/ppermute | solution.py:12
  73.5 0.6 pad_maximum_fusion
  (5 shorter events, 0.0 us)
Async XLA Ops:
  1.5 14.0 %collective-permute-start = (f32[88,128]{1,0:T(8,128)S(1)}, f32[88,128]{1,0:T(8,128)S(1)}, u32[]{:S(2)}, u32[]{:S(2)}) collective-permute-start(f32[88,128]{1,0:T(8,128)S(1)} %get-tuple-element.4), channel_id=1, source_target_pairs={{0,8},{8,16},{16,24},{24,32},{32,40},{40,48},{48,56},{56,64},{64,7... | collective-permute-start | bytes 135176 | tf_op jit(solution)/shard_map/ppermute | solution.py:12
  4.9 10.5 %collective-permute-start.1 = (f32[88,128]{1,0:T(8,128)S(1)}, f32[88,128]{1,0:T(8,128)S(1)}, u32[]{:S(2)}, u32[]{:S(2)}) collective-permute-start(f32[88,128]{1,0:T(8,128)S(1)} %get-tuple-element.5), channel_id=1, source_target_pairs={{0,504},{8,0},{16,8},{24,16},{32,24},{40,32},{48,40},{56,48},{64,5... | collective-permute-start | bytes 135176 | tf_op jit(solution)/shard_map/ppermute | solution.py:12
  15.4 2.8 %copy-start.4 = (f32[88]{0:T(128)S(1)}, f32[88]{0:T(128)}, u32[]{:S(2)}) copy-start(f32[88]{0:T(128)} %param.12) | copy-start | bytes 1060
  18.2 0.7 copy-start.1
  18.2 0.7 copy-start.5
  18.9 26.4 %copy-start.2 = (f32[2048]{0:T(1024)S(1)}, f32[2048]{0:T(1024)}, u32[]{:S(2)}) copy-start(f32[2048]{0:T(1024)} %param.19) | copy-start | bytes 24580
  18.9 26.4 %copy-start.3 = (f32[2048]{0:T(1024)S(1)}, f32[2048]{0:T(1024)}, u32[]{:S(2)}) copy-start(f32[2048]{0:T(1024)} %param.18) | copy-start | bytes 24580
  45.3 2.9 %copy-start = (f32[2048]{0:T(1024)}, f32[2048]{0:T(1024)S(1)}, u32[]{:S(2)}) copy-start(f32[2048]{0:T(1024)S(1)} %psum.7) | copy-start | bytes 24580
  51.4 10.4 %collective-permute-start.2 = (f32[88,128]{1,0:T(8,128)S(1)}, f32[88,128]{1,0:T(8,128)S(1)}, u32[]{:S(2)}, u32[]{:S(2)}) collective-permute-start(f32[88,128]{1,0:T(8,128)S(1)} %slice.150), channel_id=1, source_target_pairs={{0,8},{8,16},{16,24},{24,32},{32,40},{40,48},{48,56},{56,64},{64,7... | collective-permute-start | bytes 135176 | tf_op jit(solution)/shard_map/ppermute | solution.py:12
  61.9 11.6 %collective-permute-start.3 = (f32[88,128]{1,0:T(8,128)S(1)}, f32[88,128]{1,0:T(8,128)S(1)}, u32[]{:S(2)}, u32[]{:S(2)}) collective-permute-start(f32[88,128]{1,0:T(8,128)S(1)} %get-tuple-element.3), channel_id=1, source_target_pairs={{0,504},{8,0},{16,8},{24,16},{32,24},{40,32},{48,40},{56,48},{64,5... | collective-permute-start | bytes 135176 | tf_op jit(solution)/shard_map/ppermute | solution.py:12

commit v2 on v1

--- a/solution.py
+++ b/solution.py
@@ -10,6 +10,15 @@
 def ring(value, axis, step):
     count = lax.axis_size(axis)
     return lax.ppermute(value, axis, [(i, (i + step) % count) for i in range(count)])
+
+
+def butterfly_sum(value, axis):
+    count = lax.axis_size(axis)
+    distance = 1
+    while distance < count:
+        value = value + lax.ppermute(value, axis, [(i, i ^ distance) for i in range(count)])
+        distance *= 2
+    return value
 
 
 def on_device(
@@ -54,7 +63,7 @@
 
     at_stars = jnp.dot(weighted, spread, precision=HIGHEST, preferred_element_type=jnp.float32)
     partial_value = jnp.sum(radial * at_stars, axis=0)
-    predicted = lax.psum(partial_value, "rad")
+    predicted = butterfly_sum(partial_value, "rad")
     weight_back = (predicted - observed) / (sigma * sigma)
 
     adjoint_sum = lax.dot_general(

time: 74.8 us -> 79.8 us (1.067)
  blocking collectives: 24 us -> 0 us
  starting transfers between devices: 23.1 us -> 41.4 us
  waiting for transfers between devices: 8.61 us -> 18.5 us
    psum x1 -> x0, blocking collectives: 24 us -> none  [on_device(): predicted = lax.psum(partial_value, 'rad')]
    ppermute x0 -> x3, starting transfers between devices: none -> 19.1 us  [butterfly_sum(): lax.ppermute(value, axis, [(i, i ^ distance) for i in range(count)])]
    ppermute x0 -> x3, waiting for transfers between devices: none -> 7.64 us  [butterfly_sum(): lax.ppermute(value, axis, [(i, i ^ distance) for i in range(count)])]
    ppermute x4, waiting for transfers between devices: 8.61 us -> 10.9 us  [ring(): lax.ppermute(value, axis, [(i, (i + step) % count) for i in range(count)])]
  transfers between devices with their start and end apart: 4 -> 7, of which waited for: 2 -> 5; matrix products, arithmetic and copies ran while one was open for 6% -> 5% of each run, Pallas kernels for 0% -> 0%
where the time goes in v2:
time: 79.8 us; the launch traced here: 79 us
  starting transfers between devices  41.4 us (52%)
  waiting for transfers between devices  18.5 us (23%)
  matrix products  10.6 us (13%)
  local copies, waits for them, and re-layouts  4.92 us (6%)
  other arithmetic  2.79 us (3%)
  between operations  0.8 us (1%)
    ppermute x4, starting transfers between devices, ring(): lax.ppermute(value, axis, [(i, (i + step) % count) for i in range(count)])  22.3 us
    ppermute x3, starting transfers between devices, butterfly_sum(): lax.ppermute(value, axis, [(i, i ^ distance) for i in range(count)])  19.1 us
    ppermute x4, waiting for transfers between devices, ring(): lax.ppermute(value, axis, [(i, (i + step) % count) for i in range(count)])  10.9 us
    ppermute x3, waiting for transfers between devices, butterfly_sum(): lax.ppermute(value, axis, [(i, i ^ distance) for i in range(count)])  7.64 us
    dot_general x1, matrix products, on_device(): lax.dot_general(radial * weight_back[None, :], spread, (((1,), (1,)), (()...  2.9 us
    dot_general x1, matrix products, on_device(): jnp.dot(wide, pick, precision=HIGHEST, preferred_element_type=jnp.float32)  2.73 us
    dot_general x1, matrix products, on_device(): lax.dot_general(terms, pick, (((1,), (1,)), ((), ())), precision=HIGHEST,...  2.55 us
    dot_general x1, matrix products, on_device(): jnp.dot(weighted, spread, precision=HIGHEST, preferred_element_type=jnp.f...  2.39 us
  transfers between devices with their start and end apart: 7, of which 5 were waited for; matrix products, arithmetic and copies ran while one was open for 5% of the time, Pallas kernels for 0%

profile of v2, /device:TPU:8, one launch (start us, length us, event | category | flops | bytes accessed | tf_op | source)
XLA Modules:
  0.0 79.0 jit_solution(2292991928616731548)
XLA Ops:
  0.6 0.8 %fusion.54 = (f32[88,128]{1,0:T(8,128)S(1)}, f32[88,128]{1,0:T(8,128)S(1)}) fusion(f32[88,256]{1,0:T(8,128)} %param.10), kind=kLoop, calls=%fused_computation.95 | loop fusion | bytes 180224 | tf_op jit(solution)/shard_map/slice | solution.py:40
  1.5 3.5 %collective-permute-start = (f32[88,128]{1,0:T(8,128)S(1)}, f32[88,128]{1,0:T(8,128)S(1)}, u32[]{:S(2)}, u32[]{:S(2)}) collective-permute-start(f32[88,128]{1,0:T(8,128)S(1)} %get-tuple-element.6), channel_id=1, source_target_pairs={{0,8},{8,16},{16,24},{24,32},{32,40},{40,48},{48,56},{56,64},{64,7... | collective-permute-start | bytes 135176 | tf_op jit(solution)/shard_map/ppermute | solution.py:12
  4.9 6.2 %collective-permute-start.1 = (f32[88,128]{1,0:T(8,128)S(1)}, f32[88,128]{1,0:T(8,128)S(1)}, u32[]{:S(2)}, u32[]{:S(2)}) collective-permute-start(f32[88,128]{1,0:T(8,128)S(1)} %get-tuple-element.7), channel_id=1, source_target_pairs={{0,504},{8,0},{16,8},{24,16},{32,24},{40,32},{48,40},{56,48},{64,5... | collective-permute-start | bytes 135176 | tf_op jit(solution)/shard_map/ppermute | solution.py:12
  11.1 1.0 %slice_bitcast_fusion.8 = (f32[88]{0:T(128)S(1)}, f32[88]{0:T(128)S(1)}, f32[88]{0:T(128)S(1)}, f32[88]{0:T(128)S(1)}, f32[88]{0:T(128)S(1)}, /*index=5*/f32[88]...) fusion(f32[88,9]{0,1:T(8,128)} %param.11), kind=kLoop, calls=%fused_computation.89 | loop fusion | bytes 6336 | tf_op jit(solution)/shard_map/mul | solution.py:49
  12.1 0.7 broadcast_add_fusion
  12.8 0.9 %fusion.55 = (s32[1,2048]{1,0:T(1,128)S(1)}, s32[1,2048]{1,0:T(1,128)S(1)}, s32[1,2048]{1,0:T(1,128)S(1)}, s32[1,2048]{1,0:T(1,128)S(1)}) fusion(s32[4,2048]{1,0:T(4,128)} %param.15), kind=kLoop, calls=%fused_computation.96 | loop fusion | bytes 65536 | tf_op jit(solution)/shard_map/slice | solution.py:57
  13.7 0.9 %fusion.56 = (f32[1,2048]{1,0:T(1,128)S(1)}, f32[1,2048]{1,0:T(1,128)S(1)}, f32[1,2048]{1,0:T(1,128)S(1)}, f32[1,2048]{1,0:T(1,128)S(1)}) fusion(f32[4,2048]{1,0:T(4,128)} %param.16), kind=kLoop, calls=%fused_computation.97 | loop fusion | bytes 65536 | tf_op jit(solution)/shard_map/slice | solution.py:57
  14.7 0.7 eq.60
  15.4 0.0 copy-start.3
  15.4 0.0 collective-permute-done
  15.4 0.0 collective-permute-done.1
  15.4 2.7 %fusion.1 = f32[88,2304]{1,0:T(8,128)S(1)} fusion(s32[2304]{0:T(1024)S(1)} %eq.60, f32[88,128]{1,0:T(8,128)S(1)} %collective-permute-done.1, f32[88,256]{1,0:T(8,128)} %param.10, f32[88,128]{1,0:T(8,128)S(1)} %collective-permute-done), kind=kOutput, calls=%fused_computation.2 | convolution fusion | flops 1246978048 | bytes 1000448 | tf_op jit(solution)/shard_map/dot_general | solution.py:46
  18.2 0.0 copy-start
  18.2 0.0 copy-start.4
  18.2 0.0 copy-done.3
  18.2 0.2 fusion.42
  18.4 0.5 copy-done
  18.9 0.0 copy-done.4
  18.9 0.0 copy-start.1
  18.9 0.0 copy-start.2
  18.9 2.4 %fusion.5 = f32[2048]{0:T(1024)S(1)} fusion(f32[88,256]{1,0:T(8,128)S(1)} %fusion.42, f32[2048]{0:T(1024)S(1)} %bitcast.40, s32[2048]{0:T(1024)S(1)} %bitcast.32, f32[2048]{0:T(1024)S(1)} %bitcast.42, s32[2048]{0:T(1024)S(1)} %bitcast.34, f32[2048]{0:T(1024)S(1)} %bitcast.38, s32[2048]{0:T(1024)S(1)} %bitcast.30, f32[2048]{0:T(1024)S(1)} %bitcast.36, ...), kind=kOutput, calls=%fused_computation.12 | convolution fusion | flops 560494592 | bytes 188768 | tf_op jit(solution)/shard_map/dot_general | solution.py:64
  21.3 1.9 %collective-permute-start.2 = (f32[2048]{0:T(1024)S(1)}, f32[2048]{0:T(1024)S(1)}, u32[]{:S(2)}, u32[]{:S(2)}) collective-permute-start(f32[2048]{0:T(1024)S(1)} %fusion.5), channel_id=1, source_target_pairs={{0,1},{1,0},{2,3},{3,2},{4,5},{5,4},{6,7},{7,6},{8,9},{9,8},{10,11... | collective-permute-start | bytes 24584 | tf_op jit(solution)/shard_map/ppermute | solution.py:19
  23.2 1.1 %collective-permute-done.2 = f32[2048]{0:T(1024)S(1)} collective-permute-done((f32[2048]{0:T(1024)S(1)}, f32[2048]{0:T(1024)S(1)}, u32[]{:S(2)}, u32[]{:S(2)}) %collective-permute-start.2) | collective-permute-done | bytes 8224 | tf_op jit(solution)/shard_map/ppermute | solution.py:19
  24.4 5.3 %collective-permute-start.3 = (f32[2048]{0:T(1024)S(1)}, f32[2048]{0:T(1024)S(1)}, u32[]{:S(2)}, u32[]{:S(2)}) collective-permute-start(f32[2048]{0:T(1024)S(1)} %add.77), channel_id=1, source_target_pairs={{0,2},{1,3},{2,0},{3,1},{4,6},{5,7},{6,4},{7,5},{8,10},{9,11},{10,... | collective-permute-start | bytes 24584 | tf_op jit(solution)/shard_map/ppermute | solution.py:19
  29.6 4.2 %collective-permute-done.3 = f32[2048]{0:T(1024)S(1)} collective-permute-done((f32[2048]{0:T(1024)S(1)}, f32[2048]{0:T(1024)S(1)}, u32[]{:S(2)}, u32[]{:S(2)}) %collective-permute-start.3) | collective-permute-done | bytes 8224 | tf_op jit(solution)/shard_map/ppermute | solution.py:19
  33.8 11.9 %collective-permute-start.4 = (f32[2048]{0:T(1024)S(1)}, f32[2048]{0:T(1024)S(1)}, u32[]{:S(2)}, u32[]{:S(2)}) collective-permute-start(f32[2048]{0:T(1024)S(1)} %add.78), channel_id=1, source_target_pairs={{0,4},{1,5},{2,6},{3,7},{4,0},{5,1},{6,2},{7,3},{8,12},{9,13},{10,... | collective-permute-start | bytes 24584 | tf_op jit(solution)/shard_map/ppermute | solution.py:19
  45.7 2.3 %collective-permute-done.4 = f32[2048]{0:T(1024)S(1)} collective-permute-done((f32[2048]{0:T(1024)S(1)}, f32[2048]{0:T(1024)S(1)}, u32[]{:S(2)}, u32[]{:S(2)}) %collective-permute-start.4) | collective-permute-done | bytes 8224 | tf_op jit(solution)/shard_map/ppermute | solution.py:19
  48.0 0.0 copy-done.1
  48.1 0.0 copy-done.2
  48.1 0.6 multiply_divide_fusion
  48.7 2.9 %multiply_dynamic-update-slice_fusion.8 = (f32[88,2304]{1,0:T(8,128)S(1)}, f32[88,256]{1,0:T(8,128)S(1)}) fusion(f32[88]{0:T(128)S(1)} %get-tuple-element.16, f32[88,256]{1,0:T(8,128)S(1)} %fusion.42, f32[2048]{0:T(1024)S(1)} %bitcast.41, s32[2048]{0:T(1024)S(1)} %bitcast.33, f32[2048]{0:T(1024)S(1)} %bitcast.43, s32[2048]{0:T(1024)S(1)} %bitcast.35, ...), kind=kOutput, calls=%fused_computation.76 | convolution fusion | flops 560361472 | bytes 369344 | tf_op jit(solution)/shard_map/dot_general | solution.py:69
  51.6 0.1 multiply_dynamic-update-slice_fusion.7
  51.6 0.1 multiply_dynamic-update-slice_fusion.6
  51.7 0.1 multiply_dynamic-update-slice_fusion.5
  51.8 0.1 multiply_dynamic-update-slice_fusion.4
  51.9 0.1 multiply_dynamic-update-slice_fusion.3
  52.0 0.1 multiply_dynamic-update-slice_fusion.2
  52.0 0.1 multiply_dynamic-update-slice_fusion.1
  52.1 0.1 multiply_dynamic-update-slice_fusion
  52.2 2.6 %fusion = f32[88,512]{1,0:T(8,128)S(1)} fusion(f32[88,2304]{1,0:T(8,128)S(1)} %multiply_dynamic-update-slice_fusion, s32[2304]{0:T(1024)S(1)} %eq.60), kind=kOutput, calls=%fused_computation.1 | convolution fusion | flops 1246887936 | bytes 1000448 | tf_op jit(solution)/shard_map/dot_general | solution.py:81
  54.8 2.8 %collective-permute-start.5 = (f32[88,128]{1,0:T(8,128)S(1)}, f32[88,128]{1,0:T(8,128)S(1)}, u32[]{:S(2)}, u32[]{:S(2)}) collective-permute-start(f32[88,128]{1,0:T(8,128)S(1)} %slice.150), channel_id=1, source_target_pairs={{0,8},{8,16},{16,24},{24,32},{32,40},{40,48},{48,56},{56,64},{64,7... | collective-permute-start | bytes 135176 | tf_op jit(solution)/shard_map/ppermute | solution.py:12
  57.5 9.2 %collective-permute-done.5 = f32[88,128]{1,0:T(8,128)S(1)} collective-permute-done((f32[88,128]{1,0:T(8,128)S(1)}, f32[88,128]{1,0:T(8,128)S(1)}, u32[]{:S(2)}, u32[]{:S(2)}) %collective-permute-start.5) | collective-permute-done | bytes 45088 | tf_op jit(solution)/shard_map/ppermute | solution.py:12
  66.7 9.9 %collective-permute-start.6 = (f32[88,128]{1,0:T(8,128)S(1)}, f32[88,128]{1,0:T(8,128)S(1)}, u32[]{:S(2)}, u32[]{:S(2)}) collective-permute-start(f32[88,128]{1,0:T(8,128)S(1)} %get-tuple-element.5), channel_id=1, source_target_pairs={{0,504},{8,0},{16,8},{24,16},{32,24},{40,32},{48,40},{56,48},{64,5... | collective-permute-start | bytes 135176 | tf_op jit(solution)/shard_map/ppermute | solution.py:12
  76.7 1.7 %collective-permute-done.6 = f32[88,128]{1,0:T(8,128)S(1)} collective-permute-done((f32[88,128]{1,0:T(8,128)S(1)}, f32[88,128]{1,0:T(8,128)S(1)}, u32[]{:S(2)}, u32[]{:S(2)}) %collective-permute-start.6) | collective-permute-done | bytes 45088 | tf_op jit(solution)/shard_map/ppermute | solution.py:12
  78.4 0.6 pad_maximum_fusion
  (6 shorter events, 0.0 us)
Async XLA Ops:
  1.5 14.0 %collective-permute-start = (f32[88,128]{1,0:T(8,128)S(1)}, f32[88,128]{1,0:T(8,128)S(1)}, u32[]{:S(2)}, u32[]{:S(2)}) collective-permute-start(f32[88,128]{1,0:T(8,128)S(1)} %get-tuple-element.6), channel_id=1, source_target_pairs={{0,8},{8,16},{16,24},{24,32},{32,40},{40,48},{48,56},{56,64},{64,7... | collective-permute-start | bytes 135176 | tf_op jit(solution)/shard_map/ppermute | solution.py:12
  4.9 10.5 %collective-permute-start.1 = (f32[88,128]{1,0:T(8,128)S(1)}, f32[88,128]{1,0:T(8,128)S(1)}, u32[]{:S(2)}, u32[]{:S(2)}) collective-permute-start(f32[88,128]{1,0:T(8,128)S(1)} %get-tuple-element.7), channel_id=1, source_target_pairs={{0,504},{8,0},{16,8},{24,16},{32,24},{40,32},{48,40},{56,48},{64,5... | collective-permute-start | bytes 135176 | tf_op jit(solution)/shard_map/ppermute | solution.py:12
  15.4 2.8 %copy-start.3 = (f32[88]{0:T(128)S(1)}, f32[88]{0:T(128)}, u32[]{:S(2)}) copy-start(f32[88]{0:T(128)} %param.12) | copy-start | bytes 1060
  18.2 0.7 copy-start
  18.2 0.7 copy-start.4
  18.9 29.2 %copy-start.1 = (f32[2048]{0:T(1024)S(1)}, f32[2048]{0:T(1024)}, u32[]{:S(2)}) copy-start(f32[2048]{0:T(1024)} %param.19) | copy-start | bytes 24580
  18.9 29.2 %copy-start.2 = (f32[2048]{0:T(1024)S(1)}, f32[2048]{0:T(1024)}, u32[]{:S(2)}) copy-start(f32[2048]{0:T(1024)} %param.18) | copy-start | bytes 24580
  21.3 3.1 %collective-permute-start.2 = (f32[2048]{0:T(1024)S(1)}, f32[2048]{0:T(1024)S(1)}, u32[]{:S(2)}, u32[]{:S(2)}) collective-permute-start(f32[2048]{0:T(1024)S(1)} %fusion.5), channel_id=1, source_target_pairs={{0,1},{1,0},{2,3},{3,2},{4,5},{5,4},{6,7},{7,6},{8,9},{9,8},{10,11... | collective-permute-start | bytes 24584 | tf_op jit(solution)/shard_map/ppermute | solution.py:19
  24.4 9.4 %collective-permute-start.3 = (f32[2048]{0:T(1024)S(1)}, f32[2048]{0:T(1024)S(1)}, u32[]{:S(2)}, u32[]{:S(2)}) collective-permute-start(f32[2048]{0:T(1024)S(1)} %add.77), channel_id=1, source_target_pairs={{0,2},{1,3},{2,0},{3,1},{4,6},{5,7},{6,4},{7,5},{8,10},{9,11},{10,... | collective-permute-start | bytes 24584 | tf_op jit(solution)/shard_map/ppermute | solution.py:19
  33.8 14.2 %collective-permute-start.4 = (f32[2048]{0:T(1024)S(1)}, f32[2048]{0:T(1024)S(1)}, u32[]{:S(2)}, u32[]{:S(2)}) collective-permute-start(f32[2048]{0:T(1024)S(1)} %add.78), channel_id=1, source_target_pairs={{0,4},{1,5},{2,6},{3,7},{4,0},{5,1},{6,2},{7,3},{8,12},{9,13},{10,... | collective-permute-start | bytes 24584 | tf_op jit(solution)/shard_map/ppermute | solution.py:19
  54.8 11.9 %collective-permute-start.5 = (f32[88,128]{1,0:T(8,128)S(1)}, f32[88,128]{1,0:T(8,128)S(1)}, u32[]{:S(2)}, u32[]{:S(2)}) collective-permute-start(f32[88,128]{1,0:T(8,128)S(1)} %slice.150), channel_id=1, source_target_pairs={{0,8},{8,16},{16,24},{24,32},{32,40},{40,48},{48,56},{56,64},{64,7... | collective-permute-start | bytes 135176 | tf_op jit(solution)/shard_map/ppermute | solution.py:12
  66.7 11.6 %collective-permute-start.6 = (f32[88,128]{1,0:T(8,128)S(1)}, f32[88,128]{1,0:T(8,128)S(1)}, u32[]{:S(2)}, u32[]{:S(2)}) collective-permute-start(f32[88,128]{1,0:T(8,128)S(1)} %get-tuple-element.5), channel_id=1, source_target_pairs={{0,504},{8,0},{16,8},{24,16},{32,24},{40,32},{48,40},{56,48},{64,5... | collective-permute-start | bytes 135176 | tf_op jit(solution)/shard_map/ppermute | solution.py:12

commit v3 on v1

--- a/solution.py
+++ b/solution.py
@@ -54,7 +54,7 @@
 
     at_stars = jnp.dot(weighted, spread, precision=HIGHEST, preferred_element_type=jnp.float32)
     partial_value = jnp.sum(radial * at_stars, axis=0)
-    predicted = lax.psum(partial_value, "rad")
+    predicted = jnp.sum(lax.all_gather(partial_value, "rad"), axis=0)
     weight_back = (predicted - observed) / (sigma * sigma)
 
     adjoint_sum = lax.dot_general(
@@ -72,8 +72,9 @@
     framed = lax.dot_general(
         terms, pick, (((1,), (1,)), ((), ())), precision=HIGHEST, preferred_element_type=jnp.float32
     )
-    from_before = ring(framed[:, frame - COLS :], "ang", 1)
-    from_after = ring(framed[:, :COLS], "ang", -1)
+    to_after, to_before = lax.optimization_barrier((framed[:, frame - COLS :], framed[:, :COLS]))
+    from_before = ring(to_after, "ang", 1)
+    from_after = ring(to_before, "ang", -1)
     inner = framed[:, COLS : frame - COLS]
     gradient = jnp.concatenate(
         [inner[:, :COLS] + from_before, inner[:, COLS : pixels - COLS], inner[:, pixels - COLS :] + from_after],

time: 74.8 us -> 71.4 us (0.955)
  the two profiles are of different devices: /device:TPU:8 before, /device:TPU:1 now
where the time goes in v3:
time: 71.4 us; the launch traced here: 70.7 us
  blocking collectives  26.1 us (37%)
  starting transfers between devices  24.9 us (35%)
  matrix products  10.6 us (15%)
  local copies, waits for them, and re-layouts  4.95 us (7%)
  other arithmetic  2.2 us (3%)
  waiting for transfers between devices  1.11 us (2%)
  between operations  0.83 us (1%)
    all_gather x1, blocking collectives, on_device(): predicted = jnp.sum(lax.all_gather(partial_value, 'rad'), axis=0)  26.1 us
    ppermute x4, starting transfers between devices, ring(): lax.ppermute(value, axis, [(i, (i + step) % count) for i in range(count)])  24.9 us
    dot_general x1, matrix products, on_device(): lax.dot_general(radial * weight_back[None, :], spread, (((1,), (1,)), (()...  2.9 us
    dot_general x1, matrix products, on_device(): jnp.dot(wide, pick, precision=HIGHEST, preferred_element_type=jnp.float32)  2.73 us
    dot_general x1, matrix products, on_device(): lax.dot_general(terms, pick, (((1,), (1,)), ((), ())), precision=HIGHEST,...  2.55 us
    dot_general x1, matrix products, on_device(): jnp.dot(weighted, spread, precision=HIGHEST, preferred_element_type=jnp.f...  2.39 us
  transfers between devices with their start and end apart: 4, of which 1 were waited for; matrix products, arithmetic and copies ran while one was open for 6% of the time, Pallas kernels for 0%

profile of v3, /device:TPU:1, one launch (start us, length us, event | category | flops | bytes accessed | tf_op | source)
XLA Modules:
  0.0 70.7 jit_solution(3892974356635521461)
XLA Ops:
  0.6 0.8 %fusion.55 = (f32[88,128]{1,0:T(8,128)S(1)}, f32[88,128]{1,0:T(8,128)S(1)}) fusion(f32[88,256]{1,0:T(8,128)} %param.10), kind=kLoop, calls=%fused_computation.96 | loop fusion | bytes 180224 | tf_op jit(solution)/shard_map/slice | solution.py:31
  1.5 4.0 %collective-permute-start = (f32[88,128]{1,0:T(8,128)S(1)}, f32[88,128]{1,0:T(8,128)S(1)}, u32[]{:S(2)}, u32[]{:S(2)}) collective-permute-start(f32[88,128]{1,0:T(8,128)S(1)} %get-tuple-element.10), channel_id=1, source_target_pairs={{0,8},{8,16},{16,24},{24,32},{32,40},{40,48},{48,56},{56,64},{64,7... | collective-permute-start | bytes 135176 | tf_op jit(solution)/shard_map/ppermute | solution.py:12
  5.5 9.6 %collective-permute-start.1 = (f32[88,128]{1,0:T(8,128)S(1)}, f32[88,128]{1,0:T(8,128)S(1)}, u32[]{:S(2)}, u32[]{:S(2)}) collective-permute-start(f32[88,128]{1,0:T(8,128)S(1)} %get-tuple-element.11), channel_id=1, source_target_pairs={{0,504},{8,0},{16,8},{24,16},{32,24},{40,32},{48,40},{56,48},{64,5... | collective-permute-start | bytes 135176 | tf_op jit(solution)/shard_map/ppermute | solution.py:12
  15.1 1.0 %slice_bitcast_fusion.8 = (f32[88]{0:T(128)S(1)}, f32[88]{0:T(128)S(1)}, f32[88]{0:T(128)S(1)}, f32[88]{0:T(128)S(1)}, f32[88]{0:T(128)S(1)}, /*index=5*/f32[88]...) fusion(f32[88,9]{0,1:T(8,128)} %param.11), kind=kLoop, calls=%fused_computation.89 | loop fusion | bytes 6336 | tf_op jit(solution)/shard_map/mul | solution.py:40
  16.1 0.7 broadcast_add_fusion
  16.8 0.9 %fusion.56 = (s32[1,2048]{1,0:T(1,128)S(1)}, s32[1,2048]{1,0:T(1,128)S(1)}, s32[1,2048]{1,0:T(1,128)S(1)}, s32[1,2048]{1,0:T(1,128)S(1)}) fusion(s32[4,2048]{1,0:T(4,128)} %param.15), kind=kLoop, calls=%fused_computation.97 | loop fusion | bytes 65536 | tf_op jit(solution)/shard_map/slice | solution.py:48
  17.7 0.9 %fusion.57 = (f32[1,2048]{1,0:T(1,128)S(1)}, f32[1,2048]{1,0:T(1,128)S(1)}, f32[1,2048]{1,0:T(1,128)S(1)}, f32[1,2048]{1,0:T(1,128)S(1)}) fusion(f32[4,2048]{1,0:T(4,128)} %param.16), kind=kLoop, calls=%fused_computation.98 | loop fusion | bytes 65536 | tf_op jit(solution)/shard_map/slice | solution.py:48
  18.7 0.7 %eq.60 = s32[2304]{0:T(1024)S(1)} reshape(s32[9,256]{1,0:T(8,128)} %param.13) | data formatting | bytes 18432 | tf_op jit(solution)/shard_map/eq | solution.py:36
  19.4 0.0 copy-start.4
  19.4 0.0 collective-permute-done
  19.4 0.0 collective-permute-done.1
  19.4 2.7 %fusion.1 = f32[88,2304]{1,0:T(8,128)S(1)} fusion(s32[2304]{0:T(1024)S(1)} %eq.60, f32[88,128]{1,0:T(8,128)S(1)} %collective-permute-done.1, f32[88,256]{1,0:T(8,128)} %param.10, f32[88,128]{1,0:T(8,128)S(1)} %collective-permute-done), kind=kOutput, calls=%fused_computation.2 | convolution fusion | flops 1246978048 | bytes 1000448 | tf_op jit(solution)/shard_map/dot_general | solution.py:37
  22.2 0.0 copy-start.1
  22.2 0.0 copy-start.5
  22.2 0.0 copy-done.4
  22.2 0.2 fusion.42
  22.4 0.5 copy-done.1
  22.9 0.0 copy-done.5
  22.9 0.0 copy-start.2
  22.9 0.0 copy-start.3
  22.9 2.4 %fusion.5 = f32[2048]{0:T(1024)S(1)} fusion(f32[88,256]{1,0:T(8,128)S(1)} %fusion.42, f32[2048]{0:T(1024)S(1)} %bitcast.40, s32[2048]{0:T(1024)S(1)} %bitcast.32, f32[2048]{0:T(1024)S(1)} %bitcast.42, s32[2048]{0:T(1024)S(1)} %bitcast.34, f32[2048]{0:T(1024)S(1)} %bitcast.38, s32[2048]{0:T(1024)S(1)} %bitcast.30, f32[2048]{0:T(1024)S(1)} %bitcast.36, ...), kind=kOutput, calls=%fused_computation.12 | convolution fusion | flops 560494592 | bytes 188768 | tf_op jit(solution)/shard_map/dot_general | solution.py:55
  25.3 26.1 %all-gather = f32[16384]{0:T(1024)S(1)} all-gather(f32[2048]{0:T(1024)S(1)} %fusion.5), channel_id=2, replica_groups=mesh['ang'=64,'rad'=8] {'rad'}, dimensions={0}, use_global_device_ids=true | all-gather | bytes 73728 | tf_op jit(solution)/shard_map/all_gather | solution.py:57
  51.5 0.0 copy-done.2
  51.5 0.0 copy-done.3
  51.5 0.0 copy-start
  51.5 2.9 %multiply_dynamic-update-slice_fusion.8 = (f32[88,2304]{1,0:T(8,128)S(1)}, f32[88,256]{1,0:T(8,128)S(1)}) fusion(f32[88]{0:T(128)S(1)} %get-tuple-element.20, f32[88,256]{1,0:T(8,128)S(1)} %fusion.42, f32[2048]{0:T(1024)S(1)} %bitcast.41, s32[2048]{0:T(1024)S(1)} %bitcast.33, f32[2048]{0:T(1024)S(1)} %bitcast.43, s32[2048]{0:T(1024)S(1)} %bitcast.35, ...), kind=kOutput, calls=%fused_computation.76 | convolution fusion | flops 560361472 | bytes 369344 | tf_op jit(solution)/shard_map/dot_general | solution.py:60
  54.4 0.0 copy-done
  54.4 0.1 multiply_dynamic-update-slice_fusion.7
  54.5 0.1 multiply_dynamic-update-slice_fusion.6
  54.6 0.1 multiply_dynamic-update-slice_fusion.5
  54.7 0.1 multiply_dynamic-update-slice_fusion.4
  54.7 0.1 multiply_dynamic-update-slice_fusion.3
  54.8 0.1 multiply_dynamic-update-slice_fusion.2
  54.9 0.1 multiply_dynamic-update-slice_fusion.1
  55.0 0.1 multiply_dynamic-update-slice_fusion
  55.1 2.6 %fusion = f32[88,512]{1,0:T(8,128)S(1)} fusion(f32[88,2304]{1,0:T(8,128)S(1)} %multiply_dynamic-update-slice_fusion, s32[2304]{0:T(1024)S(1)} %eq.60), kind=kOutput, calls=%fused_computation.1 | convolution fusion | flops 1246887936 | bytes 1000448 | tf_op jit(solution)/shard_map/dot_general | solution.py:72
  57.6 1.9 %collective-permute-start.2 = (f32[88,128]{1,0:T(8,128)S(1)}, f32[88,128]{1,0:T(8,128)S(1)}, u32[]{:S(2)}, u32[]{:S(2)}) collective-permute-start(f32[88,128]{1,0:T(8,128)S(1)} %get-tuple-element.4), channel_id=1, source_target_pairs={{0,8},{8,16},{16,24},{24,32},{32,40},{40,48},{48,56},{56,64},{64,7... | collective-permute-start | bytes 135176 | tf_op jit(solution)/shard_map/ppermute | solution.py:12
  59.6 9.4 %collective-permute-start.3 = (f32[88,128]{1,0:T(8,128)S(1)}, f32[88,128]{1,0:T(8,128)S(1)}, u32[]{:S(2)}, u32[]{:S(2)}) collective-permute-start(f32[88,128]{1,0:T(8,128)S(1)} %get-tuple-element.5), channel_id=1, source_target_pairs={{0,504},{8,0},{16,8},{24,16},{32,24},{40,32},{48,40},{56,48},{64,5... | collective-permute-start | bytes 135176 | tf_op jit(solution)/shard_map/ppermute | solution.py:12
  69.0 0.0 collective-permute-done.2
  69.0 1.1 %collective-permute-done.3 = f32[88,128]{1,0:T(8,128)S(1)} collective-permute-done((f32[88,128]{1,0:T(8,128)S(1)}, f32[88,128]{1,0:T(8,128)S(1)}, u32[]{:S(2)}, u32[]{:S(2)}) %collective-permute-start.3) | collective-permute-done | bytes 45088 | tf_op jit(solution)/shard_map/ppermute | solution.py:12
  70.1 0.6 pad_maximum_fusion
  (6 shorter events, 0.1 us)
Async XLA Ops:
  1.5 18.0 %collective-permute-start = (f32[88,128]{1,0:T(8,128)S(1)}, f32[88,128]{1,0:T(8,128)S(1)}, u32[]{:S(2)}, u32[]{:S(2)}) collective-permute-start(f32[88,128]{1,0:T(8,128)S(1)} %get-tuple-element.10), channel_id=1, source_target_pairs={{0,8},{8,16},{16,24},{24,32},{32,40},{40,48},{48,56},{56,64},{64,7... | collective-permute-start | bytes 135176 | tf_op jit(solution)/shard_map/ppermute | solution.py:12
  5.5 13.9 %collective-permute-start.1 = (f32[88,128]{1,0:T(8,128)S(1)}, f32[88,128]{1,0:T(8,128)S(1)}, u32[]{:S(2)}, u32[]{:S(2)}) collective-permute-start(f32[88,128]{1,0:T(8,128)S(1)} %get-tuple-element.11), channel_id=1, source_target_pairs={{0,504},{8,0},{16,8},{24,16},{32,24},{40,32},{48,40},{56,48},{64,5... | collective-permute-start | bytes 135176 | tf_op jit(solution)/shard_map/ppermute | solution.py:12
  19.4 2.8 %copy-start.4 = (f32[88]{0:T(128)S(1)}, f32[88]{0:T(128)}, u32[]{:S(2)}) copy-start(f32[88]{0:T(128)} %param.12) | copy-start | bytes 1060
  22.2 0.7 copy-start.1
  22.2 0.7 %copy-start.5 = (f32[2048]{0:T(1024)S(1)}, f32[2048]{0:T(1024)}, u32[]{:S(2)}) copy-start(f32[2048]{0:T(1024)} %param.17) | copy-start | bytes 24580
  22.9 28.6 %copy-start.2 = (f32[2048]{0:T(1024)S(1)}, f32[2048]{0:T(1024)}, u32[]{:S(2)}) copy-start(f32[2048]{0:T(1024)} %param.19) | copy-start | bytes 24580
  22.9 28.6 %copy-start.3 = (f32[2048]{0:T(1024)S(1)}, f32[2048]{0:T(1024)}, u32[]{:S(2)}) copy-start(f32[2048]{0:T(1024)} %param.18) | copy-start | bytes 24580
  51.5 2.9 %copy-start = (f32[2048]{0:T(1024)}, f32[2048]{0:T(1024)S(1)}, u32[]{:S(2)}) copy-start(f32[2048]{0:T(1024)S(1)} %reduce_sum.19) | copy-start | bytes 24580
  57.6 11.3 %collective-permute-start.2 = (f32[88,128]{1,0:T(8,128)S(1)}, f32[88,128]{1,0:T(8,128)S(1)}, u32[]{:S(2)}, u32[]{:S(2)}) collective-permute-start(f32[88,128]{1,0:T(8,128)S(1)} %get-tuple-element.4), channel_id=1, source_target_pairs={{0,8},{8,16},{16,24},{24,32},{32,40},{40,48},{48,56},{56,64},{64,7... | collective-permute-start | bytes 135176 | tf_op jit(solution)/shard_map/ppermute | solution.py:12
  59.6 10.5 %collective-permute-start.3 = (f32[88,128]{1,0:T(8,128)S(1)}, f32[88,128]{1,0:T(8,128)S(1)}, u32[]{:S(2)}, u32[]{:S(2)}) collective-permute-start(f32[88,128]{1,0:T(8,128)S(1)} %get-tuple-element.5), channel_id=1, source_target_pairs={{0,504},{8,0},{16,8},{24,16},{32,24},{40,32},{48,40},{56,48},{64,5... | collective-permute-start | bytes 135176 | tf_op jit(solution)/shard_map/ppermute | solution.py:12

commit v4 on v3

--- a/solution.py
+++ b/solution.py
@@ -54,7 +54,9 @@
 
     at_stars = jnp.dot(weighted, spread, precision=HIGHEST, preferred_element_type=jnp.float32)
     partial_value = jnp.sum(radial * at_stars, axis=0)
-    predicted = jnp.sum(lax.all_gather(partial_value, "rad"), axis=0)
+    count = lax.axis_size("rad")
+    copies = jnp.broadcast_to(partial_value[None, :], (count, partial_value.shape[0]))
+    predicted = jnp.sum(lax.all_to_all(copies, "rad", 0, 0), axis=0)
     weight_back = (predicted - observed) / (sigma * sigma)
 
     adjoint_sum = lax.dot_general(

time: 71.4 us -> 72.2 us (1.011)
    all_to_all x0 -> x1, blocking collectives: none -> 26.8 us  [on_device(): predicted = jnp.sum(lax.all_to_all(copies, 'rad', 0, 0), axis=0)]
    all_gather x1 -> x0, blocking collectives: 26.1 us -> none  [on_device(): predicted = jnp.sum(lax.all_gather(partial_value, 'rad'), axis=0)]
where the time goes in v4:
time: 72.2 us; the launch traced here: 71.5 us
  blocking collectives  26.8 us (37%)
  starting transfers between devices  24.9 us (34%)
  matrix products  10.6 us (15%)
  local copies, waits for them, and re-layouts  4.97 us (7%)
  other arithmetic  2.23 us (3%)
  waiting for transfers between devices  1.11 us (2%)
  between operations  0.83 us (1%)
    all_to_all x1, blocking collectives, on_device(): predicted = jnp.sum(lax.all_to_all(copies, 'rad', 0, 0), axis=0)  26.8 us
    ppermute x4, starting transfers between devices, ring(): lax.ppermute(value, axis, [(i, (i + step) % count) for i in range(count)])  24.9 us
    dot_general x1, matrix products, on_device(): lax.dot_general(radial * weight_back[None, :], spread, (((1,), (1,)), (()...  2.9 us
    dot_general x1, matrix products, on_device(): jnp.dot(wide, pick, precision=HIGHEST, preferred_element_type=jnp.float32)  2.73 us
    dot_general x1, matrix products, on_device(): lax.dot_general(terms, pick, (((1,), (1,)), ((), ())), precision=HIGHEST,...  2.56 us
    dot_general x1, matrix products, on_device(): jnp.dot(weighted, spread, precision=HIGHEST, preferred_element_type=jnp.f...  2.39 us
  transfers between devices with their start and end apart: 4, of which 1 were waited for; matrix products, arithmetic and copies ran while one was open for 6% of the time, Pallas kernels for 0%

profile of v4, /device:TPU:1, one launch (start us, length us, event | category | flops | bytes accessed | tf_op | source)
XLA Modules:
  0.0 71.5 jit_solution(4540929364205779834)
XLA Ops:
  0.6 0.8 %fusion.55 = (f32[88,128]{1,0:T(8,128)S(1)}, f32[88,128]{1,0:T(8,128)S(1)}) fusion(f32[88,256]{1,0:T(8,128)} %param.10), kind=kLoop, calls=%fused_computation.96 | loop fusion | bytes 180224 | tf_op jit(solution)/shard_map/slice | solution.py:31
  1.5 4.0 %collective-permute-start = (f32[88,128]{1,0:T(8,128)S(1)}, f32[88,128]{1,0:T(8,128)S(1)}, u32[]{:S(2)}, u32[]{:S(2)}) collective-permute-start(f32[88,128]{1,0:T(8,128)S(1)} %get-tuple-element.10), channel_id=1, source_target_pairs={{0,8},{8,16},{16,24},{24,32},{32,40},{40,48},{48,56},{56,64},{64,7... | collective-permute-start | bytes 135176 | tf_op jit(solution)/shard_map/ppermute | solution.py:12
  5.5 9.6 %collective-permute-start.1 = (f32[88,128]{1,0:T(8,128)S(1)}, f32[88,128]{1,0:T(8,128)S(1)}, u32[]{:S(2)}, u32[]{:S(2)}) collective-permute-start(f32[88,128]{1,0:T(8,128)S(1)} %get-tuple-element.11), channel_id=1, source_target_pairs={{0,504},{8,0},{16,8},{24,16},{32,24},{40,32},{48,40},{56,48},{64,5... | collective-permute-start | bytes 135176 | tf_op jit(solution)/shard_map/ppermute | solution.py:12
  15.1 1.0 %slice_bitcast_fusion.8 = (f32[88]{0:T(128)S(1)}, f32[88]{0:T(128)S(1)}, f32[88]{0:T(128)S(1)}, f32[88]{0:T(128)S(1)}, f32[88]{0:T(128)S(1)}, /*index=5*/f32[88]...) fusion(f32[88,9]{0,1:T(8,128)} %param.11), kind=kLoop, calls=%fused_computation.89 | loop fusion | bytes 6336 | tf_op jit(solution)/shard_map/mul | solution.py:40
  16.1 0.7 broadcast_add_fusion
  16.8 0.9 %fusion.56 = (s32[1,2048]{1,0:T(1,128)S(1)}, s32[1,2048]{1,0:T(1,128)S(1)}, s32[1,2048]{1,0:T(1,128)S(1)}, s32[1,2048]{1,0:T(1,128)S(1)}) fusion(s32[4,2048]{1,0:T(4,128)} %param.15), kind=kLoop, calls=%fused_computation.97 | loop fusion | bytes 65536 | tf_op jit(solution)/shard_map/slice | solution.py:48
  17.7 0.9 %fusion.57 = (f32[1,2048]{1,0:T(1,128)S(1)}, f32[1,2048]{1,0:T(1,128)S(1)}, f32[1,2048]{1,0:T(1,128)S(1)}, f32[1,2048]{1,0:T(1,128)S(1)}) fusion(f32[4,2048]{1,0:T(4,128)} %param.16), kind=kLoop, calls=%fused_computation.98 | loop fusion | bytes 65536 | tf_op jit(solution)/shard_map/slice | solution.py:48
  18.7 0.7 %eq.60 = s32[2304]{0:T(1024)S(1)} reshape(s32[9,256]{1,0:T(8,128)} %param.13) | data formatting | bytes 18432 | tf_op jit(solution)/shard_map/eq | solution.py:36
  19.4 0.0 copy-start.4
  19.4 0.0 collective-permute-done
  19.4 0.0 collective-permute-done.1
  19.4 2.7 %fusion.1 = f32[88,2304]{1,0:T(8,128)S(1)} fusion(s32[2304]{0:T(1024)S(1)} %eq.60, f32[88,128]{1,0:T(8,128)S(1)} %collective-permute-done.1, f32[88,256]{1,0:T(8,128)} %param.10, f32[88,128]{1,0:T(8,128)S(1)} %collective-permute-done), kind=kOutput, calls=%fused_computation.2 | convolution fusion | flops 1246978048 | bytes 1000448 | tf_op jit(solution)/shard_map/dot_general | solution.py:37
  22.2 0.0 copy-start.1
  22.2 0.0 copy-start.5
  22.2 0.0 copy-done.4
  22.2 0.2 fusion.42
  22.4 0.5 copy-done.1
  22.9 0.0 copy-done.5
  22.9 0.0 copy-start.2
  22.9 0.0 copy-start.3
  22.9 2.4 %fusion.5 = f32[2048]{0:T(1024)S(1)} fusion(f32[88,256]{1,0:T(8,128)S(1)} %fusion.42, f32[2048]{0:T(1024)S(1)} %bitcast.40, s32[2048]{0:T(1024)S(1)} %bitcast.32, f32[2048]{0:T(1024)S(1)} %bitcast.42, s32[2048]{0:T(1024)S(1)} %bitcast.34, f32[2048]{0:T(1024)S(1)} %bitcast.38, s32[2048]{0:T(1024)S(1)} %bitcast.30, f32[2048]{0:T(1024)S(1)} %bitcast.36, ...), kind=kOutput, calls=%fused_computation.12 | convolution fusion | flops 560494592 | bytes 188768 | tf_op jit(solution)/shard_map/dot_general | solution.py:55
  25.3 26.8 %all_to_all.6 = f32[8,1,2048]{2,1,0:T(1,128)S(1)} all-to-all(f32[8,1,2048]{2,1,0:T(1,128)S(1)} %broadcast_in_dim.76), channel_id=1, replica_groups=mesh['ang'=64,'rad'=8] {'rad'}, dimensions={0} | all-to-all | bytes 131072 | tf_op jit(solution)/shard_map/all_to_all | solution.py:59
  52.2 0.1 reduce_sum.19
  52.2 0.0 copy-done.2
  52.2 0.0 copy-done.3
  52.2 0.0 copy-start
  52.3 2.9 %multiply_dynamic-update-slice_fusion.8 = (f32[88,2304]{1,0:T(8,128)S(1)}, f32[88,256]{1,0:T(8,128)S(1)}) fusion(f32[88]{0:T(128)S(1)} %get-tuple-element.20, f32[88,256]{1,0:T(8,128)S(1)} %fusion.42, f32[2048]{0:T(1024)S(1)} %bitcast.41, s32[2048]{0:T(1024)S(1)} %bitcast.33, f32[2048]{0:T(1024)S(1)} %bitcast.43, s32[2048]{0:T(1024)S(1)} %bitcast.35, ...), kind=kOutput, calls=%fused_computation.76 | convolution fusion | flops 560361472 | bytes 369344 | tf_op jit(solution)/shard_map/dot_general | solution.py:62
  55.2 0.0 copy-done
  55.2 0.1 multiply_dynamic-update-slice_fusion.7
  55.3 0.1 multiply_dynamic-update-slice_fusion.6
  55.3 0.1 multiply_dynamic-update-slice_fusion.5
  55.4 0.1 multiply_dynamic-update-slice_fusion.4
  55.5 0.1 multiply_dynamic-update-slice_fusion.3
  55.6 0.1 multiply_dynamic-update-slice_fusion.2
  55.7 0.1 multiply_dynamic-update-slice_fusion.1
  55.8 0.1 multiply_dynamic-update-slice_fusion
  55.8 2.6 %fusion = f32[88,512]{1,0:T(8,128)S(1)} fusion(f32[88,2304]{1,0:T(8,128)S(1)} %multiply_dynamic-update-slice_fusion, s32[2304]{0:T(1024)S(1)} %eq.60), kind=kOutput, calls=%fused_computation.1 | convolution fusion | flops 1246887936 | bytes 1000448 | tf_op jit(solution)/shard_map/dot_general | solution.py:74
  58.4 1.9 %collective-permute-start.2 = (f32[88,128]{1,0:T(8,128)S(1)}, f32[88,128]{1,0:T(8,128)S(1)}, u32[]{:S(2)}, u32[]{:S(2)}) collective-permute-start(f32[88,128]{1,0:T(8,128)S(1)} %get-tuple-element.4), channel_id=1, source_target_pairs={{0,8},{8,16},{16,24},{24,32},{32,40},{40,48},{48,56},{56,64},{64,7... | collective-permute-start | bytes 135176 | tf_op jit(solution)/shard_map/ppermute | solution.py:12
  60.3 9.4 %collective-permute-start.3 = (f32[88,128]{1,0:T(8,128)S(1)}, f32[88,128]{1,0:T(8,128)S(1)}, u32[]{:S(2)}, u32[]{:S(2)}) collective-permute-start(f32[88,128]{1,0:T(8,128)S(1)} %get-tuple-element.5), channel_id=1, source_target_pairs={{0,504},{8,0},{16,8},{24,16},{32,24},{40,32},{48,40},{56,48},{64,5... | collective-permute-start | bytes 135176 | tf_op jit(solution)/shard_map/ppermute | solution.py:12
  69.7 0.0 collective-permute-done.2
  69.7 1.1 %collective-permute-done.3 = f32[88,128]{1,0:T(8,128)S(1)} collective-permute-done((f32[88,128]{1,0:T(8,128)S(1)}, f32[88,128]{1,0:T(8,128)S(1)}, u32[]{:S(2)}, u32[]{:S(2)}) %collective-permute-start.3) | collective-permute-done | bytes 45088 | tf_op jit(solution)/shard_map/ppermute | solution.py:12
  70.9 0.6 pad_maximum_fusion
  (5 shorter events, 0.1 us)
Async XLA Ops:
  1.5 18.0 %collective-permute-start = (f32[88,128]{1,0:T(8,128)S(1)}, f32[88,128]{1,0:T(8,128)S(1)}, u32[]{:S(2)}, u32[]{:S(2)}) collective-permute-start(f32[88,128]{1,0:T(8,128)S(1)} %get-tuple-element.10), channel_id=1, source_target_pairs={{0,8},{8,16},{16,24},{24,32},{32,40},{40,48},{48,56},{56,64},{64,7... | collective-permute-start | bytes 135176 | tf_op jit(solution)/shard_map/ppermute | solution.py:12
  5.5 13.9 %collective-permute-start.1 = (f32[88,128]{1,0:T(8,128)S(1)}, f32[88,128]{1,0:T(8,128)S(1)}, u32[]{:S(2)}, u32[]{:S(2)}) collective-permute-start(f32[88,128]{1,0:T(8,128)S(1)} %get-tuple-element.11), channel_id=1, source_target_pairs={{0,504},{8,0},{16,8},{24,16},{32,24},{40,32},{48,40},{56,48},{64,5... | collective-permute-start | bytes 135176 | tf_op jit(solution)/shard_map/ppermute | solution.py:12
  19.4 2.8 %copy-start.4 = (f32[88]{0:T(128)S(1)}, f32[88]{0:T(128)}, u32[]{:S(2)}) copy-start(f32[88]{0:T(128)} %param.12) | copy-start | bytes 1060
  22.2 0.7 copy-start.1
  22.2 0.7 copy-start.5
  22.9 29.3 %copy-start.2 = (f32[2048]{0:T(1024)S(1)}, f32[2048]{0:T(1024)}, u32[]{:S(2)}) copy-start(f32[2048]{0:T(1024)} %param.19) | copy-start | bytes 24580
  22.9 29.3 %copy-start.3 = (f32[2048]{0:T(1024)S(1)}, f32[2048]{0:T(1024)}, u32[]{:S(2)}) copy-start(f32[2048]{0:T(1024)} %param.18) | copy-start | bytes 24580
  52.2 2.9 %copy-start = (f32[2048]{0:T(1024)}, f32[2048]{0:T(1024)S(1)}, u32[]{:S(2)}) copy-start(f32[2048]{0:T(1024)S(1)} %reduce_sum.19) | copy-start | bytes 24580
  58.4 11.3 %collective-permute-start.2 = (f32[88,128]{1,0:T(8,128)S(1)}, f32[88,128]{1,0:T(8,128)S(1)}, u32[]{:S(2)}, u32[]{:S(2)}) collective-permute-start(f32[88,128]{1,0:T(8,128)S(1)} %get-tuple-element.4), channel_id=1, source_target_pairs={{0,8},{8,16},{16,24},{24,32},{32,40},{40,48},{48,56},{56,64},{64,7... | collective-permute-start | bytes 135176 | tf_op jit(solution)/shard_map/ppermute | solution.py:12
  60.3 10.5 %collective-permute-start.3 = (f32[88,128]{1,0:T(8,128)S(1)}, f32[88,128]{1,0:T(8,128)S(1)}, u32[]{:S(2)}, u32[]{:S(2)}) collective-permute-start(f32[88,128]{1,0:T(8,128)S(1)} %get-tuple-element.5), channel_id=1, source_target_pairs={{0,504},{8,0},{16,8},{24,16},{32,24},{40,32},{48,40},{56,48},{64,5... | collective-permute-start | bytes 135176 | tf_op jit(solution)/shard_map/ppermute | solution.py:12

commit v5 on v3

--- a/solution.py
+++ b/solution.py
@@ -5,6 +5,30 @@
 
 COLS = 128
 HIGHEST = lax.Precision.HIGHEST
+
+
+def split3(value):
+    high = lax.reduce_precision(value, exponent_bits=8, mantissa_bits=7)
+    rest = value - high
+    middle = lax.reduce_precision(rest, exponent_bits=8, mantissa_bits=7)
+    low = rest - middle
+    return [part.astype(jnp.bfloat16) for part in (high, middle, low)]
+
+
+def select(value, onehot):
+    total = None
+    for part in split3(value):
+        product = jnp.dot(part, onehot, preferred_element_type=jnp.float32)
+        total = product if total is None else total + product
+    return total
+
+
+def spread_select(value, onehot):
+    total = None
+    for part in split3(value):
+        product = lax.dot_general(part, onehot, (((1,), (1,)), ((), ())), preferred_element_type=jnp.float32)
+        total = product if total is None else total + product
+    return total
 
 
 def ring(value, axis, step):
@@ -32,12 +56,22 @@
     below = ring(latent[:, :COLS], "ang", -1)
     wide = jnp.concatenate([above, latent, below], axis=1)
 
-    position = lax.broadcasted_iota(jnp.int32, (frame, taps * pixels), 0)
-    pick = (position == neighbours.reshape(1, taps * pixels)).astype(jnp.float32)
-    picked = jnp.dot(wide, pick, precision=HIGHEST, preferred_element_type=jnp.float32)
-    refined = jnp.zeros((shells, pixels), jnp.float32)
-    for offset in range(taps):
-        refined = refined + stencil[:, offset : offset + 1] * picked[:, offset * pixels : (offset + 1) * pixels]
+    cycles = pixels // COLS
+    window = 3 * COLS
+    rest = taps - 1
+    position = lax.broadcasted_iota(jnp.int32, (window, rest * COLS), 0)
+    picks = []
+    refined_cycles = []
+    for cycle in range(cycles):
+        columns = neighbours[1:, cycle * COLS : (cycle + 1) * COLS].reshape(1, rest * COLS) - cycle * COLS
+        pick = (position == columns).astype(jnp.bfloat16)
+        picks.append(pick)
+        picked = select(wide[:, cycle * COLS : cycle * COLS + window], pick)
+        value = stencil[:, 0:1] * latent[:, cycle * COLS : (cycle + 1) * COLS]
+        for offset in range(rest):
+            value = value + stencil[:, offset + 1 : offset + 2] * picked[:, offset * COLS : (offset + 1) * COLS]
+        refined_cycles.append(value)
+    refined = jnp.concatenate(refined_cycles, axis=1)
     density = jnp.exp(refined)
     weighted = bin_width[:, None] * density
 
@@ -66,12 +100,12 @@
     )
     sensitivity = adjoint_sum * weighted
 
-    terms = jnp.concatenate(
-        [stencil[:, offset : offset + 1] * sensitivity for offset in range(taps)], axis=1
-    )
-    framed = lax.dot_general(
-        terms, pick, (((1,), (1,)), ((), ())), precision=HIGHEST, preferred_element_type=jnp.float32
-    )
+    framed = jnp.pad(stencil[:, 0:1] * sensitivity, ((0, 0), (COLS, COLS)))
+    for cycle in range(cycles):
+        own = sensitivity[:, cycle * COLS : (cycle + 1) * COLS]
+        terms = jnp.concatenate([stencil[:, offset + 1 : offset + 2] * own for offset in range(rest)], axis=1)
+        spread_back = spread_select(terms, picks[cycle])
+        framed = framed + jnp.pad(spread_back, ((0, 0), (cycle * COLS, frame - window - cycle * COLS)))
     to_after, to_before = lax.optimization_barrier((framed[:, frame - COLS :], framed[:, :COLS]))
     from_before = ring(to_after, "ang", 1)
     from_after = ring(to_before, "ang", -1)

time: 71.4 us -> 73.8 us (1.034)
  waiting for transfers between devices: 1.11 us -> 7.03 us
  starting transfers between devices: 24.9 us -> 20.7 us
  other arithmetic: 2.2 us -> 3.12 us
    ppermute x4, waiting for transfers between devices: 1.11 us -> 7.03 us  [ring(): lax.ppermute(value, axis, [(i, (i + step) % count) for i in range(count)])]
    ppermute x4, starting transfers between devices: 24.9 us -> 20.7 us  [ring(): lax.ppermute(value, axis, [(i, (i + step) % count) for i in range(count)])]
    dot_general x2 -> x12, matrix products: 5.29 us -> 5.14 us  [the longest x6 2.57 us: spread_select(): lax.dot_general(part, onehot, (((1,), (1,)), ((), ())), preferred_element...]
  transfers between devices with their start and end apart: 4 -> 4, of which waited for: 1 -> 3; matrix products, arithmetic and copies ran while one was open for 6% -> 6% of each run, Pallas kernels for 0% -> 0%
where the time goes in v5:
time: 73.8 us; the launch traced here: 73.2 us
  blocking collectives  26.7 us (36%)
  starting transfers between devices  20.7 us (28%)
  matrix products  10.4 us (14%)
  waiting for transfers between devices  7.03 us (10%)
  local copies, waits for them, and re-layouts  4.31 us (6%)
  other arithmetic  3.12 us (4%)
  between operations  0.87 us (1%)
    all_gather x1, blocking collectives, on_device(): predicted = jnp.sum(lax.all_gather(partial_value, 'rad'), axis=0)  26.7 us
    ppermute x4, starting transfers between devices, ring(): lax.ppermute(value, axis, [(i, (i + step) % count) for i in range(count)])  20.7 us
    ppermute x4, waiting for transfers between devices, ring(): lax.ppermute(value, axis, [(i, (i + step) % count) for i in range(count)])  7.03 us
    dot_general x1, matrix products, on_device(): lax.dot_general(radial * weight_back[None, :], spread, (((1,), (1,)), (()...  2.9 us
    dot_general x6, matrix products, spread_select(): lax.dot_general(part, onehot, (((1,), (1,)), ((), ())), preferred_element...  2.57 us
    dot_general x6, matrix products, select(): product = jnp.dot(part, onehot, preferred_element_type=jnp.float32)  2.56 us
    dot_general x1, matrix products, on_device(): jnp.dot(weighted, spread, precision=HIGHEST, preferred_element_type=jnp.f...  2.4 us
  transfers between devices with their start and end apart: 4, of which 3 were waited for; matrix products, arithmetic and copies ran while one was open for 6% of the time, Pallas kernels for 0%

profile of v5, /device:TPU:1, one launch (start us, length us, event | category | flops | bytes accessed | tf_op | source)
XLA Modules:
  0.0 73.2 jit_solution(5564134195247034887)
XLA Ops:
  0.6 0.0 copy-start
  0.6 0.9 %slice.167 = f32[88,128]{1,0:T(8,128)S(1)} slice(f32[88,256]{1,0:T(8,128)} %param.10), slice={[0:88], [128:256]} | slice | bytes 90112 | tf_op jit(solution)/shard_map/slice | solution.py:55
  1.5 4.0 %collective-permute-start = (f32[88,128]{1,0:T(8,128)S(1)}, f32[88,128]{1,0:T(8,128)S(1)}, u32[]{:S(2)}, u32[]{:S(2)}) collective-permute-start(f32[88,128]{1,0:T(8,128)S(1)} %slice.167), channel_id=1, source_target_pairs={{0,8},{8,16},{16,24},{24,32},{32,40},{40,48},{48,56},{56,64},{64,7... | collective-permute-start | bytes 135176 | tf_op jit(solution)/shard_map/ppermute | solution.py:36
  5.5 0.7 broadcast_add_fusion
  6.2 0.7 slice_bitcast_fusion
  6.9 0.9 %fusion.95 = (s32[1,2048]{1,0:T(1,128)S(1)}, s32[1,2048]{1,0:T(1,128)S(1)}, s32[1,2048]{1,0:T(1,128)S(1)}, s32[1,2048]{1,0:T(1,128)S(1)}) fusion(s32[4,2048]{1,0:T(4,128)} %param.15), kind=kLoop, calls=%fused_computation.171 | loop fusion | bytes 65536 | tf_op jit(solution)/shard_map/slice | solution.py:82
  7.9 0.9 %fusion.96 = (f32[1,2048]{1,0:T(1,128)S(1)}, f32[1,2048]{1,0:T(1,128)S(1)}, f32[1,2048]{1,0:T(1,128)S(1)}, f32[1,2048]{1,0:T(1,128)S(1)}) fusion(f32[4,2048]{1,0:T(4,128)} %param.16), kind=kLoop, calls=%fused_computation.172 | loop fusion | bytes 65536 | tf_op jit(solution)/shard_map/slice | solution.py:82
  8.8 1.0 %slice_bitcast_fusion.9 = (f32[88]{0:T(128)S(1)}, f32[88]{0:T(128)S(1)}, f32[88]{0:T(128)S(1)}, f32[88]{0:T(128)S(1)}, f32[88]{0:T(128)S(1)}, /*index=5*/f32[88]...) fusion(f32[88,9]{0,1:T(8,128)} %param.11), kind=kLoop, calls=%fused_computation.164 | loop fusion | bytes 6336 | tf_op jit(solution)/shard_map/mul | solution.py:70
  9.8 4.8 %collective-permute-done = f32[88,128]{1,0:T(8,128)S(1)} collective-permute-done((f32[88,128]{1,0:T(8,128)S(1)}, f32[88,128]{1,0:T(8,128)S(1)}, u32[]{:S(2)}, u32[]{:S(2)}) %collective-permute-start) | collective-permute-done | bytes 45088 | tf_op jit(solution)/shard_map/ppermute | solution.py:36
  14.6 0.0 copy-done
  14.7 0.4 fusion.10
  15.1 0.4 fusion.11
  15.5 0.4 fusion.17
  15.9 0.2 fusion.81
  16.1 4.8 %collective-permute-start.1 = (f32[88,128]{1,0:T(8,128)S(1)}, f32[88,128]{1,0:T(8,128)S(1)}, u32[]{:S(2)}, u32[]{:S(2)}) collective-permute-start(f32[88,128]{1,0:T(8,128)S(1)} %get-tuple-element.27), channel_id=1, source_target_pairs={{0,504},{8,0},{16,8},{24,16},{32,24},{40,32},{48,40},{56,48},{64,5... | collective-permute-start | bytes 135176 | tf_op jit(solution)/shard_map/ppermute | solution.py:36
  21.0 1.1 %collective-permute-done.1 = f32[88,128]{1,0:T(8,128)S(1)} collective-permute-done((f32[88,128]{1,0:T(8,128)S(1)}, f32[88,128]{1,0:T(8,128)S(1)}, u32[]{:S(2)}, u32[]{:S(2)}) %collective-permute-start.1) | collective-permute-done | bytes 45088 | tf_op jit(solution)/shard_map/ppermute | solution.py:36
  22.1 0.4 fusion.4
  22.5 0.4 fusion.5
  22.9 0.4 fusion.16
  23.4 0.0 copy-start.2
  23.4 0.0 copy-start.5
  23.4 0.0 copy-start.6
  23.4 0.2 fusion.73
  23.6 0.5 copy-done.2
  24.1 0.0 copy-done.5
  24.1 0.0 copy-done.6
  24.1 0.0 copy-start.3
  24.1 0.0 copy-start.4
  24.1 2.4 %fusion.13 = f32[2048]{0:T(1024)S(1)} fusion(f32[2048]{0:T(1024)S(1)} %bitcast.42, s32[2048]{0:T(1024)S(1)} %bitcast.34, f32[2048]{0:T(1024)S(1)} %bitcast.44, s32[2048]{0:T(1024)S(1)} %bitcast.36, f32[2048]{0:T(1024)S(1)} %bitcast.40, s32[2048]{0:T(1024)S(1)} %bitcast.32, f32[2048]{0:T(1024)S(1)} %bitcast.38, s32[2048]{0:T(1024)S(1)} %bitcast.30, ...), kind=kOutput, calls=%fused_computation.21 | convolution fusion | flops 560539648 | bytes 189120 | tf_op jit(solution)/shard_map/dot_general | solution.py:89
  26.5 26.7 %all-gather = f32[16384]{0:T(1024)S(1)} all-gather(f32[2048]{0:T(1024)S(1)} %fusion.13), channel_id=2, replica_groups=mesh['ang'=64,'rad'=8] {'rad'}, dimensions={0}, use_global_device_ids=true | all-gather | bytes 73728 | tf_op jit(solution)/shard_map/all_gather | solution.py:91
  53.2 0.0 copy-done.3
  53.2 0.0 copy-done.4
  53.3 0.0 copy-start.1
  53.3 2.9 %broadcast_multiply_fusion = (f32[88,256]{1,0:T(8,128)S(1)}, f32[88,256]{1,0:T(8,128)S(1)}) fusion(f32[88]{0:T(128)S(1)} %get-tuple-element.40, f32[88,128]{1,0:T(8,128)S(1)} %fusion.73, f32[88,128]{1,0:T(8,128)S(1)} %get-tuple-element.26, f32[88]{0:T(128)S(1)} %copy-done.6, f32[2048]{0:T(1024)S(1)} %bitcast.43, s32[2048]{0:T(1024)S(1)} %bitcast.35, ...), kind=kOutput, calls=%fused_computation.146 | convolution fusion | flops 560406528 | bytes 369696 | tf_op jit(solution)/shard_map/dot_general | solution.py:94
  56.2 0.0 copy-done.1
  56.2 0.1 multiply_dynamic-update-slice_fusion.15
  56.3 0.1 multiply_dynamic-update-slice_fusion.14
  56.4 0.1 multiply_dynamic-update-slice_fusion.13
  56.4 0.1 multiply_dynamic-update-slice_fusion.12
  56.5 0.1 multiply_dynamic-update-slice_fusion.11
  56.6 0.1 multiply_dynamic-update-slice_fusion.10
  56.7 0.1 multiply_dynamic-update-slice_fusion.9
  56.8 0.1 multiply_dynamic-update-slice_fusion.8
  56.9 0.4 fusion.7
  57.3 0.4 fusion.8
  57.7 0.4 fusion.1
  58.2 0.4 fusion.2
  58.6 0.4 fusion.19
  59.0 0.4 fusion.21
  59.5 1.9 %collective-permute-start.2 = (f32[88,128]{1,0:T(8,128)S(1)}, f32[88,128]{1,0:T(8,128)S(1)}, u32[]{:S(2)}, u32[]{:S(2)}) collective-permute-start(f32[88,128]{1,0:T(8,128)S(1)} %get-tuple-element.4), channel_id=1, source_target_pairs={{0,8},{8,16},{16,24},{24,32},{32,40},{40,48},{48,56},{56,64},{64,7... | collective-permute-start | bytes 135176 | tf_op jit(solution)/shard_map/ppermute | solution.py:36
  61.4 10.0 %collective-permute-start.3 = (f32[88,128]{1,0:T(8,128)S(1)}, f32[88,128]{1,0:T(8,128)S(1)}, u32[]{:S(2)}, u32[]{:S(2)}) collective-permute-start(f32[88,128]{1,0:T(8,128)S(1)} %get-tuple-element.5), channel_id=1, source_target_pairs={{0,504},{8,0},{16,8},{24,16},{32,24},{40,32},{48,40},{56,48},{64,5... | collective-permute-start | bytes 135176 | tf_op jit(solution)/shard_map/ppermute | solution.py:36
  71.4 0.0 collective-permute-done.2
  71.4 1.1 %collective-permute-done.3 = f32[88,128]{1,0:T(8,128)S(1)} collective-permute-done((f32[88,128]{1,0:T(8,128)S(1)}, f32[88,128]{1,0:T(8,128)S(1)}, u32[]{:S(2)}, u32[]{:S(2)}) %collective-permute-start.3) | collective-permute-done | bytes 45088 | tf_op jit(solution)/shard_map/ppermute | solution.py:36
  72.5 0.6 pad_maximum_fusion
  (10 shorter events, 0.1 us)
Async XLA Ops:
  0.6 14.0 %copy-start = (f32[88,256]{1,0:T(8,128)S(1)}, f32[88,256]{1,0:T(8,128)}, u32[]{:S(2)}) copy-start(f32[88,256]{1,0:T(8,128)} %param.10) | copy-start | bytes 270340
  1.5 13.1 %collective-permute-start = (f32[88,128]{1,0:T(8,128)S(1)}, f32[88,128]{1,0:T(8,128)S(1)}, u32[]{:S(2)}, u32[]{:S(2)}) collective-permute-start(f32[88,128]{1,0:T(8,128)S(1)} %slice.167), channel_id=1, source_target_pairs={{0,8},{8,16},{16,24},{24,32},{32,40},{40,48},{48,56},{56,64},{64,7... | collective-permute-start | bytes 135176 | tf_op jit(solution)/shard_map/ppermute | solution.py:36
  16.1 5.9 %collective-permute-start.1 = (f32[88,128]{1,0:T(8,128)S(1)}, f32[88,128]{1,0:T(8,128)S(1)}, u32[]{:S(2)}, u32[]{:S(2)}) collective-permute-start(f32[88,128]{1,0:T(8,128)S(1)} %get-tuple-element.27), channel_id=1, source_target_pairs={{0,504},{8,0},{16,8},{24,16},{32,24},{40,32},{48,40},{56,48},{64,5... | collective-permute-start | bytes 135176 | tf_op jit(solution)/shard_map/ppermute | solution.py:36
  23.4 0.7 copy-start.2
  23.4 0.7 copy-start.5
  23.4 0.7 copy-start.6
  24.1 29.1 %copy-start.3 = (f32[2048]{0:T(1024)S(1)}, f32[2048]{0:T(1024)}, u32[]{:S(2)}) copy-start(f32[2048]{0:T(1024)} %param.19) | copy-start | bytes 24580
  24.1 29.2 %copy-start.4 = (f32[2048]{0:T(1024)S(1)}, f32[2048]{0:T(1024)}, u32[]{:S(2)}) copy-start(f32[2048]{0:T(1024)} %param.18) | copy-start | bytes 24580
  53.3 2.9 %copy-start.1 = (f32[2048]{0:T(1024)}, f32[2048]{0:T(1024)S(1)}, u32[]{:S(2)}) copy-start(f32[2048]{0:T(1024)S(1)} %reduce_sum.19) | copy-start | bytes 24580
  59.5 11.9 %collective-permute-start.2 = (f32[88,128]{1,0:T(8,128)S(1)}, f32[88,128]{1,0:T(8,128)S(1)}, u32[]{:S(2)}, u32[]{:S(2)}) collective-permute-start(f32[88,128]{1,0:T(8,128)S(1)} %get-tuple-element.4), channel_id=1, source_target_pairs={{0,8},{8,16},{16,24},{24,32},{32,40},{40,48},{48,56},{56,64},{64,7... | collective-permute-start | bytes 135176 | tf_op jit(solution)/shard_map/ppermute | solution.py:36
  61.4 11.1 %collective-permute-start.3 = (f32[88,128]{1,0:T(8,128)S(1)}, f32[88,128]{1,0:T(8,128)S(1)}, u32[]{:S(2)}, u32[]{:S(2)}) collective-permute-start(f32[88,128]{1,0:T(8,128)S(1)} %get-tuple-element.5), channel_id=1, source_target_pairs={{0,504},{8,0},{16,8},{24,16},{32,24},{40,32},{48,40},{56,48},{64,5... | collective-permute-start | bytes 135176 | tf_op jit(solution)/shard_map/ppermute | solution.py:36

commit v6 on v3

--- a/solution.py
+++ b/solution.py
@@ -5,6 +5,26 @@
 
 COLS = 128
 HIGHEST = lax.Precision.HIGHEST
+
+
+def split3(value):
+    high = lax.reduce_precision(value, exponent_bits=8, mantissa_bits=7)
+    rest = value - high
+    middle = lax.reduce_precision(rest, exponent_bits=8, mantissa_bits=7)
+    low = rest - middle
+    return jnp.concatenate([high, middle, low], axis=0).astype(jnp.bfloat16)
+
+
+def select(value, onehot):
+    rows = value.shape[0]
+    product = jnp.dot(split3(value), onehot, preferred_element_type=jnp.float32)
+    return product[:rows] + product[rows : 2 * rows] + product[2 * rows :]
+
+
+def spread_select(value, onehot):
+    rows = value.shape[0]
+    product = lax.dot_general(split3(value), onehot, (((1,), (1,)), ((), ())), preferred_element_type=jnp.float32)
+    return product[:rows] + product[rows : 2 * rows] + product[2 * rows :]
 
 
 def ring(value, axis, step):
@@ -32,12 +52,13 @@
     below = ring(latent[:, :COLS], "ang", -1)
     wide = jnp.concatenate([above, latent, below], axis=1)
 
-    position = lax.broadcasted_iota(jnp.int32, (frame, taps * pixels), 0)
-    pick = (position == neighbours.reshape(1, taps * pixels)).astype(jnp.float32)
-    picked = jnp.dot(wide, pick, precision=HIGHEST, preferred_element_type=jnp.float32)
-    refined = jnp.zeros((shells, pixels), jnp.float32)
-    for offset in range(taps):
-        refined = refined + stencil[:, offset : offset + 1] * picked[:, offset * pixels : (offset + 1) * pixels]
+    rest = taps - 1
+    position = lax.broadcasted_iota(jnp.int32, (frame, rest * pixels), 0)
+    pick = (position == neighbours[1:].reshape(1, rest * pixels)).astype(jnp.bfloat16)
+    picked = select(wide, pick)
+    refined = stencil[:, 0:1] * latent
+    for offset in range(rest):
+        refined = refined + stencil[:, offset + 1 : offset + 2] * picked[:, offset * pixels : (offset + 1) * pixels]
     density = jnp.exp(refined)
     weighted = bin_width[:, None] * density
 
@@ -67,11 +88,9 @@
     sensitivity = adjoint_sum * weighted
 
     terms = jnp.concatenate(
-        [stencil[:, offset : offset + 1] * sensitivity for offset in range(taps)], axis=1
+        [stencil[:, offset + 1 : offset + 2] * sensitivity for offset in range(rest)], axis=1
     )
-    framed = lax.dot_general(
-        terms, pick, (((1,), (1,)), ((), ())), precision=HIGHEST, preferred_element_type=jnp.float32
-    )
+    framed = spread_select(terms, pick) + jnp.pad(stencil[:, 0:1] * sensitivity, ((0, 0), (COLS, COLS)))
     to_after, to_before = lax.optimization_barrier((framed[:, frame - COLS :], framed[:, :COLS]))
     from_before = ring(to_after, "ang", 1)
     from_after = ring(to_before, "ang", -1)

time: 71.4 us -> 69.5 us (0.973)
  matrix products: 10.6 us -> 7.09 us
  local copies, waits for them, and re-layouts: 4.95 us -> 6.12 us
    dot_general x2, matrix products: 5.29 us -> 1.79 us  [the longest x1 0.91 us: spread_select(): lax.dot_general(split3(value), onehot, (((1,), (1,)), ((), ())), preferre...]
    unnamed x12 -> x18, local copies, waits for them, and re-layouts: 0.51 us -> 2.4 us
    eq x1 -> x0, local copies, waits for them, and re-layouts: 0.72 us -> none  [on_device(): position == neighbours.reshape(1, taps * pixels)]
  transfers between devices with their start and end apart: 4 -> 4, of which waited for: 1 -> 1; matrix products, arithmetic and copies ran while one was open for 6% -> 8% of each run, Pallas kernels for 0% -> 0%
where the time goes in v6:
time: 69.5 us; the launch traced here: 68.8 us
  blocking collectives  26.1 us (38%)
  starting transfers between devices  24.9 us (36%)
  matrix products  7.09 us (10%)
  local copies, waits for them, and re-layouts  6.12 us (9%)
  other arithmetic  2.51 us (4%)
  waiting for transfers between devices  1.11 us (2%)
  between operations  0.93 us (1%)
    all_gather x1, blocking collectives, on_device(): predicted = jnp.sum(lax.all_gather(partial_value, 'rad'), axis=0)  26.1 us
    ppermute x4, starting transfers between devices, ring(): lax.ppermute(value, axis, [(i, (i + step) % count) for i in range(count)])  24.9 us
    dot_general x1, matrix products, on_device(): lax.dot_general(radial * weight_back[None, :], spread, (((1,), (1,)), (()...  2.9 us
    unnamed x18, local copies, waits for them, and re-layouts  2.4 us
    dot_general x1, matrix products, on_device(): jnp.dot(weighted, spread, precision=HIGHEST, preferred_element_type=jnp.f...  2.4 us
  transfers between devices with their start and end apart: 4, of which 1 were waited for; matrix products, arithmetic and copies ran while one was open for 8% of the time, Pallas kernels for 0%

profile of v6, /device:TPU:1, one launch (start us, length us, event | category | flops | bytes accessed | tf_op | source)
XLA Modules:
  0.0 68.8 jit_solution(7820122769709972004)
XLA Ops:
  0.6 0.8 %fusion.64 = (f32[88,128]{1,0:T(8,128)S(1)}, f32[88,128]{1,0:T(8,128)S(1)}) fusion(f32[88,256]{1,0:T(8,128)} %param.10), kind=kLoop, calls=%fused_computation.120 | loop fusion | bytes 180224 | tf_op jit(solution)/shard_map/slice | solution.py:52
  1.4 4.0 %collective-permute-start = (f32[88,128]{1,0:T(8,128)S(1)}, f32[88,128]{1,0:T(8,128)S(1)}, u32[]{:S(2)}, u32[]{:S(2)}) collective-permute-start(f32[88,128]{1,0:T(8,128)S(1)} %get-tuple-element.19), channel_id=1, source_target_pairs={{0,8},{8,16},{16,24},{24,32},{32,40},{40,48},{48,56},{56,64},{64,7... | collective-permute-start | bytes 135176 | tf_op jit(solution)/shard_map/ppermute | solution.py:32
  5.5 9.6 %collective-permute-start.1 = (f32[88,128]{1,0:T(8,128)S(1)}, f32[88,128]{1,0:T(8,128)S(1)}, u32[]{:S(2)}, u32[]{:S(2)}) collective-permute-start(f32[88,128]{1,0:T(8,128)S(1)} %get-tuple-element.18), channel_id=1, source_target_pairs={{0,504},{8,0},{16,8},{24,16},{32,24},{40,32},{48,40},{56,48},{64,5... | collective-permute-start | bytes 135176 | tf_op jit(solution)/shard_map/ppermute | solution.py:32
  15.1 0.7 %slice_bitcast_fusion = s32[1,2,8,128]{3,2,1,0:T(8,128)S(1)} fusion(s32[9,256]{1,0:T(8,128)} %param.13), kind=kLoop, calls=%fused_computation.102 | loop fusion | bytes 16384
  15.8 1.0 %slice_bitcast_fusion.9 = (f32[88]{0:T(128)S(1)}, f32[88]{0:T(128)S(1)}, f32[88]{0:T(128)S(1)}, f32[88]{0:T(128)S(1)}, f32[88]{0:T(128)S(1)}, /*index=5*/f32[88]...) fusion(f32[88,9]{0,1:T(8,128)} %param.11), kind=kLoop, calls=%fused_computation.112 | loop fusion | bytes 6336 | tf_op jit(solution)/shard_map/mul | solution.py:59
  16.8 0.9 %fusion.66 = (f32[1,2048]{1,0:T(1,128)S(1)}, f32[1,2048]{1,0:T(1,128)S(1)}, f32[1,2048]{1,0:T(1,128)S(1)}, f32[1,2048]{1,0:T(1,128)S(1)}) fusion(f32[4,2048]{1,0:T(4,128)} %param.16), kind=kLoop, calls=%fused_computation.122 | loop fusion | bytes 65536 | tf_op jit(solution)/shard_map/slice | solution.py:69
  17.8 0.9 %fusion.65 = (s32[1,2048]{1,0:T(1,128)S(1)}, s32[1,2048]{1,0:T(1,128)S(1)}, s32[1,2048]{1,0:T(1,128)S(1)}, s32[1,2048]{1,0:T(1,128)S(1)}) fusion(s32[4,2048]{1,0:T(4,128)} %param.15), kind=kLoop, calls=%fused_computation.121 | loop fusion | bytes 65536 | tf_op jit(solution)/shard_map/slice | solution.py:69
  18.7 0.7 %broadcast_add_fusion = s32[2048]{0:T(1024)S(1)} fusion(s32[2048]{0:T(1024)} %param.14), kind=kLoop, calls=%fused_computation.103 | loop fusion | flops 2048 | bytes 16384 | tf_op jit(solution)/shard_map/add | solution.py:74
  19.4 0.0 collective-permute-done
  19.4 0.9 %constant_dynamic-update-slice_fusion.1 = f32[88,512]{1,0:T(8,128)S(1)} fusion(f32[88,512]{1,0:T(8,128)S(1)} %constant_dynamic-update-slice_fusion.2, f32[88,256]{1,0:T(8,128)} %param.10), kind=kLoop, calls=%fused_computation.99 | loop fusion | bytes 180224
  20.3 0.0 collective-permute-done.1
  20.4 0.9 %fusion.1 = f32[264,2048]{1,0:T(8,128)S(1)} fusion(s32[2048]{0:T(1024)S(1)} %bitcast.30, bf16[88,512]{1,0:T(8,128)(2,1)S(1)} %get-tuple-element.14, bf16[88,512]{1,0:T(8,128)(2,1)S(1)} %get-tuple-element.15, bf16[88,512]{1,0:T(8,128)(2,1)S(1)} %get-tuple-element.13), kind=kOutput, calls=%fused_computation.2 | convolution fusion | flops 555507712 | bytes 2441216 | tf_op jit(solution)/shard_map/dot_general | solution.py:20
  21.3 0.0 copy-start
  21.3 0.0 copy-start.5
  21.3 0.0 copy-start.2
  21.3 0.0 copy-start.6
  21.3 0.1 slice_add_fusion
  21.5 0.7 %copy-done = f32[88,256]{1,0:T(8,128)S(1)} copy-done((f32[88,256]{1,0:T(8,128)S(1)}, f32[88,256]{1,0:T(8,128)}, u32[]{:S(2)}) %copy-start) | copy-done | bytes 90136
  22.2 0.0 copy-done.5
  22.2 0.2 fusion.50
  22.4 0.0 copy-done.2
  22.4 0.0 copy-done.6
  22.4 0.0 copy-start.3
  22.4 0.0 copy-start.4
  22.4 2.4 %fusion.5 = f32[2048]{0:T(1024)S(1)} fusion(f32[88,256]{1,0:T(8,128)S(1)} %fusion.50, f32[2048]{0:T(1024)S(1)} %bitcast.36, s32[2048]{0:T(1024)S(1)} %bitcast.44, f32[2048]{0:T(1024)S(1)} %bitcast.38, s32[2048]{0:T(1024)S(1)} %bitcast.46, f32[2048]{0:T(1024)S(1)} %bitcast.34, s32[2048]{0:T(1024)S(1)} %bitcast.42, f32[2048]{0:T(1024)S(1)} %bitcast.32, ...), kind=kOutput, calls=%fused_computation.12 | convolution fusion | flops 560494592 | bytes 188768 | tf_op jit(solution)/shard_map/dot_general | solution.py:76
  24.8 26.1 %all-gather = f32[16384]{0:T(1024)S(1)} all-gather(f32[2048]{0:T(1024)S(1)} %fusion.5), channel_id=2, replica_groups=mesh['ang'=64,'rad'=8] {'rad'}, dimensions={0}, use_global_device_ids=true | all-gather | bytes 73728 | tf_op jit(solution)/shard_map/all_gather | solution.py:78
  51.0 0.0 copy-done.3
  51.0 0.0 copy-done.4
  51.0 0.0 copy-start.1
  51.1 2.9 %multiply_dynamic-update-slice_fusion.7 = (f32[88,2048]{1,0:T(8,128)S(1)}, f32[88,256]{1,0:T(8,128)S(1)}) fusion(f32[88]{0:T(128)S(1)} %get-tuple-element.34, f32[88,256]{1,0:T(8,128)S(1)} %fusion.50, f32[2048]{0:T(1024)S(1)} %bitcast.37, s32[2048]{0:T(1024)S(1)} %bitcast.45, f32[2048]{0:T(1024)S(1)} %bitcast.39, s32[2048]{0:T(1024)S(1)} %bitcast.47, ...), kind=kOutput, calls=%fused_computation.94 | convolution fusion | flops 560361472 | bytes 369344 | tf_op jit(solution)/shard_map/dot_general | solution.py:81
  54.0 0.0 copy-done.1
  54.0 0.1 multiply_dynamic-update-slice_fusion.6
  54.1 0.1 multiply_dynamic-update-slice_fusion.5
  54.1 0.1 multiply_dynamic-update-slice_fusion.4
  54.2 0.1 multiply_dynamic-update-slice_fusion.3
  54.3 0.1 multiply_dynamic-update-slice_fusion.2
  54.4 0.1 multiply_dynamic-update-slice_fusion.1
  54.5 0.1 broadcast_multiply_fusion
  54.6 0.2 reduce-precision_convert_fusion.1
  54.7 0.9 %fusion = f32[264,512]{1,0:T(8,128)S(1)} fusion(s32[2048]{0:T(1024)S(1)} %bitcast.31, bf16[88,2048]{1,0:T(8,128)(2,1)S(1)} %get-tuple-element.7, bf16[88,2048]{1,0:T(8,128)(2,1)S(1)} %get-tuple-element.8, bf16[88,2048]{1,0:T(8,128)(2,1)S(1)} %get-tuple-element.6), kind=kOutput, calls=%fused_computation.1 | convolution fusion | flops 557940736 | bytes 1630208 | tf_op jit(solution)/shard_map/dot_general | solution.py:26
  55.7 1.9 %collective-permute-start.2 = (f32[88,128]{1,0:T(8,128)S(1)}, f32[88,128]{1,0:T(8,128)S(1)}, u32[]{:S(2)}, u32[]{:S(2)}) collective-permute-start(f32[88,128]{1,0:T(8,128)S(1)} %get-tuple-element.4), channel_id=1, source_target_pairs={{0,8},{8,16},{16,24},{24,32},{32,40},{40,48},{48,56},{56,64},{64,7... | collective-permute-start | bytes 135176 | tf_op jit(solution)/shard_map/ppermute | solution.py:32
  57.7 9.4 %collective-permute-start.3 = (f32[88,128]{1,0:T(8,128)S(1)}, f32[88,128]{1,0:T(8,128)S(1)}, u32[]{:S(2)}, u32[]{:S(2)}) collective-permute-start(f32[88,128]{1,0:T(8,128)S(1)} %get-tuple-element.5), channel_id=1, source_target_pairs={{0,504},{8,0},{16,8},{24,16},{32,24},{40,32},{48,40},{56,48},{64,5... | collective-permute-start | bytes 135176 | tf_op jit(solution)/shard_map/ppermute | solution.py:32
  67.0 0.0 collective-permute-done.2
  67.1 1.1 %collective-permute-done.3 = f32[88,128]{1,0:T(8,128)S(1)} collective-permute-done((f32[88,128]{1,0:T(8,128)S(1)}, f32[88,128]{1,0:T(8,128)S(1)}, u32[]{:S(2)}, u32[]{:S(2)}) %collective-permute-start.3) | collective-permute-done | bytes 45088 | tf_op jit(solution)/shard_map/ppermute | solution.py:32
  68.2 0.6 pad_maximum_fusion
  (11 shorter events, 0.2 us)
Async XLA Ops:
  1.4 18.0 %collective-permute-start = (f32[88,128]{1,0:T(8,128)S(1)}, f32[88,128]{1,0:T(8,128)S(1)}, u32[]{:S(2)}, u32[]{:S(2)}) collective-permute-start(f32[88,128]{1,0:T(8,128)S(1)} %get-tuple-element.19), channel_id=1, source_target_pairs={{0,8},{8,16},{16,24},{24,32},{32,40},{40,48},{48,56},{56,64},{64,7... | collective-permute-start | bytes 135176 | tf_op jit(solution)/shard_map/ppermute | solution.py:32
  5.5 14.9 %collective-permute-start.1 = (f32[88,128]{1,0:T(8,128)S(1)}, f32[88,128]{1,0:T(8,128)S(1)}, u32[]{:S(2)}, u32[]{:S(2)}) collective-permute-start(f32[88,128]{1,0:T(8,128)S(1)} %get-tuple-element.18), channel_id=1, source_target_pairs={{0,504},{8,0},{16,8},{24,16},{32,24},{40,32},{48,40},{56,48},{64,5... | collective-permute-start | bytes 135176 | tf_op jit(solution)/shard_map/ppermute | solution.py:32
  21.3 0.9 %copy-start = (f32[88,256]{1,0:T(8,128)S(1)}, f32[88,256]{1,0:T(8,128)}, u32[]{:S(2)}) copy-start(f32[88,256]{1,0:T(8,128)} %param.10) | copy-start | bytes 270340
  21.3 0.9 %copy-start.5 = (f32[88]{0:T(128)S(1)}, f32[88]{0:T(128)}, u32[]{:S(2)}) copy-start(f32[88]{0:T(128)} %param.12) | copy-start | bytes 1060
  21.3 1.1 %copy-start.2 = (s32[2048]{0:T(1024)S(1)}, s32[2048]{0:T(1024)}, u32[]{:S(2)}) copy-start(s32[2048]{0:T(1024)} %param.14) | copy-start | bytes 24580
  21.3 1.1 %copy-start.6 = (f32[2048]{0:T(1024)S(1)}, f32[2048]{0:T(1024)}, u32[]{:S(2)}) copy-start(f32[2048]{0:T(1024)} %param.17) | copy-start | bytes 24580
  22.4 28.6 %copy-start.3 = (f32[2048]{0:T(1024)S(1)}, f32[2048]{0:T(1024)}, u32[]{:S(2)}) copy-start(f32[2048]{0:T(1024)} %param.19) | copy-start | bytes 24580
  22.4 28.6 %copy-start.4 = (f32[2048]{0:T(1024)S(1)}, f32[2048]{0:T(1024)}, u32[]{:S(2)}) copy-start(f32[2048]{0:T(1024)} %param.18) | copy-start | bytes 24580
  51.0 2.9 %copy-start.1 = (f32[2048]{0:T(1024)}, f32[2048]{0:T(1024)S(1)}, u32[]{:S(2)}) copy-start(f32[2048]{0:T(1024)S(1)} %reduce_sum.19) | copy-start | bytes 24580
  55.7 11.3 %collective-permute-start.2 = (f32[88,128]{1,0:T(8,128)S(1)}, f32[88,128]{1,0:T(8,128)S(1)}, u32[]{:S(2)}, u32[]{:S(2)}) collective-permute-start(f32[88,128]{1,0:T(8,128)S(1)} %get-tuple-element.4), channel_id=1, source_target_pairs={{0,8},{8,16},{16,24},{24,32},{32,40},{40,48},{48,56},{56,64},{64,7... | collective-permute-start | bytes 135176 | tf_op jit(solution)/shard_map/ppermute | solution.py:32
  57.7 10.5 %collective-permute-start.3 = (f32[88,128]{1,0:T(8,128)S(1)}, f32[88,128]{1,0:T(8,128)S(1)}, u32[]{:S(2)}, u32[]{:S(2)}) collective-permute-start(f32[88,128]{1,0:T(8,128)S(1)} %get-tuple-element.5), channel_id=1, source_target_pairs={{0,504},{8,0},{16,8},{24,16},{32,24},{40,32},{48,40},{56,48},{64,5... | collective-permute-start | bytes 135176 | tf_op jit(solution)/shard_map/ppermute | solution.py:32

commit v7 on v6

--- a/solution.py
+++ b/solution.py
@@ -56,17 +56,14 @@
     position = lax.broadcasted_iota(jnp.int32, (frame, rest * pixels), 0)
     pick = (position == neighbours[1:].reshape(1, rest * pixels)).astype(jnp.bfloat16)
     picked = select(wide, pick)
-    refined = stencil[:, 0:1] * latent
-    for offset in range(rest):
-        refined = refined + stencil[:, offset + 1 : offset + 2] * picked[:, offset * pixels : (offset + 1) * pixels]
+    scaled = picked.reshape(shells, rest, pixels) * stencil[:, 1:, None]
+    refined = stencil[:, 0:1] * latent + jnp.sum(scaled, axis=1)
     density = jnp.exp(refined)
     weighted = bin_width[:, None] * density
 
     nstars = star_bin.shape[0]
     pixel_id = lax.broadcasted_iota(jnp.int32, (pixels, nstars), 0)
-    spread = jnp.zeros((pixels, nstars), jnp.float32)
-    for corner in range(star_pixels.shape[0]):
-        spread = spread + jnp.where(pixel_id == star_pixels[corner][None, :], star_weights[corner][None, :], 0.0)
+    spread = jnp.sum(jnp.where(pixel_id[None] == star_pixels[:, None, :], star_weights[:, None, :], 0.0), axis=0)
 
     shell_start = lax.axis_index("rad") * shells
     bin_id = shell_start + lax.broadcasted_iota(jnp.int32, (shells, nstars), 0)
@@ -87,9 +84,7 @@
     )
     sensitivity = adjoint_sum * weighted
 
-    terms = jnp.concatenate(
-        [stencil[:, offset + 1 : offset + 2] * sensitivity for offset in range(rest)], axis=1
-    )
+    terms = (stencil[:, 1:, None] * sensitivity[:, None, :]).reshape(shells, rest * pixels)
     framed = spread_select(terms, pick) + jnp.pad(stencil[:, 0:1] * sensitivity, ((0, 0), (COLS, COLS)))
     to_after, to_before = lax.optimization_barrier((framed[:, frame - COLS :], framed[:, :COLS]))
     from_before = ring(to_after, "ang", 1)

time: 69.5 us -> 66.3 us (0.954)
  local copies, waits for them, and re-layouts: 6.12 us -> 2.94 us
  other arithmetic: 2.51 us -> 4.48 us
  matrix products: 7.09 us -> 5.25 us
    reduce_sum x0 -> x2, other arithmetic: none -> 2.55 us  [the longest x1 2.28 us: on_device(): jnp.sum(jnp.where(pixel_id[None] == star_pixels[:, None, :], star_weights...]
    slice x2, local copies, waits for them, and re-layouts: 1.88 us -> 0.1 us  [on_device(): scaled = picked.reshape(shells, rest, pixels) * stencil[:, 1:, None]]
    unnamed x18 -> x22, local copies, waits for them, and re-layouts: 2.4 us -> 1.27 us
    dot_general x1, matrix products: 2.4 us -> 1.41 us  [on_device(): jnp.dot(weighted, spread, precision=HIGHEST, preferred_element_type=jnp.f...]
    dot_general x1, matrix products: 2.9 us -> 2.06 us  [on_device(): lax.dot_general(radial * weight_back[None, :], spread, (((1,), (1,)), (()...]
  transfers between devices with their start and end apart: 4 -> 4, of which waited for: 1 -> 1; matrix products, arithmetic and copies ran while one was open for 8% -> 7% of each run, Pallas kernels for 0% -> 0%
where the time goes in v7:
time: 66.3 us; the launch traced here: 65.8 us
  blocking collectives  26.1 us (39%)
  starting transfers between devices  24.9 us (38%)
  matrix products  5.25 us (8%)
  other arithmetic  4.48 us (7%)
  local copies, waits for them, and re-layouts  2.94 us (4%)
  waiting for transfers between devices  1.11 us (2%)
  between operations  0.95 us (1%)
    all_gather x1, blocking collectives, on_device(): predicted = jnp.sum(lax.all_gather(partial_value, 'rad'), axis=0)  26.1 us
    ppermute x4, starting transfers between devices, ring(): lax.ppermute(value, axis, [(i, (i + step) % count) for i in range(count)])  24.9 us
    reduce_sum x1, other arithmetic, on_device(): jnp.sum(jnp.where(pixel_id[None] == star_pixels[:, None, :], star_weights...  2.28 us
    dot_general x1, matrix products, on_device(): lax.dot_general(radial * weight_back[None, :], spread, (((1,), (1,)), (()...  2.06 us
    dot_general x1, matrix products, on_device(): jnp.dot(weighted, spread, precision=HIGHEST, preferred_element_type=jnp.f...  1.41 us
  transfers between devices with their start and end apart: 4, of which 1 were waited for; matrix products, arithmetic and copies ran while one was open for 7% of the time, Pallas kernels for 0%

profile of v7, /device:TPU:1, one launch (start us, length us, event | category | flops | bytes accessed | tf_op | source)
XLA Modules:
  0.0 65.8 jit_solution(11605513390540794748)
XLA Ops:
  0.6 0.0 copy-start
  0.6 0.0 copy-start.7
  0.7 0.9 %fusion.34 = (f32[88,128]{1,0:T(8,128)S(1)}, f32[88,128]{1,0:T(8,128)S(1)}) fusion(f32[88,256]{1,0:T(8,128)} %param.10), kind=kLoop, calls=%fused_computation.67 | loop fusion | bytes 180224 | tf_op jit(solution)/shard_map/slice | solution.py:52
  1.5 4.0 %collective-permute-start = (f32[88,128]{1,0:T(8,128)S(1)}, f32[88,128]{1,0:T(8,128)S(1)}, u32[]{:S(2)}, u32[]{:S(2)}) collective-permute-start(f32[88,128]{1,0:T(8,128)S(1)} %get-tuple-element.17), channel_id=1, source_target_pairs={{0,8},{8,16},{16,24},{24,32},{32,40},{40,48},{48,56},{56,64},{64,7... | collective-permute-start | bytes 135176 | tf_op jit(solution)/shard_map/ppermute | solution.py:32
  5.5 9.6 %collective-permute-start.1 = (f32[88,128]{1,0:T(8,128)S(1)}, f32[88,128]{1,0:T(8,128)S(1)}, u32[]{:S(2)}, u32[]{:S(2)}) collective-permute-start(f32[88,128]{1,0:T(8,128)S(1)} %get-tuple-element.16), channel_id=1, source_target_pairs={{0,504},{8,0},{16,8},{24,16},{32,24},{40,32},{48,40},{56,48},{64,5... | collective-permute-start | bytes 135176 | tf_op jit(solution)/shard_map/ppermute | solution.py:32
  15.2 0.7 %slice_bitcast_fusion = s32[1,2,8,128]{3,2,1,0:T(8,128)S(1)} fusion(s32[9,256]{1,0:T(8,128)} %param.13), kind=kLoop, calls=%fused_computation.58 | loop fusion | bytes 16384
  15.9 0.7 %broadcast_add_fusion = s32[2048]{0:T(1024)S(1)} fusion(s32[2048]{0:T(1024)} %param.14), kind=kLoop, calls=%fused_computation.59 | loop fusion | flops 2048 | bytes 16384 | tf_op jit(solution)/shard_map/add | solution.py:71
  16.6 0.7 %slice_bitcast_fusion.1 = f32[88]{0:T(128)S(1)} fusion(f32[88,9]{0,1:T(8,128)} %param.11), kind=kLoop, calls=%fused_computation.60 | loop fusion | bytes 704 | tf_op jit(solution)/shard_map/mul | solution.py:60
  17.3 2.3 %select_reduce_fusion = f32[256,2048]{1,0:T(8,128)S(1)} fusion(f32[4,2048]{1,0:T(4,128)} %param.16, s32[4,2048]{1,0:T(4,128)} %param.15), kind=kLoop, calls=%fused_computation | loop fusion | flops 5767168 | bytes 2162688 | tf_op jit(solution)/shard_map/reduce_sum | solution.py:66
  19.6 0.0 copy-done.7
  19.6 0.1 copy.14
  19.7 0.0 collective-permute-done
  19.7 0.0 copy-done
  19.7 0.0 collective-permute-done.1
  19.8 0.9 %fusion.1 = f32[264,2048]{1,0:T(8,128)S(1)} fusion(s32[2048]{0:T(1024)S(1)} %bitcast.17, bf16[88,512]{1,0:T(8,128)(2,1)S(1)} %get-tuple-element.14, bf16[88,512]{1,0:T(8,128)(2,1)S(1)} %get-tuple-element.15, bf16[88,512]{1,0:T(8,128)(2,1)S(1)} %get-tuple-element.13), kind=kOutput, calls=%fused_computation.4 | convolution fusion | flops 555507712 | bytes 2441216 | tf_op jit(solution)/shard_map/dot_general | solution.py:20
  20.7 0.0 copy-start.1
  20.7 0.0 copy-start.2
  20.7 0.0 copy-start.6
  20.7 0.1 slice_add_fusion
  20.9 0.0 copy-start.4
  20.9 0.0 copy-start.5
  20.9 0.2 copy.16
  21.1 0.3 fusion.11
  21.4 0.0 copy-done.1
  21.4 0.0 copy-done.2
  21.4 0.0 copy-done.6
  21.4 1.4 %fusion.4 = f32[2048]{0:T(1024)S(1)} fusion(f32[256,2048]{1,0:T(8,128)S(1)} %select_reduce_fusion, f32[2048]{0:T(1024)S(1)} %copy-done.2, s32[2048]{0:T(1024)S(1)} %broadcast_add_fusion, s32[2048]{0:T(1024)S(1)} %copy-done.1, s32[88]{0:T(128)S(1)} %iota_add_fusion, f32[88,256]{1,0:T(8,128)S(1)} %fusion.11, f32[88,256]{1,0:T(8,128)S(1)} %copy-done, ...), kind=kOutput, calls=%fused_computation.8 | convolution fusion | flops 554795008 | bytes 2311200 | tf_op jit(solution)/shard_map/dot_general | solution.py:73
  22.8 26.1 %all-gather = f32[16384]{0:T(1024)S(1)} all-gather(f32[2048]{0:T(1024)S(1)} %fusion.4), channel_id=2, replica_groups=mesh['ang'=64,'rad'=8] {'rad'}, dimensions={0}, use_global_device_ids=true | all-gather | bytes 73728 | tf_op jit(solution)/shard_map/all_gather | solution.py:75
  49.0 0.0 copy-done.4
  49.0 0.0 copy-done.5
  49.0 0.0 copy-start.3
  49.1 2.1 %broadcast_multiply_fusion.1 = (f32[88,256]{1,0:T(8,128)S(1)}, f32[88,256]{1,0:T(8,128)S(1)}) fusion(f32[88]{0:T(128)S(1)} %slice_bitcast_fusion.1, f32[88,256]{1,0:T(8,128)S(1)} %fusion.11, f32[88,256]{1,0:T(8,128)S(1)} %copy-done, f32[88]{0:T(128)S(1)} %copy-done.6, f32[256,2048]{1,0:T(8,128)S(1)} %select_reduce_fusion, ...), kind=kOutput, calls=%fused_computation.53 | convolution fusion | flops 554661888 | bytes 2491424 | tf_op jit(solution)/shard_map/dot_general | solution.py:78
  51.1 0.2 broadcast_multiply_fusion
  51.3 0.2 copy.17
  51.5 0.0 copy-done.3
  51.5 0.2 reduce-precision_convert_fusion.1
  51.7 0.9 %fusion = f32[264,512]{1,0:T(8,128)S(1)} fusion(s32[2048]{0:T(1024)S(1)} %bitcast.18, bf16[88,2048]{1,0:T(8,128)(2,1)S(1)} %get-tuple-element.7, bf16[88,2048]{1,0:T(8,128)(2,1)S(1)} %get-tuple-element.8, bf16[88,2048]{1,0:T(8,128)(2,1)S(1)} %get-tuple-element.6), kind=kOutput, calls=%fused_computation.3 | convolution fusion | flops 557940736 | bytes 1630208 | tf_op jit(solution)/shard_map/dot_general | solution.py:26
  52.7 1.9 %collective-permute-start.2 = (f32[88,128]{1,0:T(8,128)S(1)}, f32[88,128]{1,0:T(8,128)S(1)}, u32[]{:S(2)}, u32[]{:S(2)}) collective-permute-start(f32[88,128]{1,0:T(8,128)S(1)} %get-tuple-element.4), channel_id=1, source_target_pairs={{0,8},{8,16},{16,24},{24,32},{32,40},{40,48},{48,56},{56,64},{64,7... | collective-permute-start | bytes 135176 | tf_op jit(solution)/shard_map/ppermute | solution.py:32
  54.6 9.4 %collective-permute-start.3 = (f32[88,128]{1,0:T(8,128)S(1)}, f32[88,128]{1,0:T(8,128)S(1)}, u32[]{:S(2)}, u32[]{:S(2)}) collective-permute-start(f32[88,128]{1,0:T(8,128)S(1)} %get-tuple-element.5), channel_id=1, source_target_pairs={{0,504},{8,0},{16,8},{24,16},{32,24},{40,32},{48,40},{56,48},{64,5... | collective-permute-start | bytes 135176 | tf_op jit(solution)/shard_map/ppermute | solution.py:32
  64.0 0.0 collective-permute-done.2
  64.0 1.1 %collective-permute-done.3 = f32[88,128]{1,0:T(8,128)S(1)} collective-permute-done((f32[88,128]{1,0:T(8,128)S(1)}, f32[88,128]{1,0:T(8,128)S(1)}, u32[]{:S(2)}, u32[]{:S(2)}) %collective-permute-start.3) | collective-permute-done | bytes 45088 | tf_op jit(solution)/shard_map/ppermute | solution.py:32
  65.2 0.6 pad_maximum_fusion
  (13 shorter events, 0.2 us)
Async XLA Ops:
  0.6 19.1 %copy-start = (f32[88,256]{1,0:T(8,128)S(1)}, f32[88,256]{1,0:T(8,128)}, u32[]{:S(2)}) copy-start(f32[88,256]{1,0:T(8,128)} %param.10) | copy-start | bytes 270340
  0.6 18.9 %copy-start.7 = (f32[88,9]{0,1:T(8,128)S(1)}, f32[88,9]{0,1:T(8,128)}, u32[]{:S(2)}) copy-start(f32[88,9]{0,1:T(8,128)} %param.11) | copy-start | bytes 9508
  1.5 18.2 %collective-permute-start = (f32[88,128]{1,0:T(8,128)S(1)}, f32[88,128]{1,0:T(8,128)S(1)}, u32[]{:S(2)}, u32[]{:S(2)}) collective-permute-start(f32[88,128]{1,0:T(8,128)S(1)} %get-tuple-element.17), channel_id=1, source_target_pairs={{0,8},{8,16},{16,24},{24,32},{32,40},{40,48},{48,56},{56,64},{64,7... | collective-permute-start | bytes 135176 | tf_op jit(solution)/shard_map/ppermute | solution.py:32
  5.5 14.2 %collective-permute-start.1 = (f32[88,128]{1,0:T(8,128)S(1)}, f32[88,128]{1,0:T(8,128)S(1)}, u32[]{:S(2)}, u32[]{:S(2)}) collective-permute-start(f32[88,128]{1,0:T(8,128)S(1)} %get-tuple-element.16), channel_id=1, source_target_pairs={{0,504},{8,0},{16,8},{24,16},{32,24},{40,32},{48,40},{56,48},{64,5... | collective-permute-start | bytes 135176 | tf_op jit(solution)/shard_map/ppermute | solution.py:32
  20.7 0.7 %copy-start.1 = (s32[2048]{0:T(1024)S(1)}, s32[2048]{0:T(1024)}, u32[]{:S(2)}) copy-start(s32[2048]{0:T(1024)} %param.14) | copy-start | bytes 24580
  20.7 0.7 %copy-start.2 = (f32[2048]{0:T(1024)S(1)}, f32[2048]{0:T(1024)}, u32[]{:S(2)}) copy-start(f32[2048]{0:T(1024)} %param.17) | copy-start | bytes 24580
  20.7 0.7 %copy-start.6 = (f32[88]{0:T(128)S(1)}, f32[88]{0:T(128)}, u32[]{:S(2)}) copy-start(f32[88]{0:T(128)} %param.12) | copy-start | bytes 1060
  20.9 28.2 %copy-start.4 = (f32[2048]{0:T(1024)S(1)}, f32[2048]{0:T(1024)}, u32[]{:S(2)}) copy-start(f32[2048]{0:T(1024)} %param.19) | copy-start | bytes 24580
  20.9 28.2 %copy-start.5 = (f32[2048]{0:T(1024)S(1)}, f32[2048]{0:T(1024)}, u32[]{:S(2)}) copy-start(f32[2048]{0:T(1024)} %param.18) | copy-start | bytes 24580
  49.0 2.5 %copy-start.3 = (f32[2048]{0:T(1024)}, f32[2048]{0:T(1024)S(1)}, u32[]{:S(2)}) copy-start(f32[2048]{0:T(1024)S(1)} %reduce_sum.39) | copy-start | bytes 24580
  52.7 11.3 %collective-permute-start.2 = (f32[88,128]{1,0:T(8,128)S(1)}, f32[88,128]{1,0:T(8,128)S(1)}, u32[]{:S(2)}, u32[]{:S(2)}) collective-permute-start(f32[88,128]{1,0:T(8,128)S(1)} %get-tuple-element.4), channel_id=1, source_target_pairs={{0,8},{8,16},{16,24},{24,32},{32,40},{40,48},{48,56},{56,64},{64,7... | collective-permute-start | bytes 135176 | tf_op jit(solution)/shard_map/ppermute | solution.py:32
  54.6 10.5 %collective-permute-start.3 = (f32[88,128]{1,0:T(8,128)S(1)}, f32[88,128]{1,0:T(8,128)S(1)}, u32[]{:S(2)}, u32[]{:S(2)}) collective-permute-start(f32[88,128]{1,0:T(8,128)S(1)} %get-tuple-element.5), channel_id=1, source_target_pairs={{0,504},{8,0},{16,8},{24,16},{32,24},{40,32},{48,40},{56,48},{64,5... | collective-permute-start | bytes 135176 | tf_op jit(solution)/shard_map/ppermute | solution.py:32

commit v8 on v7

--- a/solution.py
+++ b/solution.py
@@ -17,13 +17,15 @@
 
 def select(value, onehot):
     rows = value.shape[0]
-    product = jnp.dot(split3(value), onehot, preferred_element_type=jnp.float32)
+    product = lax.dot_general(split3(value), onehot, (((1,), (0,)), ((), ())), preferred_element_type=jnp.float32)
     return product[:rows] + product[rows : 2 * rows] + product[2 * rows :]
 
 
 def spread_select(value, onehot):
     rows = value.shape[0]
-    product = lax.dot_general(split3(value), onehot, (((1,), (1,)), ((), ())), preferred_element_type=jnp.float32)
+    product = lax.dot_general(
+        split3(value), onehot, (((1, 2), (1, 2)), ((), ())), preferred_element_type=jnp.float32
+    )
     return product[:rows] + product[rows : 2 * rows] + product[2 * rows :]
 
 
@@ -52,12 +54,10 @@
     below = ring(latent[:, :COLS], "ang", -1)
     wide = jnp.concatenate([above, latent, below], axis=1)
 
-    rest = taps - 1
-    position = lax.broadcasted_iota(jnp.int32, (frame, rest * pixels), 0)
-    pick = (position == neighbours[1:].reshape(1, rest * pixels)).astype(jnp.bfloat16)
+    position = lax.broadcasted_iota(jnp.int32, (frame, taps, pixels), 0)
+    pick = (position == neighbours[None, :, :]).astype(jnp.bfloat16)
     picked = select(wide, pick)
-    scaled = picked.reshape(shells, rest, pixels) * stencil[:, 1:, None]
-    refined = stencil[:, 0:1] * latent + jnp.sum(scaled, axis=1)
+    refined = jnp.sum(picked * stencil[:, :, None], axis=1)
     density = jnp.exp(refined)
     weighted = bin_width[:, None] * density
 
@@ -68,7 +68,7 @@
     shell_start = lax.axis_index("rad") * shells
     bin_id = shell_start + lax.broadcasted_iota(jnp.int32, (shells, nstars), 0)
     lower = star_bin[None, :]
-    radial = jnp.where(bin_id <= lower, 1.0, jnp.where(bin_id == lower + 1, star_frac[None, :], 0.0))
+    radial = jnp.where(bin_id <= lower, 1.0, jnp.where(bin_id - 1 == lower, star_frac[None, :], 0.0))
 
     at_stars = jnp.dot(weighted, spread, precision=HIGHEST, preferred_element_type=jnp.float32)
     partial_value = jnp.sum(radial * at_stars, axis=0)
@@ -84,8 +84,8 @@
     )
     sensitivity = adjoint_sum * weighted
 
-    terms = (stencil[:, 1:, None] * sensitivity[:, None, :]).reshape(shells, rest * pixels)
-    framed = spread_select(terms, pick) + jnp.pad(stencil[:, 0:1] * sensitivity, ((0, 0), (COLS, COLS)))
+    terms = stencil[:, :, None] * sensitivity[:, None, :]
+    framed = spread_select(terms, pick)
     to_after, to_before = lax.optimization_barrier((framed[:, frame - COLS :], framed[:, :COLS]))
     from_before = ring(to_after, "ang", 1)
     from_after = ring(to_before, "ang", -1)

time: 66.3 us -> 63.9 us (0.964)
  local copies, waits for them, and re-layouts: 2.94 us -> 1.42 us
  other arithmetic: 4.48 us -> 3.48 us
    add x3 -> x1, other arithmetic: 0.85 us -> 0.04 us  [spread_select(): return product[:rows] + product[rows:2 * rows] + product[2 * rows:]]
    unnamed x22 -> x20, local copies, waits for them, and re-layouts: 1.27 us -> 0.54 us
    mul x1 -> x0, local copies, waits for them, and re-layouts: 0.69 us -> none  [on_device(): refined = stencil[:, 0:1] * latent + jnp.sum(scaled, axis=1)]
  transfers between devices with their start and end apart: 4 -> 4, of which waited for: 1 -> 1; matrix products, arithmetic and copies ran while one was open for 7% -> 4% of each run, Pallas kernels for 0% -> 0%
where the time goes in v8:
time: 63.9 us; the launch traced here: 63.5 us
  blocking collectives  26.1 us (41%)
  starting transfers between devices  24.9 us (39%)
  matrix products  5.5 us (9%)
  other arithmetic  3.48 us (5%)
  local copies, waits for them, and re-layouts  1.42 us (2%)
  waiting for transfers between devices  1.11 us (2%)
  between operations  0.93 us (1%)
    all_gather x1, blocking collectives, on_device(): predicted = jnp.sum(lax.all_gather(partial_value, 'rad'), axis=0)  26.1 us
    ppermute x4, starting transfers between devices, ring(): lax.ppermute(value, axis, [(i, (i + step) % count) for i in range(count)])  24.9 us
    reduce_sum x1, other arithmetic, on_device(): jnp.sum(jnp.where(pixel_id[None] == star_pixels[:, None, :], star_weights...  2.29 us
    dot_general x1, matrix products, on_device(): lax.dot_general(radial * weight_back[None, :], spread, (((1,), (1,)), (()...  2.06 us
    dot_general x1, matrix products, on_device(): jnp.dot(weighted, spread, precision=HIGHEST, preferred_element_type=jnp.f...  1.4 us
  transfers between devices with their start and end apart: 4, of which 1 were waited for; matrix products, arithmetic and copies ran while one was open for 4% of the time, Pallas kernels for 0%

profile of v8, /device:TPU:1, one launch (start us, length us, event | category | flops | bytes accessed | tf_op | source)
XLA Modules:
  0.0 63.5 jit_solution(7795901153964238690)
XLA Ops:
  0.6 0.0 copy-start
  0.6 0.0 copy-start.8
  0.6 0.9 %fusion.35 = (f32[88,128]{1,0:T(8,128)S(1)}, f32[88,128]{1,0:T(8,128)S(1)}) fusion(f32[88,256]{1,0:T(8,128)} %param.10), kind=kLoop, calls=%fused_computation.64 | loop fusion | bytes 180224 | tf_op jit(solution)/shard_map/slice | solution.py:54
  1.5 4.0 %collective-permute-start = (f32[88,128]{1,0:T(8,128)S(1)}, f32[88,128]{1,0:T(8,128)S(1)}, u32[]{:S(2)}, u32[]{:S(2)}) collective-permute-start(f32[88,128]{1,0:T(8,128)S(1)} %get-tuple-element.17), channel_id=1, source_target_pairs={{0,8},{8,16},{16,24},{24,32},{32,40},{40,48},{48,56},{56,64},{64,7... | collective-permute-start | bytes 135176 | tf_op jit(solution)/shard_map/ppermute | solution.py:34
  5.5 9.6 %collective-permute-start.1 = (f32[88,128]{1,0:T(8,128)S(1)}, f32[88,128]{1,0:T(8,128)S(1)}, u32[]{:S(2)}, u32[]{:S(2)}) collective-permute-start(f32[88,128]{1,0:T(8,128)S(1)} %get-tuple-element.16), channel_id=1, source_target_pairs={{0,504},{8,0},{16,8},{24,16},{32,24},{40,32},{48,40},{56,48},{64,5... | collective-permute-start | bytes 135176 | tf_op jit(solution)/shard_map/ppermute | solution.py:34
  15.2 2.3 %select_reduce_fusion = f32[256,2048]{1,0:T(8,128)S(1)} fusion(f32[4,2048]{1,0:T(4,128)} %param.16, s32[4,2048]{1,0:T(4,128)} %param.15), kind=kLoop, calls=%fused_computation | loop fusion | flops 5767168 | bytes 2162688 | tf_op jit(solution)/shard_map/reduce_sum | solution.py:66
  17.5 0.0 collective-permute-done
  17.5 0.0 copy-done
  17.5 0.0 copy-start.3
  17.5 0.0 collective-permute-done.1
  17.6 0.0 copy-done.8
  17.6 1.1 %fusion.1 = f32[264,9,256]{2,0,1:T(8,128)S(1)} fusion(s32[9,256]{1,0:T(8,128)S(1)} %copy-done.8, bf16[88,512]{1,0:T(8,128)(2,1)S(1)} %get-tuple-element.11, bf16[88,512]{1,0:T(8,128)(2,1)S(1)} %get-tuple-element.12, bf16[88,512]{1,0:T(8,128)(2,1)S(1)} %get-tuple-element.10), kind=kOutput, calls=%fused_computation.4 | convolution fusion | flops 624844800 | bytes 2712576 | tf_op jit(solution)/shard_map/dot_general | solution.py:20
  18.7 0.0 copy-done.3
  18.7 0.0 copy-start.1
  18.7 0.0 copy-start.2
  18.7 0.0 copy-start.7
  18.7 0.0 copy-start.5
  18.7 0.0 copy-start.6
  18.7 0.2 fusion.13
  18.9 0.5 copy-done.1
  19.4 0.0 copy-done.2
  19.4 0.0 copy-done.7
  19.4 1.4 %fusion.10 = f32[2048]{0:T(1024)S(1)} fusion(f32[256,2048]{1,0:T(8,128)S(1)} %select_reduce_fusion, f32[2048]{0:T(1024)S(1)} %copy-done.1, s32[2048]{0:T(1024)S(1)} %copy-done.2, s32[88]{0:T(128)S(1)} %get-tuple-element.19, s32[88]{0:T(128)S(1)} %get-tuple-element.18, f32[88,256]{1,0:T(8,128)S(1)} %fusion.13, f32[88]{0:T(128)S(1)} %copy-done.7), kind=kOutput, calls=%fused_computation.14 | convolution fusion | flops 554749952 | bytes 2212896 | tf_op jit(solution)/shard_map/dot_general | solution.py:73
  20.8 26.1 %all-gather = f32[16384]{0:T(1024)S(1)} all-gather(f32[2048]{0:T(1024)S(1)} %fusion.10), channel_id=2, replica_groups=mesh['ang'=64,'rad'=8] {'rad'}, dimensions={0}, use_global_device_ids=true | all-gather | bytes 73728 | tf_op jit(solution)/shard_map/all_gather | solution.py:75
  47.0 0.0 copy-done.5
  47.0 0.0 copy-done.6
  47.0 0.0 copy-start.4
  47.0 2.1 %convolution_multiply_fusion.1 = f32[88,256]{1,0:T(8,128)S(1)} fusion(f32[256,2048]{1,0:T(8,128)S(1)} %select_reduce_fusion, f32[2048]{0:T(1024)S(1)} %multiply_divide_fusion, f32[2048]{0:T(1024)S(1)} %copy-done.1, s32[2048]{0:T(1024)S(1)} %copy-done.2, s32[88]{0:T(128)S(1)} %get-tuple-element.19, s32[88]{0:T(128)S(1)} %get-tuple-element.18, ...), kind=kOutput, calls=%fused_computation.19 | convolution fusion | flops 554594304 | bytes 2303008 | tf_op jit(solution)/shard_map/dot_general | solution.py:78
  49.1 0.2 reduce-precision_convert_fusion.1
  49.4 1.0 %fusion.4 = f32[264,512]{1,0:T(8,128)S(1)} fusion(s32[9,256]{1,0:T(8,128)S(1)} %copy-done.8, bf16[88,9,256]{2,0,1:T(8,128)(2,1)S(1)} %get-tuple-element.15, bf16[88,9,256]{2,0,1:T(8,128)(2,1)S(1)} %get-tuple-element.14, bf16[88,9,256]{2,0,1:T(8,128)(2,1)S(1)} %get-tuple-element.13), kind=kOutput, calls=%fused_computation.8 | convolution fusion | flops 627683328 | bytes 1766400 | tf_op jit(solution)/shard_map/dot_general | solution.py:26
  50.3 0.0 copy-done.4
  50.4 1.9 %collective-permute-start.2 = (f32[88,128]{1,0:T(8,128)S(1)}, f32[88,128]{1,0:T(8,128)S(1)}, u32[]{:S(2)}, u32[]{:S(2)}) collective-permute-start(f32[88,128]{1,0:T(8,128)S(1)} %get-tuple-element.4), channel_id=1, source_target_pairs={{0,8},{8,16},{16,24},{24,32},{32,40},{40,48},{48,56},{56,64},{64,7... | collective-permute-start | bytes 135176 | tf_op jit(solution)/shard_map/ppermute | solution.py:34
  52.3 9.4 %collective-permute-start.3 = (f32[88,128]{1,0:T(8,128)S(1)}, f32[88,128]{1,0:T(8,128)S(1)}, u32[]{:S(2)}, u32[]{:S(2)}) collective-permute-start(f32[88,128]{1,0:T(8,128)S(1)} %get-tuple-element.5), channel_id=1, source_target_pairs={{0,504},{8,0},{16,8},{24,16},{32,24},{40,32},{48,40},{56,48},{64,5... | collective-permute-start | bytes 135176 | tf_op jit(solution)/shard_map/ppermute | solution.py:34
  61.7 0.0 collective-permute-done.2
  61.7 1.1 %collective-permute-done.3 = f32[88,128]{1,0:T(8,128)S(1)} collective-permute-done((f32[88,128]{1,0:T(8,128)S(1)}, f32[88,128]{1,0:T(8,128)S(1)}, u32[]{:S(2)}, u32[]{:S(2)}) %collective-permute-start.3) | collective-permute-done | bytes 45088 | tf_op jit(solution)/shard_map/ppermute | solution.py:34
  62.9 0.6 %pad_maximum_fusion = f32[88,256]{1,0:T(8,128)} fusion(f32[88,128]{1,0:T(8,128)S(1)} %get-tuple-element.7, f32[88,128]{1,0:T(8,128)S(1)} %get-tuple-element.6), kind=kLoop, calls=%fused_computation.48 | loop fusion | flops 22528 | bytes 180224 | tf_op jit(solution)/shard_map/concatenate | solution.py:93
  (11 shorter events, 0.2 us)
Async XLA Ops:
  0.6 16.9 %copy-start = (f32[88,256]{1,0:T(8,128)S(1)}, f32[88,256]{1,0:T(8,128)}, u32[]{:S(2)}) copy-start(f32[88,256]{1,0:T(8,128)} %param.10) | copy-start | bytes 270340
  0.6 17.0 %copy-start.8 = (s32[9,256]{1,0:T(8,128)S(1)}, s32[9,256]{1,0:T(8,128)}, u32[]{:S(2)}) copy-start(s32[9,256]{1,0:T(8,128)} %param.13) | copy-start | bytes 27652
  1.5 16.0 %collective-permute-start = (f32[88,128]{1,0:T(8,128)S(1)}, f32[88,128]{1,0:T(8,128)S(1)}, u32[]{:S(2)}, u32[]{:S(2)}) collective-permute-start(f32[88,128]{1,0:T(8,128)S(1)} %get-tuple-element.17), channel_id=1, source_target_pairs={{0,8},{8,16},{16,24},{24,32},{32,40},{40,48},{48,56},{56,64},{64,7... | collective-permute-start | bytes 135176 | tf_op jit(solution)/shard_map/ppermute | solution.py:34
  5.5 12.0 %collective-permute-start.1 = (f32[88,128]{1,0:T(8,128)S(1)}, f32[88,128]{1,0:T(8,128)S(1)}, u32[]{:S(2)}, u32[]{:S(2)}) collective-permute-start(f32[88,128]{1,0:T(8,128)S(1)} %get-tuple-element.16), channel_id=1, source_target_pairs={{0,504},{8,0},{16,8},{24,16},{32,24},{40,32},{48,40},{56,48},{64,5... | collective-permute-start | bytes 135176 | tf_op jit(solution)/shard_map/ppermute | solution.py:34
  17.5 1.2 %copy-start.3 = (f32[88,9]{0,1:T(8,128)S(1)}, f32[88,9]{0,1:T(8,128)}, u32[]{:S(2)}) copy-start(f32[88,9]{0,1:T(8,128)} %param.11) | copy-start | bytes 9508
  18.7 0.7 %copy-start.1 = (f32[2048]{0:T(1024)S(1)}, f32[2048]{0:T(1024)}, u32[]{:S(2)}) copy-start(f32[2048]{0:T(1024)} %param.17) | copy-start | bytes 24580
  18.7 0.7 %copy-start.2 = (s32[2048]{0:T(1024)S(1)}, s32[2048]{0:T(1024)}, u32[]{:S(2)}) copy-start(s32[2048]{0:T(1024)} %param.14) | copy-start | bytes 24580
  18.7 0.7 %copy-start.7 = (f32[88]{0:T(128)S(1)}, f32[88]{0:T(128)}, u32[]{:S(2)}) copy-start(f32[88]{0:T(128)} %param.12) | copy-start | bytes 1060
  18.7 28.3 %copy-start.5 = (f32[2048]{0:T(1024)S(1)}, f32[2048]{0:T(1024)}, u32[]{:S(2)}) copy-start(f32[2048]{0:T(1024)} %param.19) | copy-start | bytes 24580
  18.7 28.3 %copy-start.6 = (f32[2048]{0:T(1024)S(1)}, f32[2048]{0:T(1024)}, u32[]{:S(2)}) copy-start(f32[2048]{0:T(1024)} %param.18) | copy-start | bytes 24580
  47.0 3.3 %copy-start.4 = (f32[2048]{0:T(1024)}, f32[2048]{0:T(1024)S(1)}, u32[]{:S(2)}) copy-start(f32[2048]{0:T(1024)S(1)} %reduce_sum.39) | copy-start | bytes 24580
  50.4 11.3 %collective-permute-start.2 = (f32[88,128]{1,0:T(8,128)S(1)}, f32[88,128]{1,0:T(8,128)S(1)}, u32[]{:S(2)}, u32[]{:S(2)}) collective-permute-start(f32[88,128]{1,0:T(8,128)S(1)} %get-tuple-element.4), channel_id=1, source_target_pairs={{0,8},{8,16},{16,24},{24,32},{32,40},{40,48},{48,56},{56,64},{64,7... | collective-permute-start | bytes 135176 | tf_op jit(solution)/shard_map/ppermute | solution.py:34
  52.3 10.5 %collective-permute-start.3 = (f32[88,128]{1,0:T(8,128)S(1)}, f32[88,128]{1,0:T(8,128)S(1)}, u32[]{:S(2)}, u32[]{:S(2)}) collective-permute-start(f32[88,128]{1,0:T(8,128)S(1)} %get-tuple-element.5), channel_id=1, source_target_pairs={{0,504},{8,0},{16,8},{24,16},{32,24},{40,32},{48,40},{56,48},{64,5... | collective-permute-start | bytes 135176 | tf_op jit(solution)/shard_map/ppermute | solution.py:34

commit v9 on v8

--- a/solution.py
+++ b/solution.py
@@ -72,7 +72,8 @@
 
     at_stars = jnp.dot(weighted, spread, precision=HIGHEST, preferred_element_type=jnp.float32)
     partial_value = jnp.sum(radial * at_stars, axis=0)
-    predicted = jnp.sum(lax.all_gather(partial_value, "rad"), axis=0)
+    padded = jnp.pad(partial_value, (0, 7 * nstars))
+    predicted = lax.psum(padded, "rad")[:nstars]
     weight_back = (predicted - observed) / (sigma * sigma)
 
     adjoint_sum = lax.dot_general(

time: 63.9 us -> 152 us (2.38)
  waiting for transfers between devices: 1.11 us -> 100 us
  blocking collectives: 26.1 us -> 0 us
  between operations: 0.93 us -> 14.3 us
    psum x0 -> x1, waiting for transfers between devices: none -> 99.1 us  [on_device(): predicted = lax.psum(padded, 'rad')[:nstars]]
    all_gather x1 -> x0, blocking collectives: 26.1 us -> none  [on_device(): predicted = jnp.sum(lax.all_gather(partial_value, 'rad'), axis=0)]
  transfers between devices with their start and end apart: 4 -> 5, of which waited for: 1 -> 2; matrix products, arithmetic and copies ran while one was open for 4% -> 2% of each run, Pallas kernels for 0% -> 0%
where the time goes in v9:
time: 152 us
  waiting for transfers between devices  100 us (66%)
  starting transfers between devices  25 us (16%)
  between operations  14.3 us (9%)
  matrix products  5.51 us (4%)
  other arithmetic  4.75 us (3%)
  local copies, waits for them, and re-layouts  2 us (1%)
    psum x1, waiting for transfers between devices, on_device(): predicted = lax.psum(padded, 'rad')[:nstars]  99.1 us
    ppermute x4, starting transfers between devices, ring(): lax.ppermute(value, axis, [(i, (i + step) % count) for i in range(count)])  24.9 us
  transfers between devices with their start and end apart: 5, of which 2 were waited for; matrix products, arithmetic and copies ran while one was open for 2% of the time, Pallas kernels for 0%

profile of v9, /device:TPU:1, one launch (start us, length us, event | category | flops | bytes accessed | tf_op | source)
XLA Modules:
  0.0 151.7 jit_solution(5022426899087318824)
XLA Ops:
  7.2 0.0 copy-start
  7.2 0.0 copy-start.7
  7.2 0.0 all-reduce.3.cloned.1.call-start
  7.2 0.8 fusion.35
  8.0 4.0 %collective-permute-start = (f32[88,128]{1,0:T(8,128)S(1)}, f32[88,128]{1,0:T(8,128)S(1)}, u32[]{:S(2)}, u32[]{:S(2)}) collective-permute-start(f32[88,128]{1,0:T(8,128)S(1)} %get-tuple-element.19), channel_id=1, source_target_pairs={{0,8},{8,16},{16,24},{24,32},{32,40},{40,48},{48,56},{56,64},{64,7... | collective-permute-start | bytes 135176 | tf_op jit(solution)/shard_map/ppermute | solution.py:34
  12.1 9.6 %collective-permute-start.1 = (f32[88,128]{1,0:T(8,128)S(1)}, f32[88,128]{1,0:T(8,128)S(1)}, u32[]{:S(2)}, u32[]{:S(2)}) collective-permute-start(f32[88,128]{1,0:T(8,128)S(1)} %get-tuple-element.18), channel_id=1, source_target_pairs={{0,504},{8,0},{16,8},{24,16},{32,24},{40,32},{48,40},{56,48},{64,5... | collective-permute-start | bytes 135176 | tf_op jit(solution)/shard_map/ppermute | solution.py:34
  21.7 2.3 %select_reduce_fusion = f32[256,2048]{1,0:T(8,128)S(1)} fusion(f32[4,2048]{1,0:T(4,128)} %param.16, s32[4,2048]{1,0:T(4,128)} %param.15), kind=kLoop, calls=%fused_computation | loop fusion | flops 5767168 | bytes 2162688 | tf_op jit(solution)/shard_map/reduce_sum | solution.py:66
  24.0 0.0 collective-permute-done
  24.0 0.0 copy-done
  24.0 0.0 copy-start.3
  24.1 0.0 collective-permute-done.1
  24.1 0.0 copy-done.7
  24.2 1.1 fusion.1
  25.2 0.0 copy-done.3
  25.2 0.0 copy-start.1
  25.2 0.0 copy-start.2
  25.3 0.0 copy-start.6
  25.3 0.0 copy-start.4
  25.3 0.0 copy-start.5
  25.3 0.2 fusion.13
  25.5 0.5 copy-done.1
  25.9 0.0 copy-done.2
  26.0 0.0 copy-done.6
  26.0 1.4 fusion.10
  27.4 0.6 pad.4
  28.0 0.0 all-reduce.3.cloned.1.call-update
  28.0 99.1 %all-reduce.3.cloned.1.call-done = f32[16384]{0:T(1024)} async-done(((f32[16384]{0:T(1024)}), f32[16384]{0:T(1024)}) %all-reduce.3.cloned.1.call-update) | async-done | bytes 65552 | tf_op jit(solution)/shard_map/psum | solution.py:76
  127.1 0.0 copy-done.4
  127.1 0.0 copy-done.5
  127.1 1.3 multiply_divide_fusion
  128.4 2.1 %convolution_multiply_fusion.1 = f32[88,256]{1,0:T(8,128)S(1)} fusion(f32[256,2048]{1,0:T(8,128)S(1)} %select_reduce_fusion, f32[2048]{0:T(1024)S(1)} %get-tuple-element.6, f32[2048]{0:T(1024)S(1)} %copy-done.1, s32[2048]{0:T(1024)S(1)} %copy-done.2, s32[88]{0:T(128)S(1)} %get-tuple-element.21, s32[88]{0:T(128)S(1)} %get-tuple-element.20, ...), kind=kOutput, calls=%fused_computation.19 | convolution fusion | flops 554594304 | bytes 2303008 | tf_op jit(solution)/shard_map/dot_general | solution.py:79
  130.4 0.2 reduce-precision_convert_fusion.1
  130.7 1.0 fusion.4
  131.8 3.1 %collective-permute-start.2 = (f32[88,128]{1,0:T(8,128)S(1)}, f32[88,128]{1,0:T(8,128)S(1)}, u32[]{:S(2)}, u32[]{:S(2)}) collective-permute-start(f32[88,128]{1,0:T(8,128)S(1)} %get-tuple-element.4), channel_id=1, source_target_pairs={{0,8},{8,16},{16,24},{24,32},{32,40},{40,48},{48,56},{56,64},{64,7... | collective-permute-start | bytes 135176 | tf_op jit(solution)/shard_map/ppermute | solution.py:34
  134.9 8.2 %collective-permute-start.3 = (f32[88,128]{1,0:T(8,128)S(1)}, f32[88,128]{1,0:T(8,128)S(1)}, u32[]{:S(2)}, u32[]{:S(2)}) collective-permute-start(f32[88,128]{1,0:T(8,128)S(1)} %get-tuple-element.5), channel_id=1, source_target_pairs={{0,504},{8,0},{16,8},{24,16},{32,24},{40,32},{48,40},{56,48},{64,5... | collective-permute-start | bytes 135176 | tf_op jit(solution)/shard_map/ppermute | solution.py:34
  143.1 0.0 collective-permute-done.2
  143.1 1.1 collective-permute-done.3
  144.2 0.6 pad_maximum_fusion
  (8 shorter events, 0.1 us)
Async XLA Ops:
  7.2 16.9 %copy-start = (f32[88,256]{1,0:T(8,128)S(1)}, f32[88,256]{1,0:T(8,128)}, u32[]{:S(2)}) copy-start(f32[88,256]{1,0:T(8,128)} %param.10) | copy-start | bytes 270340
  7.2 17.0 %copy-start.7 = (s32[9,256]{1,0:T(8,128)S(1)}, s32[9,256]{1,0:T(8,128)}, u32[]{:S(2)}) copy-start(s32[9,256]{1,0:T(8,128)} %param.13) | copy-start | bytes 27652
  7.2 119.9 %all-reduce.3.cloned.1.call-start = ((), (), s32[]{:S(2)}) async-start(), calls=%async_computation | async-start | bytes 131072 | tf_op jit(solution)/shard_map/psum | solution.py:76
  8.0 16.0 %collective-permute-start = (f32[88,128]{1,0:T(8,128)S(1)}, f32[88,128]{1,0:T(8,128)S(1)}, u32[]{:S(2)}, u32[]{:S(2)}) collective-permute-start(f32[88,128]{1,0:T(8,128)S(1)} %get-tuple-element.19), channel_id=1, source_target_pairs={{0,8},{8,16},{16,24},{24,32},{32,40},{40,48},{48,56},{56,64},{64,7... | collective-permute-start | bytes 135176 | tf_op jit(solution)/shard_map/ppermute | solution.py:34
  12.1 12.0 %collective-permute-start.1 = (f32[88,128]{1,0:T(8,128)S(1)}, f32[88,128]{1,0:T(8,128)S(1)}, u32[]{:S(2)}, u32[]{:S(2)}) collective-permute-start(f32[88,128]{1,0:T(8,128)S(1)} %get-tuple-element.18), channel_id=1, source_target_pairs={{0,504},{8,0},{16,8},{24,16},{32,24},{40,32},{48,40},{56,48},{64,5... | collective-permute-start | bytes 135176 | tf_op jit(solution)/shard_map/ppermute | solution.py:34
  24.0 1.2 copy-start.3
  25.2 0.7 copy-start.1
  25.2 0.7 copy-start.2
  25.3 0.7 copy-start.6
  25.3 101.8 %copy-start.4 = (f32[2048]{0:T(1024)S(1)}, f32[2048]{0:T(1024)}, u32[]{:S(2)}) copy-start(f32[2048]{0:T(1024)} %param.19) | copy-start | bytes 24580
  25.3 101.8 %copy-start.5 = (f32[2048]{0:T(1024)S(1)}, f32[2048]{0:T(1024)}, u32[]{:S(2)}) copy-start(f32[2048]{0:T(1024)} %param.18) | copy-start | bytes 24580
  131.8 11.3 %collective-permute-start.2 = (f32[88,128]{1,0:T(8,128)S(1)}, f32[88,128]{1,0:T(8,128)S(1)}, u32[]{:S(2)}, u32[]{:S(2)}) collective-permute-start(f32[88,128]{1,0:T(8,128)S(1)} %get-tuple-element.4), channel_id=1, source_target_pairs={{0,8},{8,16},{16,24},{24,32},{32,40},{40,48},{48,56},{56,64},{64,7... | collective-permute-start | bytes 135176 | tf_op jit(solution)/shard_map/ppermute | solution.py:34
  134.9 9.3 %collective-permute-start.3 = (f32[88,128]{1,0:T(8,128)S(1)}, f32[88,128]{1,0:T(8,128)S(1)}, u32[]{:S(2)}, u32[]{:S(2)}) collective-permute-start(f32[88,128]{1,0:T(8,128)S(1)} %get-tuple-element.5), channel_id=1, source_target_pairs={{0,504},{8,0},{16,8},{24,16},{32,24},{40,32},{48,40},{56,48},{64,5... | collective-permute-start | bytes 135176 | tf_op jit(solution)/shard_map/ppermute | solution.py:34
Sparse Core Ops, SparseCore 0:
  28.1 98.8 all-reduce.2

commit v10 on v8

--- a/solution.py
+++ b/solution.py
@@ -1,7 +1,7 @@
 import jax
 import jax.numpy as jnp
 from jax import lax
-from jax.sharding import PartitionSpec as P
+from jax.sharding import Mesh, PartitionSpec as P
 
 COLS = 128
 HIGHEST = lax.Precision.HIGHEST
@@ -65,14 +65,15 @@
     pixel_id = lax.broadcasted_iota(jnp.int32, (pixels, nstars), 0)
     spread = jnp.sum(jnp.where(pixel_id[None] == star_pixels[:, None, :], star_weights[:, None, :], 0.0), axis=0)
 
-    shell_start = lax.axis_index("rad") * shells
+    shell_start = (lax.axis_index("zhi") * lax.axis_size("core") + lax.axis_index("core")) * shells
     bin_id = shell_start + lax.broadcasted_iota(jnp.int32, (shells, nstars), 0)
     lower = star_bin[None, :]
     radial = jnp.where(bin_id <= lower, 1.0, jnp.where(bin_id - 1 == lower, star_frac[None, :], 0.0))
 
     at_stars = jnp.dot(weighted, spread, precision=HIGHEST, preferred_element_type=jnp.float32)
     partial_value = jnp.sum(radial * at_stars, axis=0)
-    predicted = jnp.sum(lax.all_gather(partial_value, "rad"), axis=0)
+    pair = partial_value + lax.ppermute(partial_value, "core", [(0, 1), (1, 0)])
+    predicted = jnp.sum(lax.all_gather(pair, "zhi"), axis=0)
     weight_back = (predicted - observed) / (sigma * sigma)
 
     adjoint_sum = lax.dot_general(
@@ -98,13 +99,16 @@
 
 
 def solution(mesh):
+    ang, rad = mesh.devices.shape
+    split = Mesh(mesh.devices.reshape(ang, rad // 2, 2), ("ang", "zhi", "core"))
+    shell = ("zhi", "core")
     return jax.shard_map(
         on_device,
-        mesh=mesh,
+        mesh=split,
         in_specs=(
-            P("rad", "ang"),
-            P("rad", None),
-            P("rad"),
+            P(shell, "ang"),
+            P(shell, None),
+            P(shell),
             P(None, "ang"),
             P("ang"),
             P(None, "ang"),
@@ -113,6 +117,6 @@
             P("ang"),
             P("ang"),
         ),
-        out_specs=(P("ang"), P("rad", "ang")),
+        out_specs=(P("ang"), P(shell, "ang")),
         check_vma=False,
     )

time: 63.9 us -> 65 us (1.017)
  the two profiles are of different devices: /device:TPU:1 before, /device:TPU:126 now
where the time goes in v10:
time: 65 us; the launch traced here: 64.6 us
  blocking collectives  20.4 us (31%)
  waiting for transfers between devices  17.2 us (26%)
  starting transfers between devices  15.7 us (24%)
  matrix products  5.51 us (8%)
  other arithmetic  3.49 us (5%)
  local copies, waits for them, and re-layouts  1.42 us (2%)
  between operations  0.91 us (1%)
    all_gather x1, blocking collectives, on_device(): predicted = jnp.sum(lax.all_gather(pair, 'zhi'), axis=0)  20.4 us
    ppermute x4, waiting for transfers between devices, ring(): lax.ppermute(value, axis, [(i, (i + step) % count) for i in range(count)])  16 us
    ppermute x4, starting transfers between devices, ring(): lax.ppermute(value, axis, [(i, (i + step) % count) for i in range(count)])  13.8 us
    reduce_sum x1, other arithmetic, on_device(): jnp.sum(jnp.where(pixel_id[None] == star_pixels[:, None, :], star_weights...  2.29 us
    dot_general x1, matrix products, on_device(): lax.dot_general(radial * weight_back[None, :], spread, (((1,), (1,)), (()...  2.06 us
    ppermute x1, starting transfers between devices, on_device(): pair = partial_value + lax.ppermute(partial_value, 'core', [(0, 1), (1, 0)])  1.92 us
    dot_general x1, matrix products, on_device(): jnp.dot(weighted, spread, precision=HIGHEST, preferred_element_type=jnp.f...  1.4 us
  transfers between devices with their start and end apart: 5, of which 4 were waited for; matrix products, arithmetic and copies ran while one was open for 4% of the time, Pallas kernels for 0%

profile of v10, /device:TPU:126, one launch (start us, length us, event | category | flops | bytes accessed | tf_op | source)
XLA Modules:
  0.0 64.6 jit_solution(4595891303811740490)
XLA Ops:
  0.6 0.0 copy-start
  0.6 0.0 copy-start.8
  0.6 0.9 %fusion.35 = (f32[88,128]{1,0:T(8,128)S(1)}, f32[88,128]{1,0:T(8,128)S(1)}) fusion(f32[88,256]{1,0:T(8,128)} %param.10), kind=kLoop, calls=%fused_computation.64 | loop fusion | bytes 180224 | tf_op jit(solution)/shard_map/slice | solution.py:54
  1.5 6.0 %collective-permute-start = (f32[88,128]{1,0:T(8,128)S(1)}, f32[88,128]{1,0:T(8,128)S(1)}, u32[]{:S(2)}, u32[]{:S(2)}) collective-permute-start(f32[88,128]{1,0:T(8,128)S(1)} %get-tuple-element.17), channel_id=1, source_target_pairs={{0,8},{8,16},{16,24},{24,32},{32,40},{40,48},{48,56},{56,64},{64,7... | collective-permute-start | bytes 135176 | tf_op jit(solution)/shard_map/ppermute | solution.py:34
  7.6 1.9 %collective-permute-start.1 = (f32[88,128]{1,0:T(8,128)S(1)}, f32[88,128]{1,0:T(8,128)S(1)}, u32[]{:S(2)}, u32[]{:S(2)}) collective-permute-start(f32[88,128]{1,0:T(8,128)S(1)} %get-tuple-element.16), channel_id=1, source_target_pairs={{0,504},{8,0},{16,8},{24,16},{32,24},{40,32},{48,40},{56,48},{64,5... | collective-permute-start | bytes 135176 | tf_op jit(solution)/shard_map/ppermute | solution.py:34
  9.5 2.3 %select_reduce_fusion = f32[256,2048]{1,0:T(8,128)S(1)} fusion(f32[4,2048]{1,0:T(4,128)} %param.16, s32[4,2048]{1,0:T(4,128)} %param.15), kind=kLoop, calls=%fused_computation | loop fusion | flops 5767168 | bytes 2162688 | tf_op jit(solution)/shard_map/reduce_sum | solution.py:66
  11.8 0.0 collective-permute-done
  11.8 0.0 copy-done
  11.8 0.0 copy-start.3
  11.9 7.7 %collective-permute-done.1 = f32[88,128]{1,0:T(8,128)S(1)} collective-permute-done((f32[88,128]{1,0:T(8,128)S(1)}, f32[88,128]{1,0:T(8,128)S(1)}, u32[]{:S(2)}, u32[]{:S(2)}) %collective-permute-start.1) | collective-permute-done | bytes 45088 | tf_op jit(solution)/shard_map/ppermute | solution.py:34
  19.6 0.0 copy-done.8
  19.6 1.1 %fusion.1 = f32[264,9,256]{2,0,1:T(8,128)S(1)} fusion(s32[9,256]{1,0:T(8,128)S(1)} %copy-done.8, bf16[88,512]{1,0:T(8,128)(2,1)S(1)} %get-tuple-element.11, bf16[88,512]{1,0:T(8,128)(2,1)S(1)} %get-tuple-element.12, bf16[88,512]{1,0:T(8,128)(2,1)S(1)} %get-tuple-element.10), kind=kOutput, calls=%fused_computation.4 | convolution fusion | flops 624844800 | bytes 2712576 | tf_op jit(solution)/shard_map/dot_general | solution.py:20
  20.6 0.0 copy-done.3
  20.7 0.0 copy-start.1
  20.7 0.0 copy-start.2
  20.7 0.0 copy-start.7
  20.7 0.0 copy-start.5
  20.7 0.0 copy-start.6
  20.7 0.2 fusion.13
  20.9 0.5 copy-done.1
  21.4 0.0 copy-done.2
  21.4 0.0 copy-done.7
  21.4 1.4 %fusion.10 = f32[2048]{0:T(1024)S(1)} fusion(f32[256,2048]{1,0:T(8,128)S(1)} %select_reduce_fusion, f32[2048]{0:T(1024)S(1)} %copy-done.1, s32[2048]{0:T(1024)S(1)} %copy-done.2, s32[88]{0:T(128)S(1)} %get-tuple-element.19, s32[88]{0:T(128)S(1)} %get-tuple-element.18, f32[88,256]{1,0:T(8,128)S(1)} %fusion.13, f32[88]{0:T(128)S(1)} %copy-done.7), kind=kOutput, calls=%fused_computation.14 | convolution fusion | flops 554749952 | bytes 2212896 | tf_op jit(solution)/shard_map/dot_general | solution.py:73
  22.8 1.9 %collective-permute-start.2 = (f32[2048]{0:T(1024)S(1)}, f32[2048]{0:T(1024)S(1)}, u32[]{:S(2)}, u32[]{:S(2)}) collective-permute-start(f32[2048]{0:T(1024)S(1)} %fusion.10), channel_id=1, source_target_pairs={{0,1},{1,0},{2,3},{3,2},{4,5},{5,4},{6,7},{7,6},{8,9},{9,8},{10,11... | collective-permute-start | bytes 24584 | tf_op jit(solution)/shard_map/ppermute | solution.py:75
  24.7 1.1 %collective-permute-done.2 = f32[2048]{0:T(1024)S(1)} collective-permute-done((f32[2048]{0:T(1024)S(1)}, f32[2048]{0:T(1024)S(1)}, u32[]{:S(2)}, u32[]{:S(2)}) %collective-permute-start.2) | collective-permute-done | bytes 8224 | tf_op jit(solution)/shard_map/ppermute | solution.py:75
  25.8 20.4 %all-gather = f32[8192]{0:T(1024)S(1)} all-gather(f32[2048]{0:T(1024)S(1)} %add.38), channel_id=2, replica_groups=mesh['ang'=64,'zhi'=4,'core'=2] {'zhi'}, dimensions={0}, use_global_device_ids=true | all-gather | bytes 40960 | tf_op jit(solution)/shard_map/all_gather | solution.py:76
  46.3 0.0 copy-done.5
  46.3 0.0 copy-done.6
  46.3 0.0 copy-start.4
  46.4 2.1 %convolution_multiply_fusion.1 = f32[88,256]{1,0:T(8,128)S(1)} fusion(f32[256,2048]{1,0:T(8,128)S(1)} %select_reduce_fusion, f32[2048]{0:T(1024)S(1)} %multiply_divide_fusion, f32[2048]{0:T(1024)S(1)} %copy-done.1, s32[2048]{0:T(1024)S(1)} %copy-done.2, s32[88]{0:T(128)S(1)} %get-tuple-element.19, s32[88]{0:T(128)S(1)} %get-tuple-element.18, ...), kind=kOutput, calls=%fused_computation.19 | convolution fusion | flops 554594304 | bytes 2303008 | tf_op jit(solution)/shard_map/dot_general | solution.py:79
  48.4 0.2 reduce-precision_convert_fusion.1
  48.7 1.0 %fusion.4 = f32[264,512]{1,0:T(8,128)S(1)} fusion(s32[9,256]{1,0:T(8,128)S(1)} %copy-done.8, bf16[88,9,256]{2,0,1:T(8,128)(2,1)S(1)} %get-tuple-element.15, bf16[88,9,256]{2,0,1:T(8,128)(2,1)S(1)} %get-tuple-element.14, bf16[88,9,256]{2,0,1:T(8,128)(2,1)S(1)} %get-tuple-element.13), kind=kOutput, calls=%fused_computation.8 | convolution fusion | flops 627683328 | bytes 1766400 | tf_op jit(solution)/shard_map/dot_general | solution.py:26
  49.7 0.0 copy-done.4
  49.8 2.3 %collective-permute-start.3 = (f32[88,128]{1,0:T(8,128)S(1)}, f32[88,128]{1,0:T(8,128)S(1)}, u32[]{:S(2)}, u32[]{:S(2)}) collective-permute-start(f32[88,128]{1,0:T(8,128)S(1)} %get-tuple-element.4), channel_id=1, source_target_pairs={{0,8},{8,16},{16,24},{24,32},{32,40},{40,48},{48,56},{56,64},{64,7... | collective-permute-start | bytes 135176 | tf_op jit(solution)/shard_map/ppermute | solution.py:34
  52.0 3.6 %collective-permute-start.4 = (f32[88,128]{1,0:T(8,128)S(1)}, f32[88,128]{1,0:T(8,128)S(1)}, u32[]{:S(2)}, u32[]{:S(2)}) collective-permute-start(f32[88,128]{1,0:T(8,128)S(1)} %get-tuple-element.5), channel_id=1, source_target_pairs={{0,504},{8,0},{16,8},{24,16},{32,24},{40,32},{48,40},{56,48},{64,5... | collective-permute-start | bytes 135176 | tf_op jit(solution)/shard_map/ppermute | solution.py:34
  55.6 0.1 collective-permute-done.3
  55.7 8.3 %collective-permute-done.4 = f32[88,128]{1,0:T(8,128)S(1)} collective-permute-done((f32[88,128]{1,0:T(8,128)S(1)}, f32[88,128]{1,0:T(8,128)S(1)}, u32[]{:S(2)}, u32[]{:S(2)}) %collective-permute-start.4) | collective-permute-done | bytes 45088 | tf_op jit(solution)/shard_map/ppermute | solution.py:34
  64.0 0.6 pad_maximum_fusion
  (12 shorter events, 0.2 us)
Async XLA Ops:
  0.6 11.2 %copy-start = (f32[88,256]{1,0:T(8,128)S(1)}, f32[88,256]{1,0:T(8,128)}, u32[]{:S(2)}) copy-start(f32[88,256]{1,0:T(8,128)} %param.10) | copy-start | bytes 270340
  0.6 18.9 %copy-start.8 = (s32[9,256]{1,0:T(8,128)S(1)}, s32[9,256]{1,0:T(8,128)}, u32[]{:S(2)}) copy-start(s32[9,256]{1,0:T(8,128)} %param.13) | copy-start | bytes 27652
  1.5 10.3 %collective-permute-start = (f32[88,128]{1,0:T(8,128)S(1)}, f32[88,128]{1,0:T(8,128)S(1)}, u32[]{:S(2)}, u32[]{:S(2)}) collective-permute-start(f32[88,128]{1,0:T(8,128)S(1)} %get-tuple-element.17), channel_id=1, source_target_pairs={{0,8},{8,16},{16,24},{24,32},{32,40},{40,48},{48,56},{56,64},{64,7... | collective-permute-start | bytes 135176 | tf_op jit(solution)/shard_map/ppermute | solution.py:34
  7.6 12.0 %collective-permute-start.1 = (f32[88,128]{1,0:T(8,128)S(1)}, f32[88,128]{1,0:T(8,128)S(1)}, u32[]{:S(2)}, u32[]{:S(2)}) collective-permute-start(f32[88,128]{1,0:T(8,128)S(1)} %get-tuple-element.16), channel_id=1, source_target_pairs={{0,504},{8,0},{16,8},{24,16},{32,24},{40,32},{48,40},{56,48},{64,5... | collective-permute-start | bytes 135176 | tf_op jit(solution)/shard_map/ppermute | solution.py:34
  11.8 8.8 %copy-start.3 = (f32[88,9]{0,1:T(8,128)S(1)}, f32[88,9]{0,1:T(8,128)}, u32[]{:S(2)}) copy-start(f32[88,9]{0,1:T(8,128)} %param.11) | copy-start | bytes 9508
  20.7 0.7 %copy-start.1 = (f32[2048]{0:T(1024)S(1)}, f32[2048]{0:T(1024)}, u32[]{:S(2)}) copy-start(f32[2048]{0:T(1024)} %param.17) | copy-start | bytes 24580
  20.7 0.7 %copy-start.2 = (s32[2048]{0:T(1024)S(1)}, s32[2048]{0:T(1024)}, u32[]{:S(2)}) copy-start(s32[2048]{0:T(1024)} %param.14) | copy-start | bytes 24580
  20.7 0.7 %copy-start.7 = (f32[88]{0:T(128)S(1)}, f32[88]{0:T(128)}, u32[]{:S(2)}) copy-start(f32[88]{0:T(128)} %param.12) | copy-start | bytes 1060
  20.7 25.6 %copy-start.5 = (f32[2048]{0:T(1024)S(1)}, f32[2048]{0:T(1024)}, u32[]{:S(2)}) copy-start(f32[2048]{0:T(1024)} %param.19) | copy-start | bytes 24580
  20.7 25.6 %copy-start.6 = (f32[2048]{0:T(1024)S(1)}, f32[2048]{0:T(1024)}, u32[]{:S(2)}) copy-start(f32[2048]{0:T(1024)} %param.18) | copy-start | bytes 24580
  22.8 3.1 %collective-permute-start.2 = (f32[2048]{0:T(1024)S(1)}, f32[2048]{0:T(1024)S(1)}, u32[]{:S(2)}, u32[]{:S(2)}) collective-permute-start(f32[2048]{0:T(1024)S(1)} %fusion.10), channel_id=1, source_target_pairs={{0,1},{1,0},{2,3},{3,2},{4,5},{5,4},{6,7},{7,6},{8,9},{9,8},{10,11... | collective-permute-start | bytes 24584 | tf_op jit(solution)/shard_map/ppermute | solution.py:75
  46.3 3.3 %copy-start.4 = (f32[2048]{0:T(1024)}, f32[2048]{0:T(1024)S(1)}, u32[]{:S(2)}) copy-start(f32[2048]{0:T(1024)S(1)} %reduce_sum.39) | copy-start | bytes 24580
  49.8 5.9 %collective-permute-start.3 = (f32[88,128]{1,0:T(8,128)S(1)}, f32[88,128]{1,0:T(8,128)S(1)}, u32[]{:S(2)}, u32[]{:S(2)}) collective-permute-start(f32[88,128]{1,0:T(8,128)S(1)} %get-tuple-element.4), channel_id=1, source_target_pairs={{0,8},{8,16},{16,24},{24,32},{32,40},{40,48},{48,56},{56,64},{64,7... | collective-permute-start | bytes 135176 | tf_op jit(solution)/shard_map/ppermute | solution.py:34
  52.0 12.0 %collective-permute-start.4 = (f32[88,128]{1,0:T(8,128)S(1)}, f32[88,128]{1,0:T(8,128)S(1)}, u32[]{:S(2)}, u32[]{:S(2)}) collective-permute-start(f32[88,128]{1,0:T(8,128)S(1)} %get-tuple-element.5), channel_id=1, source_target_pairs={{0,504},{8,0},{16,8},{24,16},{32,24},{40,32},{48,40},{56,48},{64,5... | collective-permute-start | bytes 135176 | tf_op jit(solution)/shard_map/ppermute | solution.py:34

commit v11 on v8

--- a/solution.py
+++ b/solution.py
@@ -50,9 +50,9 @@
     taps = neighbours.shape[0]
     frame = pixels + 2 * COLS
 
-    above = ring(latent[:, pixels - COLS :], "ang", 1)
-    below = ring(latent[:, :COLS], "ang", -1)
-    wide = jnp.concatenate([above, latent, below], axis=1)
+    before = ring(latent, "ang", 1)
+    after = ring(latent, "ang", -1)
+    wide = jnp.concatenate([before[:, pixels - COLS :], latent, after[:, :COLS]], axis=1)
 
     position = lax.broadcasted_iota(jnp.int32, (frame, taps, pixels), 0)
     pick = (position == neighbours[None, :, :]).astype(jnp.bfloat16)

time: 63.9 us -> 63.7 us (level)
  local copies, waits for them, and re-layouts: 1.42 us -> 0.56 us
  starting transfers between devices: 24.9 us -> 25.6 us
    slice x1 -> x2, local copies, waits for them, and re-layouts: 0.86 us -> 0.01 us  [the longest x1 0.01 us: on_device(): before[:, pixels - COLS:]]
    ppermute x4, starting transfers between devices: 24.9 us -> 25.6 us  [ring(): lax.ppermute(value, axis, [(i, (i + step) % count) for i in range(count)])]
where the time goes in v11:
time: 63.7 us; the launch traced here: 63.4 us
  blocking collectives  26.2 us (41%)
  starting transfers between devices  25.6 us (40%)
  matrix products  5.51 us (9%)
  other arithmetic  3.48 us (5%)
  waiting for transfers between devices  1.11 us (2%)
  between operations  0.92 us (1%)
    all_gather x1, blocking collectives, on_device(): predicted = jnp.sum(lax.all_gather(partial_value, 'rad'), axis=0)  26.2 us
    ppermute x4, starting transfers between devices, ring(): lax.ppermute(value, axis, [(i, (i + step) % count) for i in range(count)])  25.6 us
    reduce_sum x1, other arithmetic, on_device(): jnp.sum(jnp.where(pixel_id[None] == star_pixels[:, None, :], star_weights...  2.28 us
    dot_general x1, matrix products, on_device(): lax.dot_general(radial * weight_back[None, :], spread, (((1,), (1,)), (()...  2.06 us
    dot_general x1, matrix products, on_device(): jnp.dot(weighted, spread, precision=HIGHEST, preferred_element_type=jnp.f...  1.4 us
  transfers between devices with their start and end apart: 4, of which 1 were waited for; matrix products, arithmetic and copies ran while one was open for 4% of the time, Pallas kernels for 0%

profile of v11, /device:TPU:1, one launch (start us, length us, event | category | flops | bytes accessed | tf_op | source)
XLA Modules:
  0.0 63.4 jit_solution(6558793242450546212)
XLA Ops:
  0.6 0.0 copy-start
  0.6 0.0 copy-start.8
  0.7 4.2 %collective-permute-start = (f32[88,256]{1,0:T(8,128)}, f32[88,256]{1,0:T(8,128)S(1)}, u32[]{:S(2)}, u32[]{:S(2)}) collective-permute-start(f32[88,256]{1,0:T(8,128)} %param.10), channel_id=1, source_target_pairs={{0,8},{8,16},{16,24},{24,32},{32,40},{40,48},{48,56},{56,64},{64,7... | collective-permute-start | bytes 270344 | tf_op jit(solution)/shard_map/ppermute | solution.py:34
  4.8 9.6 %collective-permute-start.1 = (f32[88,256]{1,0:T(8,128)}, f32[88,256]{1,0:T(8,128)S(1)}, u32[]{:S(2)}, u32[]{:S(2)}) collective-permute-start(f32[88,256]{1,0:T(8,128)} %param.10), channel_id=1, source_target_pairs={{0,504},{8,0},{16,8},{24,16},{32,24},{40,32},{48,40},{56,48},{64,5... | collective-permute-start | bytes 270344 | tf_op jit(solution)/shard_map/ppermute | solution.py:34
  14.4 2.3 %select_reduce_fusion = f32[256,2048]{1,0:T(8,128)S(1)} fusion(f32[4,2048]{1,0:T(4,128)} %param.16, s32[4,2048]{1,0:T(4,128)} %param.15), kind=kLoop, calls=%fused_computation | loop fusion | flops 5767168 | bytes 2162688 | tf_op jit(solution)/shard_map/reduce_sum | solution.py:66
  16.7 0.0 copy-start.3
  16.8 0.0 collective-permute-done
  16.8 0.0 collective-permute-done.1
  16.8 0.0 copy-done
  16.9 0.0 copy-done.8
  16.9 1.1 %fusion.1 = f32[264,9,256]{2,0,1:T(8,128)S(1)} fusion(s32[9,256]{1,0:T(8,128)S(1)} %copy-done.8, bf16[88,512]{1,0:T(8,128)(2,1)S(1)} %get-tuple-element.12, bf16[88,512]{1,0:T(8,128)(2,1)S(1)} %get-tuple-element.11, bf16[88,512]{1,0:T(8,128)(2,1)S(1)} %get-tuple-element.10), kind=kOutput, calls=%fused_computation.4 | convolution fusion | flops 624844800 | bytes 2712576 | tf_op jit(solution)/shard_map/dot_general | solution.py:20
  18.0 0.0 copy-done.3
  18.0 0.0 copy-start.1
  18.0 0.0 copy-start.2
  18.0 0.0 copy-start.7
  18.0 0.0 copy-start.5
  18.0 0.0 copy-start.6
  18.0 0.2 fusion.13
  18.2 0.5 copy-done.1
  18.7 0.0 copy-done.2
  18.7 0.0 copy-done.7
  18.7 1.4 %fusion.10 = f32[2048]{0:T(1024)S(1)} fusion(f32[256,2048]{1,0:T(8,128)S(1)} %select_reduce_fusion, f32[2048]{0:T(1024)S(1)} %copy-done.1, s32[2048]{0:T(1024)S(1)} %copy-done.2, s32[88]{0:T(128)S(1)} %get-tuple-element.17, s32[88]{0:T(128)S(1)} %get-tuple-element.16, f32[88,256]{1,0:T(8,128)S(1)} %fusion.13, f32[88]{0:T(128)S(1)} %copy-done.7), kind=kOutput, calls=%fused_computation.14 | convolution fusion | flops 554749952 | bytes 2212896 | tf_op jit(solution)/shard_map/dot_general | solution.py:73
  20.1 26.2 %all-gather = f32[16384]{0:T(1024)S(1)} all-gather(f32[2048]{0:T(1024)S(1)} %fusion.10), channel_id=2, replica_groups=mesh['ang'=64,'rad'=8] {'rad'}, dimensions={0}, use_global_device_ids=true | all-gather | bytes 73728 | tf_op jit(solution)/shard_map/all_gather | solution.py:75
  46.3 0.0 copy-done.5
  46.3 0.0 copy-done.6
  46.3 0.0 copy-start.4
  46.4 2.1 %convolution_multiply_fusion.1 = f32[88,256]{1,0:T(8,128)S(1)} fusion(f32[256,2048]{1,0:T(8,128)S(1)} %select_reduce_fusion, f32[2048]{0:T(1024)S(1)} %multiply_divide_fusion, f32[2048]{0:T(1024)S(1)} %copy-done.1, s32[2048]{0:T(1024)S(1)} %copy-done.2, s32[88]{0:T(128)S(1)} %get-tuple-element.17, s32[88]{0:T(128)S(1)} %get-tuple-element.16, ...), kind=kOutput, calls=%fused_computation.19 | convolution fusion | flops 554594304 | bytes 2303008 | tf_op jit(solution)/shard_map/dot_general | solution.py:78
  48.4 0.2 reduce-precision_convert_fusion.1
  48.7 1.0 %fusion.4 = f32[264,512]{1,0:T(8,128)S(1)} fusion(s32[9,256]{1,0:T(8,128)S(1)} %copy-done.8, bf16[88,9,256]{2,0,1:T(8,128)(2,1)S(1)} %get-tuple-element.15, bf16[88,9,256]{2,0,1:T(8,128)(2,1)S(1)} %get-tuple-element.14, bf16[88,9,256]{2,0,1:T(8,128)(2,1)S(1)} %get-tuple-element.13), kind=kOutput, calls=%fused_computation.8 | convolution fusion | flops 627683328 | bytes 1766400 | tf_op jit(solution)/shard_map/dot_general | solution.py:26
  49.7 0.0 copy-done.4
  49.7 1.9 %collective-permute-start.2 = (f32[88,128]{1,0:T(8,128)S(1)}, f32[88,128]{1,0:T(8,128)S(1)}, u32[]{:S(2)}, u32[]{:S(2)}) collective-permute-start(f32[88,128]{1,0:T(8,128)S(1)} %get-tuple-element.4), channel_id=1, source_target_pairs={{0,8},{8,16},{16,24},{24,32},{32,40},{40,48},{48,56},{56,64},{64,7... | collective-permute-start | bytes 135176 | tf_op jit(solution)/shard_map/ppermute | solution.py:34
  51.7 9.9 %collective-permute-start.3 = (f32[88,128]{1,0:T(8,128)S(1)}, f32[88,128]{1,0:T(8,128)S(1)}, u32[]{:S(2)}, u32[]{:S(2)}) collective-permute-start(f32[88,128]{1,0:T(8,128)S(1)} %get-tuple-element.5), channel_id=1, source_target_pairs={{0,504},{8,0},{16,8},{24,16},{32,24},{40,32},{48,40},{56,48},{64,5... | collective-permute-start | bytes 135176 | tf_op jit(solution)/shard_map/ppermute | solution.py:34
  61.6 0.0 collective-permute-done.2
  61.6 1.1 %collective-permute-done.3 = f32[88,128]{1,0:T(8,128)S(1)} collective-permute-done((f32[88,128]{1,0:T(8,128)S(1)}, f32[88,128]{1,0:T(8,128)S(1)}, u32[]{:S(2)}, u32[]{:S(2)}) %collective-permute-start.3) | collective-permute-done | bytes 45088 | tf_op jit(solution)/shard_map/ppermute | solution.py:34
  62.7 0.6 %pad_maximum_fusion.1 = f32[88,256]{1,0:T(8,128)} fusion(f32[88,128]{1,0:T(8,128)S(1)} %get-tuple-element.7, f32[88,128]{1,0:T(8,128)S(1)} %get-tuple-element.6), kind=kLoop, calls=%fused_computation.49 | loop fusion | flops 22528 | bytes 180224 | tf_op jit(solution)/shard_map/concatenate | solution.py:93
  (10 shorter events, 0.2 us)
Async XLA Ops:
  0.6 16.2 %copy-start = (f32[88,256]{1,0:T(8,128)S(1)}, f32[88,256]{1,0:T(8,128)}, u32[]{:S(2)}) copy-start(f32[88,256]{1,0:T(8,128)} %param.10) | copy-start | bytes 270340
  0.6 16.2 %copy-start.8 = (s32[9,256]{1,0:T(8,128)S(1)}, s32[9,256]{1,0:T(8,128)}, u32[]{:S(2)}) copy-start(s32[9,256]{1,0:T(8,128)} %param.13) | copy-start | bytes 27652
  0.7 16.1 %collective-permute-start = (f32[88,256]{1,0:T(8,128)}, f32[88,256]{1,0:T(8,128)S(1)}, u32[]{:S(2)}, u32[]{:S(2)}) collective-permute-start(f32[88,256]{1,0:T(8,128)} %param.10), channel_id=1, source_target_pairs={{0,8},{8,16},{16,24},{24,32},{32,40},{40,48},{48,56},{56,64},{64,7... | collective-permute-start | bytes 270344 | tf_op jit(solution)/shard_map/ppermute | solution.py:34
  4.8 12.0 %collective-permute-start.1 = (f32[88,256]{1,0:T(8,128)}, f32[88,256]{1,0:T(8,128)S(1)}, u32[]{:S(2)}, u32[]{:S(2)}) collective-permute-start(f32[88,256]{1,0:T(8,128)} %param.10), channel_id=1, source_target_pairs={{0,504},{8,0},{16,8},{24,16},{32,24},{40,32},{48,40},{56,48},{64,5... | collective-permute-start | bytes 270344 | tf_op jit(solution)/shard_map/ppermute | solution.py:34
  16.7 1.2 %copy-start.3 = (f32[88,9]{0,1:T(8,128)S(1)}, f32[88,9]{0,1:T(8,128)}, u32[]{:S(2)}) copy-start(f32[88,9]{0,1:T(8,128)} %param.11) | copy-start | bytes 9508
  18.0 0.7 %copy-start.1 = (f32[2048]{0:T(1024)S(1)}, f32[2048]{0:T(1024)}, u32[]{:S(2)}) copy-start(f32[2048]{0:T(1024)} %param.17) | copy-start | bytes 24580
  18.0 0.7 %copy-start.2 = (s32[2048]{0:T(1024)S(1)}, s32[2048]{0:T(1024)}, u32[]{:S(2)}) copy-start(s32[2048]{0:T(1024)} %param.14) | copy-start | bytes 24580
  18.0 0.7 %copy-start.7 = (f32[88]{0:T(128)S(1)}, f32[88]{0:T(128)}, u32[]{:S(2)}) copy-start(f32[88]{0:T(128)} %param.12) | copy-start | bytes 1060
  18.0 28.3 %copy-start.5 = (f32[2048]{0:T(1024)S(1)}, f32[2048]{0:T(1024)}, u32[]{:S(2)}) copy-start(f32[2048]{0:T(1024)} %param.19) | copy-start | bytes 24580
  18.0 28.3 %copy-start.6 = (f32[2048]{0:T(1024)S(1)}, f32[2048]{0:T(1024)}, u32[]{:S(2)}) copy-start(f32[2048]{0:T(1024)} %param.18) | copy-start | bytes 24580
  46.3 3.3 %copy-start.4 = (f32[2048]{0:T(1024)}, f32[2048]{0:T(1024)S(1)}, u32[]{:S(2)}) copy-start(f32[2048]{0:T(1024)S(1)} %reduce_sum.39) | copy-start | bytes 24580
  49.7 11.9 %collective-permute-start.2 = (f32[88,128]{1,0:T(8,128)S(1)}, f32[88,128]{1,0:T(8,128)S(1)}, u32[]{:S(2)}, u32[]{:S(2)}) collective-permute-start(f32[88,128]{1,0:T(8,128)S(1)} %get-tuple-element.4), channel_id=1, source_target_pairs={{0,8},{8,16},{16,24},{24,32},{32,40},{40,48},{48,56},{56,64},{64,7... | collective-permute-start | bytes 135176 | tf_op jit(solution)/shard_map/ppermute | solution.py:34
  51.7 11.1 %collective-permute-start.3 = (f32[88,128]{1,0:T(8,128)S(1)}, f32[88,128]{1,0:T(8,128)S(1)}, u32[]{:S(2)}, u32[]{:S(2)}) collective-permute-start(f32[88,128]{1,0:T(8,128)S(1)} %get-tuple-element.5), channel_id=1, source_target_pairs={{0,504},{8,0},{16,8},{24,16},{32,24},{40,32},{48,40},{56,48},{64,5... | collective-permute-start | bytes 135176 | tf_op jit(solution)/shard_map/ppermute | solution.py:34

commit v12 on v10

--- a/solution.py
+++ b/solution.py
@@ -50,9 +50,9 @@
     taps = neighbours.shape[0]
     frame = pixels + 2 * COLS
 
-    above = ring(latent[:, pixels - COLS :], "ang", 1)
-    below = ring(latent[:, :COLS], "ang", -1)
-    wide = jnp.concatenate([above, latent, below], axis=1)
+    before = ring(latent, "ang", 1)
+    after = ring(latent, "ang", -1)
+    wide = jnp.concatenate([before[:, pixels - COLS :], latent, after[:, :COLS]], axis=1)
 
     position = lax.broadcasted_iota(jnp.int32, (frame, taps, pixels), 0)
     pick = (position == neighbours[None, :, :]).astype(jnp.bfloat16)
@@ -72,7 +72,7 @@
 
     at_stars = jnp.dot(weighted, spread, precision=HIGHEST, preferred_element_type=jnp.float32)
     partial_value = jnp.sum(radial * at_stars, axis=0)
-    pair = partial_value + lax.ppermute(partial_value, "core", [(0, 1), (1, 0)])
+    pair = lax.psum(partial_value, "core")
     predicted = jnp.sum(lax.all_gather(pair, "zhi"), axis=0)
     weight_back = (predicted - observed) / (sigma * sigma)
 

time: 65 us -> 64.1 us (0.986)
  blocking collectives: 20.4 us -> 22.9 us
  starting transfers between devices: 15.7 us -> 13.9 us
  local copies, waits for them, and re-layouts: 1.42 us -> 0.54 us
  waiting for transfers between devices: 17.2 us -> 16.4 us
    psum x0 -> x1, blocking collectives: none -> 2.5 us  [on_device(): pair = lax.psum(partial_value, 'core')]
    ppermute x1 -> x0, starting transfers between devices: 1.92 us -> none  [on_device(): pair = partial_value + lax.ppermute(partial_value, 'core', [(0, 1), (1, 0)])]
    ppermute x1 -> x0, waiting for transfers between devices: 1.14 us -> none  [on_device(): pair = partial_value + lax.ppermute(partial_value, 'core', [(0, 1), (1, 0)])]
    slice x1 -> x2, local copies, waits for them, and re-layouts: 0.86 us -> 0.01 us  [the longest x1 0.01 us: on_device(): before[:, pixels - COLS:]]
  transfers between devices with their start and end apart: 5 -> 4, of which waited for: 4 -> 3; matrix products, arithmetic and copies ran while one was open for 4% -> 4% of each run, Pallas kernels for 0% -> 0%
where the time goes in v12:
time: 64.1 us; the launch traced here: 63.7 us
  blocking collectives  22.9 us (36%)
  waiting for transfers between devices  16.4 us (26%)
  starting transfers between devices  13.9 us (22%)
  matrix products  5.51 us (9%)
  other arithmetic  3.49 us (5%)
  between operations  0.88 us (1%)
    all_gather x1, blocking collectives, on_device(): predicted = jnp.sum(lax.all_gather(pair, 'zhi'), axis=0)  20.4 us
    ppermute x4, waiting for transfers between devices, ring(): lax.ppermute(value, axis, [(i, (i + step) % count) for i in range(count)])  16.4 us
    ppermute x4, starting transfers between devices, ring(): lax.ppermute(value, axis, [(i, (i + step) % count) for i in range(count)])  13.9 us
    psum x1, blocking collectives, on_device(): pair = lax.psum(partial_value, 'core')  2.5 us
    reduce_sum x1, other arithmetic, on_device(): jnp.sum(jnp.where(pixel_id[None] == star_pixels[:, None, :], star_weights...  2.28 us
    dot_general x1, matrix products, on_device(): lax.dot_general(radial * weight_back[None, :], spread, (((1,), (1,)), (()...  2.06 us
    dot_general x1, matrix products, on_device(): jnp.dot(weighted, spread, precision=HIGHEST, preferred_element_type=jnp.f...  1.4 us
  transfers between devices with their start and end apart: 4, of which 3 were waited for; matrix products, arithmetic and copies ran while one was open for 4% of the time, Pallas kernels for 0%

profile of v12, /device:TPU:126, one launch (start us, length us, event | category | flops | bytes accessed | tf_op | source)
XLA Modules:
  0.0 63.7 jit_solution(12265674700053972729)
XLA Ops:
  0.6 0.0 copy-start
  0.6 0.0 copy-start.8
  0.7 6.2 %collective-permute-start = (f32[88,256]{1,0:T(8,128)}, f32[88,256]{1,0:T(8,128)S(1)}, u32[]{:S(2)}, u32[]{:S(2)}) collective-permute-start(f32[88,256]{1,0:T(8,128)} %param.10), channel_id=1, source_target_pairs={{0,8},{8,16},{16,24},{24,32},{32,40},{40,48},{48,56},{56,64},{64,7... | collective-permute-start | bytes 270344 | tf_op jit(solution)/shard_map/ppermute | solution.py:34
  6.8 1.9 %collective-permute-start.1 = (f32[88,256]{1,0:T(8,128)}, f32[88,256]{1,0:T(8,128)S(1)}, u32[]{:S(2)}, u32[]{:S(2)}) collective-permute-start(f32[88,256]{1,0:T(8,128)} %param.10), channel_id=1, source_target_pairs={{0,504},{8,0},{16,8},{24,16},{32,24},{40,32},{48,40},{56,48},{64,5... | collective-permute-start | bytes 270344 | tf_op jit(solution)/shard_map/ppermute | solution.py:34
  8.8 2.3 %select_reduce_fusion = f32[256,2048]{1,0:T(8,128)S(1)} fusion(f32[4,2048]{1,0:T(4,128)} %param.16, s32[4,2048]{1,0:T(4,128)} %param.15), kind=kLoop, calls=%fused_computation | loop fusion | flops 5767168 | bytes 2162688 | tf_op jit(solution)/shard_map/reduce_sum | solution.py:66
  11.1 0.0 copy-start.3
  11.1 0.0 collective-permute-done
  11.1 8.4 %collective-permute-done.1 = f32[88,256]{1,0:T(8,128)S(1)} collective-permute-done((f32[88,256]{1,0:T(8,128)}, f32[88,256]{1,0:T(8,128)S(1)}, u32[]{:S(2)}, u32[]{:S(2)}) %collective-permute-start.1) | collective-permute-done | bytes 90144 | tf_op jit(solution)/shard_map/ppermute | solution.py:34
  19.5 0.0 copy-done
  19.5 0.0 copy-done.8
  19.6 1.1 %fusion.1 = f32[264,9,256]{2,0,1:T(8,128)S(1)} fusion(s32[9,256]{1,0:T(8,128)S(1)} %copy-done.8, bf16[88,512]{1,0:T(8,128)(2,1)S(1)} %get-tuple-element.12, bf16[88,512]{1,0:T(8,128)(2,1)S(1)} %get-tuple-element.11, bf16[88,512]{1,0:T(8,128)(2,1)S(1)} %get-tuple-element.10), kind=kOutput, calls=%fused_computation.4 | convolution fusion | flops 624844800 | bytes 2712576 | tf_op jit(solution)/shard_map/dot_general | solution.py:20
  20.6 0.0 copy-done.3
  20.6 0.0 copy-start.1
  20.6 0.0 copy-start.2
  20.7 0.0 copy-start.7
  20.7 0.0 copy-start.5
  20.7 0.0 copy-start.6
  20.7 0.2 fusion.13
  20.9 0.5 copy-done.1
  21.3 0.0 copy-done.2
  21.4 0.0 copy-done.7
  21.4 1.4 %fusion.10 = f32[2048]{0:T(1024)S(1)} fusion(f32[256,2048]{1,0:T(8,128)S(1)} %select_reduce_fusion, f32[2048]{0:T(1024)S(1)} %copy-done.1, s32[2048]{0:T(1024)S(1)} %copy-done.2, s32[88]{0:T(128)S(1)} %get-tuple-element.17, s32[88]{0:T(128)S(1)} %get-tuple-element.16, f32[88,256]{1,0:T(8,128)S(1)} %fusion.13, f32[88]{0:T(128)S(1)} %copy-done.7), kind=kOutput, calls=%fused_computation.14 | convolution fusion | flops 554749952 | bytes 2212896 | tf_op jit(solution)/shard_map/dot_general | solution.py:73
  22.8 2.5 %psum.7 = f32[1,2048]{1,0:T(1,128)S(1)} all-reduce(f32[1,2048]{1,0:T(1,128)S(1)} %bitcast.9), channel_id=1, replica_groups=mesh['ang'=64,'zhi'=4,'core'=2] {'core'}, use_global_device_ids=true, to_apply=%region_3.4 | all-reduce | flops 2048 | bytes 16384 | tf_op jit(solution)/shard_map/psum | solution.py:75
  25.3 20.4 %all-gather = f32[4,1,2048]{2,1,0:T(1,128)S(1)} all-gather(f32[1,1,2048]{2,1,0:T(1,128)S(1)} %bitcast.10), channel_id=1, replica_groups=mesh['ang'=64,'zhi'=4,'core'=2] {'zhi'}, dimensions={0}, use_global_device_ids=true | all-gather | bytes 40960 | tf_op jit(solution)/shard_map/all_gather | solution.py:76
  45.7 0.0 copy-done.5
  45.7 0.0 copy-done.6
  45.7 0.0 copy-start.4
  45.8 2.1 %convolution_multiply_fusion.1 = f32[88,256]{1,0:T(8,128)S(1)} fusion(f32[256,2048]{1,0:T(8,128)S(1)} %select_reduce_fusion, f32[2048]{0:T(1024)S(1)} %multiply_divide_fusion, f32[2048]{0:T(1024)S(1)} %copy-done.1, s32[2048]{0:T(1024)S(1)} %copy-done.2, s32[88]{0:T(128)S(1)} %get-tuple-element.17, s32[88]{0:T(128)S(1)} %get-tuple-element.16, ...), kind=kOutput, calls=%fused_computation.19 | convolution fusion | flops 554594304 | bytes 2303008 | tf_op jit(solution)/shard_map/dot_general | solution.py:79
  47.8 0.2 reduce-precision_convert_fusion.1
  48.1 1.0 %fusion.4 = f32[264,512]{1,0:T(8,128)S(1)} fusion(s32[9,256]{1,0:T(8,128)S(1)} %copy-done.8, bf16[88,9,256]{2,0,1:T(8,128)(2,1)S(1)} %get-tuple-element.15, bf16[88,9,256]{2,0,1:T(8,128)(2,1)S(1)} %get-tuple-element.14, bf16[88,9,256]{2,0,1:T(8,128)(2,1)S(1)} %get-tuple-element.13), kind=kOutput, calls=%fused_computation.8 | convolution fusion | flops 627683328 | bytes 1766400 | tf_op jit(solution)/shard_map/dot_general | solution.py:26
  49.1 0.0 copy-done.4
  49.2 1.9 %collective-permute-start.2 = (f32[88,128]{1,0:T(8,128)S(1)}, f32[88,128]{1,0:T(8,128)S(1)}, u32[]{:S(2)}, u32[]{:S(2)}) collective-permute-start(f32[88,128]{1,0:T(8,128)S(1)} %get-tuple-element.4), channel_id=1, source_target_pairs={{0,8},{8,16},{16,24},{24,32},{32,40},{40,48},{48,56},{56,64},{64,7... | collective-permute-start | bytes 135176 | tf_op jit(solution)/shard_map/ppermute | solution.py:34
  51.1 3.9 %collective-permute-start.3 = (f32[88,128]{1,0:T(8,128)S(1)}, f32[88,128]{1,0:T(8,128)S(1)}, u32[]{:S(2)}, u32[]{:S(2)}) collective-permute-start(f32[88,128]{1,0:T(8,128)S(1)} %get-tuple-element.5), channel_id=1, source_target_pairs={{0,504},{8,0},{16,8},{24,16},{32,24},{40,32},{48,40},{56,48},{64,5... | collective-permute-start | bytes 135176 | tf_op jit(solution)/shard_map/ppermute | solution.py:34
  55.0 0.1 collective-permute-done.2
  55.1 7.9 %collective-permute-done.3 = f32[88,128]{1,0:T(8,128)S(1)} collective-permute-done((f32[88,128]{1,0:T(8,128)S(1)}, f32[88,128]{1,0:T(8,128)S(1)}, u32[]{:S(2)}, u32[]{:S(2)}) %collective-permute-start.3) | collective-permute-done | bytes 45088 | tf_op jit(solution)/shard_map/ppermute | solution.py:34
  63.1 0.6 %pad_maximum_fusion.1 = f32[88,256]{1,0:T(8,128)} fusion(f32[88,128]{1,0:T(8,128)S(1)} %get-tuple-element.7, f32[88,128]{1,0:T(8,128)S(1)} %get-tuple-element.6), kind=kLoop, calls=%fused_computation.49 | loop fusion | flops 22528 | bytes 180224 | tf_op jit(solution)/shard_map/concatenate | solution.py:94
  (9 shorter events, 0.2 us)
Async XLA Ops:
  0.6 18.9 %copy-start = (f32[88,256]{1,0:T(8,128)S(1)}, f32[88,256]{1,0:T(8,128)}, u32[]{:S(2)}) copy-start(f32[88,256]{1,0:T(8,128)} %param.10) | copy-start | bytes 270340
  0.6 18.9 %copy-start.8 = (s32[9,256]{1,0:T(8,128)S(1)}, s32[9,256]{1,0:T(8,128)}, u32[]{:S(2)}) copy-start(s32[9,256]{1,0:T(8,128)} %param.13) | copy-start | bytes 27652
  0.7 10.4 %collective-permute-start = (f32[88,256]{1,0:T(8,128)}, f32[88,256]{1,0:T(8,128)S(1)}, u32[]{:S(2)}, u32[]{:S(2)}) collective-permute-start(f32[88,256]{1,0:T(8,128)} %param.10), channel_id=1, source_target_pairs={{0,8},{8,16},{16,24},{24,32},{32,40},{40,48},{48,56},{56,64},{64,7... | collective-permute-start | bytes 270344 | tf_op jit(solution)/shard_map/ppermute | solution.py:34
  6.8 12.6 %collective-permute-start.1 = (f32[88,256]{1,0:T(8,128)}, f32[88,256]{1,0:T(8,128)S(1)}, u32[]{:S(2)}, u32[]{:S(2)}) collective-permute-start(f32[88,256]{1,0:T(8,128)} %param.10), channel_id=1, source_target_pairs={{0,504},{8,0},{16,8},{24,16},{32,24},{40,32},{48,40},{56,48},{64,5... | collective-permute-start | bytes 270344 | tf_op jit(solution)/shard_map/ppermute | solution.py:34
  11.1 9.6 %copy-start.3 = (f32[88,9]{0,1:T(8,128)S(1)}, f32[88,9]{0,1:T(8,128)}, u32[]{:S(2)}) copy-start(f32[88,9]{0,1:T(8,128)} %param.11) | copy-start | bytes 9508
  20.6 0.7 %copy-start.1 = (f32[2048]{0:T(1024)S(1)}, f32[2048]{0:T(1024)}, u32[]{:S(2)}) copy-start(f32[2048]{0:T(1024)} %param.17) | copy-start | bytes 24580
  20.6 0.7 %copy-start.2 = (s32[2048]{0:T(1024)S(1)}, s32[2048]{0:T(1024)}, u32[]{:S(2)}) copy-start(s32[2048]{0:T(1024)} %param.14) | copy-start | bytes 24580
  20.7 0.7 %copy-start.7 = (f32[88]{0:T(128)S(1)}, f32[88]{0:T(128)}, u32[]{:S(2)}) copy-start(f32[88]{0:T(128)} %param.12) | copy-start | bytes 1060
  20.7 25.1 %copy-start.5 = (f32[2048]{0:T(1024)S(1)}, f32[2048]{0:T(1024)}, u32[]{:S(2)}) copy-start(f32[2048]{0:T(1024)} %param.19) | copy-start | bytes 24580
  20.7 25.1 %copy-start.6 = (f32[2048]{0:T(1024)S(1)}, f32[2048]{0:T(1024)}, u32[]{:S(2)}) copy-start(f32[2048]{0:T(1024)} %param.18) | copy-start | bytes 24580
  45.7 3.3 %copy-start.4 = (f32[2048]{0:T(1024)}, f32[2048]{0:T(1024)S(1)}, u32[]{:S(2)}) copy-start(f32[2048]{0:T(1024)S(1)} %reduce_sum.39) | copy-start | bytes 24580
  49.2 5.9 %collective-permute-start.2 = (f32[88,128]{1,0:T(8,128)S(1)}, f32[88,128]{1,0:T(8,128)S(1)}, u32[]{:S(2)}, u32[]{:S(2)}) collective-permute-start(f32[88,128]{1,0:T(8,128)S(1)} %get-tuple-element.4), channel_id=1, source_target_pairs={{0,8},{8,16},{16,24},{24,32},{32,40},{40,48},{48,56},{56,64},{64,7... | collective-permute-start | bytes 135176 | tf_op jit(solution)/shard_map/ppermute | solution.py:34
  51.1 12.0 %collective-permute-start.3 = (f32[88,128]{1,0:T(8,128)S(1)}, f32[88,128]{1,0:T(8,128)S(1)}, u32[]{:S(2)}, u32[]{:S(2)}) collective-permute-start(f32[88,128]{1,0:T(8,128)S(1)} %get-tuple-element.5), channel_id=1, source_target_pairs={{0,504},{8,0},{16,8},{24,16},{32,24},{40,32},{48,40},{56,48},{64,5... | collective-permute-start | bytes 135176 | tf_op jit(solution)/shard_map/ppermute | solution.py:34

commit v13 on v12

--- a/solution.py
+++ b/solution.py
@@ -27,6 +27,18 @@
         split3(value), onehot, (((1, 2), (1, 2)), ((), ())), preferred_element_type=jnp.float32
     )
     return product[:rows] + product[rows : 2 * rows] + product[2 * rows :]
+
+
+def chip_sum(value, axis):
+    count = lax.axis_size(axis)
+    if count != 4:
+        return jnp.sum(lax.all_gather(value, axis), axis=0)
+    from_next = ring(value, axis, -1)
+    from_prev = ring(value, axis, 1)
+    opposite = ring(from_next, axis, -1)
+    relative = jnp.stack([value, from_next, opposite, from_prev])
+    ordered = jnp.roll(relative, lax.axis_index(axis), axis=0)
+    return jnp.sum(ordered, axis=0)
 
 
 def ring(value, axis, step):
@@ -73,7 +85,7 @@
     at_stars = jnp.dot(weighted, spread, precision=HIGHEST, preferred_element_type=jnp.float32)
     partial_value = jnp.sum(radial * at_stars, axis=0)
     pair = lax.psum(partial_value, "core")
-    predicted = jnp.sum(lax.all_gather(pair, "zhi"), axis=0)
+    predicted = chip_sum(pair, "zhi")
     weight_back = (predicted - observed) / (sigma * sigma)
 
     adjoint_sum = lax.dot_general(

time: 64.1 us -> 63 us (0.983)
  the two profiles are of different devices: /device:TPU:126 before, /device:TPU:1 now
where the time goes in v13:
time: 63 us; the launch traced here: 62.1 us
  starting transfers between devices  41.9 us (67%)
  blocking collectives  7.3 us (12%)
  matrix products  5.52 us (9%)
  other arithmetic  3.49 us (6%)
  waiting for transfers between devices  2.31 us (4%)
  between operations  0.98 us (2%)
  local copies, waits for them, and re-layouts  0.65 us (1%)
    ppermute x7, starting transfers between devices, ring(): lax.ppermute(value, axis, [(i, (i + step) % count) for i in range(count)])  41.9 us
    psum x1, blocking collectives, on_device(): pair = lax.psum(partial_value, 'core')  7.3 us
    ppermute x7, waiting for transfers between devices, ring(): lax.ppermute(value, axis, [(i, (i + step) % count) for i in range(count)])  2.31 us
    reduce_sum x1, other arithmetic, on_device(): jnp.sum(jnp.where(pixel_id[None] == star_pixels[:, None, :], star_weights...  2.28 us
    dot_general x1, matrix products, on_device(): lax.dot_general(radial * weight_back[None, :], spread, (((1,), (1,)), (()...  2.06 us
    dot_general x1, matrix products, on_device(): jnp.dot(weighted, spread, precision=HIGHEST, preferred_element_type=jnp.f...  1.4 us
  transfers between devices with their start and end apart: 7, of which 2 were waited for; matrix products, arithmetic and copies ran while one was open for 4% of the time, Pallas kernels for 0%

profile of v13, /device:TPU:1, one launch (start us, length us, event | category | flops | bytes accessed | tf_op | source)
XLA Modules:
  0.0 62.1 jit_solution(11735617142519952114)
XLA Ops:
  0.6 0.0 copy-start
  0.6 0.0 copy-start.8
  0.7 4.2 %collective-permute-start = (f32[88,256]{1,0:T(8,128)}, f32[88,256]{1,0:T(8,128)S(1)}, u32[]{:S(2)}, u32[]{:S(2)}) collective-permute-start(f32[88,256]{1,0:T(8,128)} %param.10), channel_id=1, source_target_pairs={{0,8},{8,16},{16,24},{24,32},{32,40},{40,48},{48,56},{56,64},{64,7... | collective-permute-start | bytes 270344 | tf_op jit(solution)/shard_map/ppermute | solution.py:46
  4.8 9.6 %collective-permute-start.1 = (f32[88,256]{1,0:T(8,128)}, f32[88,256]{1,0:T(8,128)S(1)}, u32[]{:S(2)}, u32[]{:S(2)}) collective-permute-start(f32[88,256]{1,0:T(8,128)} %param.10), channel_id=1, source_target_pairs={{0,504},{8,0},{16,8},{24,16},{32,24},{40,32},{48,40},{56,48},{64,5... | collective-permute-start | bytes 270344 | tf_op jit(solution)/shard_map/ppermute | solution.py:46
  14.5 2.3 %select_reduce_fusion = f32[256,2048]{1,0:T(8,128)S(1)} fusion(f32[4,2048]{1,0:T(4,128)} %param.16, s32[4,2048]{1,0:T(4,128)} %param.15), kind=kLoop, calls=%fused_computation | loop fusion | flops 5767168 | bytes 2162688 | tf_op jit(solution)/shard_map/reduce_sum | solution.py:78
  16.7 0.0 copy-start.3
  16.8 0.0 collective-permute-done
  16.8 0.0 collective-permute-done.1
  16.8 0.0 copy-done
  16.9 0.0 copy-done.8
  16.9 1.1 %fusion.1 = f32[264,9,256]{2,0,1:T(8,128)S(1)} fusion(s32[9,256]{1,0:T(8,128)S(1)} %copy-done.8, bf16[88,512]{1,0:T(8,128)(2,1)S(1)} %get-tuple-element.12, bf16[88,512]{1,0:T(8,128)(2,1)S(1)} %get-tuple-element.11, bf16[88,512]{1,0:T(8,128)(2,1)S(1)} %get-tuple-element.10), kind=kOutput, calls=%fused_computation.4 | convolution fusion | flops 624844800 | bytes 2712576 | tf_op jit(solution)/shard_map/dot_general | solution.py:20
  18.0 0.0 copy-done.3
  18.0 0.0 copy-start.1
  18.0 0.0 copy-start.2
  18.0 0.0 copy-start.7
  18.0 0.0 copy-start.5
  18.0 0.0 copy-start.6
  18.0 0.2 fusion.13
  18.2 0.5 copy-done.1
  18.7 0.0 copy-done.2
  18.7 0.0 copy-done.7
  18.7 1.4 %fusion.10 = f32[2048]{0:T(1024)S(1)} fusion(f32[256,2048]{1,0:T(8,128)S(1)} %select_reduce_fusion, f32[2048]{0:T(1024)S(1)} %copy-done.1, s32[2048]{0:T(1024)S(1)} %copy-done.2, s32[88]{0:T(128)S(1)} %get-tuple-element.17, s32[88]{0:T(128)S(1)} %get-tuple-element.16, f32[88,256]{1,0:T(8,128)S(1)} %fusion.13, f32[88]{0:T(128)S(1)} %copy-done.7), kind=kOutput, calls=%fused_computation.14 | convolution fusion | flops 554749952 | bytes 2212896 | tf_op jit(solution)/shard_map/dot_general | solution.py:85
  20.1 7.3 %psum.7 = f32[2048]{0:T(1024)S(1)} all-reduce(f32[2048]{0:T(1024)S(1)} %fusion.10), channel_id=1, replica_groups=mesh['ang'=64,'zhi'=4,'core'=2] {'core'}, use_global_device_ids=true, to_apply=%region_3.4 | all-reduce | flops 2048 | bytes 16384 | tf_op jit(solution)/shard_map/psum | solution.py:87
  27.4 7.1 %collective-permute-start.2 = (f32[2048]{0:T(1024)S(1)}, f32[2048]{0:T(1024)S(1)}, u32[]{:S(2)}, u32[]{:S(2)}) collective-permute-start(f32[2048]{0:T(1024)S(1)} %psum.7), channel_id=1, source_target_pairs={{0,6},{2,0},{4,2},{6,4},{1,7},{3,1},{5,3},{7,5},{8,14},{10,8},{12,... | collective-permute-start | bytes 24584 | tf_op jit(solution)/shard_map/ppermute | solution.py:46
  34.5 2.1 %collective-permute-start.4 = (f32[2048]{0:T(1024)S(1)}, f32[2048]{0:T(1024)S(1)}, u32[]{:S(2)}, u32[]{:S(2)}) collective-permute-start(f32[2048]{0:T(1024)S(1)} %psum.7), channel_id=1, source_target_pairs={{0,2},{2,4},{4,6},{6,0},{1,3},{3,5},{5,7},{7,1},{8,10},{10,12},{12... | collective-permute-start | bytes 24584 | tf_op jit(solution)/shard_map/ppermute | solution.py:46
  36.6 0.0 collective-permute-done.2
  36.6 7.1 %collective-permute-start.3 = (f32[2048]{0:T(1024)S(1)}, f32[2048]{0:T(1024)S(1)}, u32[]{:S(2)}, u32[]{:S(2)}) collective-permute-start(f32[2048]{0:T(1024)S(1)} %collective-permute-done.2), channel_id=1, source_target_pairs={{0,6},{2,0},{4,2},{6,4},{1,7},{3,1},{5,3},{7,5},{8,14},{10,8},{12,... | collective-permute-start | bytes 24584 | tf_op jit(solution)/shard_map/ppermute | solution.py:46
  43.7 0.0 collective-permute-done.4
  43.7 1.2 %collective-permute-done.3 = f32[2048]{0:T(1024)S(1)} collective-permute-done((f32[2048]{0:T(1024)S(1)}, f32[2048]{0:T(1024)S(1)}, u32[]{:S(2)}, u32[]{:S(2)}) %collective-permute-start.3) | collective-permute-done | bytes 8224 | tf_op jit(solution)/shard_map/ppermute | solution.py:46
  44.9 0.1 concatenate.21
  45.0 0.0 copy-done.5
  45.1 0.0 copy-done.6
  45.1 0.0 copy-start.4
  45.1 2.1 %convolution_multiply_fusion.1 = f32[88,256]{1,0:T(8,128)S(1)} fusion(f32[256,2048]{1,0:T(8,128)S(1)} %select_reduce_fusion, f32[2048]{0:T(1024)S(1)} %multiply_divide_fusion, f32[2048]{0:T(1024)S(1)} %copy-done.1, s32[2048]{0:T(1024)S(1)} %copy-done.2, s32[88]{0:T(128)S(1)} %get-tuple-element.17, s32[88]{0:T(128)S(1)} %get-tuple-element.16, ...), kind=kOutput, calls=%fused_computation.19 | convolution fusion | flops 554594304 | bytes 2303008 | tf_op jit(solution)/shard_map/dot_general | solution.py:91
  47.2 0.2 reduce-precision_convert_fusion.1
  47.4 1.0 %fusion.4 = f32[264,512]{1,0:T(8,128)S(1)} fusion(s32[9,256]{1,0:T(8,128)S(1)} %copy-done.8, bf16[88,9,256]{2,0,1:T(8,128)(2,1)S(1)} %get-tuple-element.15, bf16[88,9,256]{2,0,1:T(8,128)(2,1)S(1)} %get-tuple-element.14, bf16[88,9,256]{2,0,1:T(8,128)(2,1)S(1)} %get-tuple-element.13), kind=kOutput, calls=%fused_computation.8 | convolution fusion | flops 627683328 | bytes 1766400 | tf_op jit(solution)/shard_map/dot_general | solution.py:26
  48.4 0.0 copy-done.4
  48.5 1.9 %collective-permute-start.5 = (f32[88,128]{1,0:T(8,128)S(1)}, f32[88,128]{1,0:T(8,128)S(1)}, u32[]{:S(2)}, u32[]{:S(2)}) collective-permute-start(f32[88,128]{1,0:T(8,128)S(1)} %get-tuple-element.4), channel_id=1, source_target_pairs={{0,8},{8,16},{16,24},{24,32},{32,40},{40,48},{48,56},{56,64},{64,7... | collective-permute-start | bytes 135176 | tf_op jit(solution)/shard_map/ppermute | solution.py:46
  50.4 9.9 %collective-permute-start.6 = (f32[88,128]{1,0:T(8,128)S(1)}, f32[88,128]{1,0:T(8,128)S(1)}, u32[]{:S(2)}, u32[]{:S(2)}) collective-permute-start(f32[88,128]{1,0:T(8,128)S(1)} %get-tuple-element.5), channel_id=1, source_target_pairs={{0,504},{8,0},{16,8},{24,16},{32,24},{40,32},{48,40},{56,48},{64,5... | collective-permute-start | bytes 135176 | tf_op jit(solution)/shard_map/ppermute | solution.py:46
  60.3 0.0 collective-permute-done.5
  60.4 1.1 %collective-permute-done.6 = f32[88,128]{1,0:T(8,128)S(1)} collective-permute-done((f32[88,128]{1,0:T(8,128)S(1)}, f32[88,128]{1,0:T(8,128)S(1)}, u32[]{:S(2)}, u32[]{:S(2)}) %collective-permute-start.6) | collective-permute-done | bytes 45088 | tf_op jit(solution)/shard_map/ppermute | solution.py:46
  61.5 0.6 %pad_maximum_fusion.1 = f32[88,256]{1,0:T(8,128)} fusion(f32[88,128]{1,0:T(8,128)S(1)} %get-tuple-element.7, f32[88,128]{1,0:T(8,128)S(1)} %get-tuple-element.6), kind=kLoop, calls=%fused_computation.49 | loop fusion | flops 22528 | bytes 180224 | tf_op jit(solution)/shard_map/concatenate | solution.py:106
  (9 shorter events, 0.2 us)
Async XLA Ops:
  0.6 16.2 %copy-start = (f32[88,256]{1,0:T(8,128)S(1)}, f32[88,256]{1,0:T(8,128)}, u32[]{:S(2)}) copy-start(f32[88,256]{1,0:T(8,128)} %param.10) | copy-start | bytes 270340
  0.6 16.2 %copy-start.8 = (s32[9,256]{1,0:T(8,128)S(1)}, s32[9,256]{1,0:T(8,128)}, u32[]{:S(2)}) copy-start(s32[9,256]{1,0:T(8,128)} %param.13) | copy-start | bytes 27652
  0.7 16.1 %collective-permute-start = (f32[88,256]{1,0:T(8,128)}, f32[88,256]{1,0:T(8,128)S(1)}, u32[]{:S(2)}, u32[]{:S(2)}) collective-permute-start(f32[88,256]{1,0:T(8,128)} %param.10), channel_id=1, source_target_pairs={{0,8},{8,16},{16,24},{24,32},{32,40},{40,48},{48,56},{56,64},{64,7... | collective-permute-start | bytes 270344 | tf_op jit(solution)/shard_map/ppermute | solution.py:46
  4.8 12.0 %collective-permute-start.1 = (f32[88,256]{1,0:T(8,128)}, f32[88,256]{1,0:T(8,128)S(1)}, u32[]{:S(2)}, u32[]{:S(2)}) collective-permute-start(f32[88,256]{1,0:T(8,128)} %param.10), channel_id=1, source_target_pairs={{0,504},{8,0},{16,8},{24,16},{32,24},{40,32},{48,40},{56,48},{64,5... | collective-permute-start | bytes 270344 | tf_op jit(solution)/shard_map/ppermute | solution.py:46
  16.7 1.2 %copy-start.3 = (f32[88,9]{0,1:T(8,128)S(1)}, f32[88,9]{0,1:T(8,128)}, u32[]{:S(2)}) copy-start(f32[88,9]{0,1:T(8,128)} %param.11) | copy-start | bytes 9508
  18.0 0.7 %copy-start.1 = (f32[2048]{0:T(1024)S(1)}, f32[2048]{0:T(1024)}, u32[]{:S(2)}) copy-start(f32[2048]{0:T(1024)} %param.17) | copy-start | bytes 24580
  18.0 0.7 %copy-start.2 = (s32[2048]{0:T(1024)S(1)}, s32[2048]{0:T(1024)}, u32[]{:S(2)}) copy-start(s32[2048]{0:T(1024)} %param.14) | copy-start | bytes 24580
  18.0 0.7 %copy-start.7 = (f32[88]{0:T(128)S(1)}, f32[88]{0:T(128)}, u32[]{:S(2)}) copy-start(f32[88]{0:T(128)} %param.12) | copy-start | bytes 1060
  18.0 27.0 %copy-start.5 = (f32[2048]{0:T(1024)S(1)}, f32[2048]{0:T(1024)}, u32[]{:S(2)}) copy-start(f32[2048]{0:T(1024)} %param.19) | copy-start | bytes 24580
  18.0 27.0 %copy-start.6 = (f32[2048]{0:T(1024)S(1)}, f32[2048]{0:T(1024)}, u32[]{:S(2)}) copy-start(f32[2048]{0:T(1024)} %param.18) | copy-start | bytes 24580
  27.4 9.2 %collective-permute-start.2 = (f32[2048]{0:T(1024)S(1)}, f32[2048]{0:T(1024)S(1)}, u32[]{:S(2)}, u32[]{:S(2)}) collective-permute-start(f32[2048]{0:T(1024)S(1)} %psum.7), channel_id=1, source_target_pairs={{0,6},{2,0},{4,2},{6,4},{1,7},{3,1},{5,3},{7,5},{8,14},{10,8},{12,... | collective-permute-start | bytes 24584 | tf_op jit(solution)/shard_map/ppermute | solution.py:46
  34.5 9.2 %collective-permute-start.4 = (f32[2048]{0:T(1024)S(1)}, f32[2048]{0:T(1024)S(1)}, u32[]{:S(2)}, u32[]{:S(2)}) collective-permute-start(f32[2048]{0:T(1024)S(1)} %psum.7), channel_id=1, source_target_pairs={{0,2},{2,4},{4,6},{6,0},{1,3},{3,5},{5,7},{7,1},{8,10},{10,12},{12... | collective-permute-start | bytes 24584 | tf_op jit(solution)/shard_map/ppermute | solution.py:46
  36.6 8.3 %collective-permute-start.3 = (f32[2048]{0:T(1024)S(1)}, f32[2048]{0:T(1024)S(1)}, u32[]{:S(2)}, u32[]{:S(2)}) collective-permute-start(f32[2048]{0:T(1024)S(1)} %collective-permute-done.2), channel_id=1, source_target_pairs={{0,6},{2,0},{4,2},{6,4},{1,7},{3,1},{5,3},{7,5},{8,14},{10,8},{12,... | collective-permute-start | bytes 24584 | tf_op jit(solution)/shard_map/ppermute | solution.py:46
  45.1 3.3 %copy-start.4 = (f32[2048]{0:T(1024)}, f32[2048]{0:T(1024)S(1)}, u32[]{:S(2)}) copy-start(f32[2048]{0:T(1024)S(1)} %dynamic-slice_reduce_fusion) | copy-start | bytes 24580
  48.5 11.9 %collective-permute-start.5 = (f32[88,128]{1,0:T(8,128)S(1)}, f32[88,128]{1,0:T(8,128)S(1)}, u32[]{:S(2)}, u32[]{:S(2)}) collective-permute-start(f32[88,128]{1,0:T(8,128)S(1)} %get-tuple-element.4), channel_id=1, source_target_pairs={{0,8},{8,16},{16,24},{24,32},{32,40},{40,48},{48,56},{56,64},{64,7... | collective-permute-start | bytes 135176 | tf_op jit(solution)/shard_map/ppermute | solution.py:46
  50.4 11.1 %collective-permute-start.6 = (f32[88,128]{1,0:T(8,128)S(1)}, f32[88,128]{1,0:T(8,128)S(1)}, u32[]{:S(2)}, u32[]{:S(2)}) collective-permute-start(f32[88,128]{1,0:T(8,128)S(1)} %get-tuple-element.5), channel_id=1, source_target_pairs={{0,504},{8,0},{16,8},{24,16},{32,24},{40,32},{48,40},{56,48},{64,5... | collective-permute-start | bytes 135176 | tf_op jit(solution)/shard_map/ppermute | solution.py:46

commit v14 on v13

--- a/solution.py
+++ b/solution.py
@@ -7,26 +7,28 @@
 HIGHEST = lax.Precision.HIGHEST
 
 
-def split3(value):
+def split3(value, axis):
     high = lax.reduce_precision(value, exponent_bits=8, mantissa_bits=7)
     rest = value - high
     middle = lax.reduce_precision(rest, exponent_bits=8, mantissa_bits=7)
     low = rest - middle
-    return jnp.concatenate([high, middle, low], axis=0).astype(jnp.bfloat16)
+    return jnp.concatenate([high, middle, low], axis=axis).astype(jnp.bfloat16)
 
 
-def select(value, onehot):
-    rows = value.shape[0]
-    product = lax.dot_general(split3(value), onehot, (((1,), (0,)), ((), ())), preferred_element_type=jnp.float32)
-    return product[:rows] + product[rows : 2 * rows] + product[2 * rows :]
+def select(value, table):
+    frame = value.shape[1]
+    position = lax.broadcasted_iota(jnp.int32, (3 * frame,) + table.shape, 0) % frame
+    onehot = (position == table[None]).astype(jnp.bfloat16)
+    return lax.dot_general(split3(value, 1), onehot, (((1,), (0,)), ((), ())), preferred_element_type=jnp.float32)
 
 
-def spread_select(value, onehot):
-    rows = value.shape[0]
-    product = lax.dot_general(
-        split3(value), onehot, (((1, 2), (1, 2)), ((), ())), preferred_element_type=jnp.float32
+def spread_select(value, table, frame):
+    tiled = jnp.concatenate([table] * 3, axis=0)
+    position = lax.broadcasted_iota(jnp.int32, (frame,) + tiled.shape, 0)
+    onehot = (position == tiled[None]).astype(jnp.bfloat16)
+    return lax.dot_general(
+        split3(value, 1), onehot, (((1, 2), (1, 2)), ((), ())), preferred_element_type=jnp.float32
     )
-    return product[:rows] + product[rows : 2 * rows] + product[2 * rows :]
 
 
 def chip_sum(value, axis):
@@ -66,9 +68,7 @@
     after = ring(latent, "ang", -1)
     wide = jnp.concatenate([before[:, pixels - COLS :], latent, after[:, :COLS]], axis=1)
 
-    position = lax.broadcasted_iota(jnp.int32, (frame, taps, pixels), 0)
-    pick = (position == neighbours[None, :, :]).astype(jnp.bfloat16)
-    picked = select(wide, pick)
+    picked = select(wide, neighbours)
     refined = jnp.sum(picked * stencil[:, :, None], axis=1)
     density = jnp.exp(refined)
     weighted = bin_width[:, None] * density
@@ -98,7 +98,7 @@
     sensitivity = adjoint_sum * weighted
 
     terms = stencil[:, :, None] * sensitivity[:, None, :]
-    framed = spread_select(terms, pick)
+    framed = spread_select(terms, neighbours, frame)
     to_after, to_before = lax.optimization_barrier((framed[:, frame - COLS :], framed[:, :COLS]))
     from_before = ring(to_after, "ang", 1)
     from_after = ring(to_before, "ang", -1)

time: 63 us -> 65.7 us (1.043)
  matrix products: 5.52 us -> 8.85 us
    dot_general x2, matrix products: 2.06 us -> 5.39 us  [the longest x1 2.79 us: spread_select(): lax.dot_general(split3(value, 1), onehot, (((1, 2), (1, 2)), ((), ())), p...]
where the time goes in v14:
time: 65.7 us; the launch traced here: 64.8 us
  starting transfers between devices  41.9 us (64%)
  matrix products  8.85 us (13%)
  blocking collectives  7.29 us (11%)
  other arithmetic  3.3 us (5%)
  waiting for transfers between devices  2.28 us (3%)
  between operations  1 us (2%)
    ppermute x7, starting transfers between devices, ring(): lax.ppermute(value, axis, [(i, (i + step) % count) for i in range(count)])  41.9 us
    psum x1, blocking collectives, on_device(): pair = lax.psum(partial_value, 'core')  7.29 us
    dot_general x1, matrix products, spread_select(): lax.dot_general(split3(value, 1), onehot, (((1, 2), (1, 2)), ((), ())), p...  2.79 us
    dot_general x1, matrix products, select(): lax.dot_general(split3(value, 1), onehot, (((1,), (0,)), ((), ())), prefe...  2.61 us
    reduce_sum x1, other arithmetic, on_device(): jnp.sum(jnp.where(pixel_id[None] == star_pixels[:, None, :], star_weights...  2.29 us
    ppermute x7, waiting for transfers between devices, ring(): lax.ppermute(value, axis, [(i, (i + step) % count) for i in range(count)])  2.28 us
    dot_general x1, matrix products, on_device(): lax.dot_general(radial * weight_back[None, :], spread, (((1,), (1,)), (()...  2.06 us
    dot_general x1, matrix products, on_device(): jnp.dot(weighted, spread, precision=HIGHEST, preferred_element_type=jnp.f...  1.4 us
  transfers between devices with their start and end apart: 7, of which 2 were waited for; matrix products, arithmetic and copies ran while one was open for 4% of the time, Pallas kernels for 0%

profile of v14, /device:TPU:1, one launch (start us, length us, event | category | flops | bytes accessed | tf_op | source)
XLA Modules:
  0.0 64.8 jit_solution(10569910147020873184)
XLA Ops:
  0.6 0.0 copy-start
  0.6 0.0 copy-start.5
  0.6 0.0 copy-start.4
  0.7 4.2 %collective-permute-start = (f32[88,256]{1,0:T(8,128)}, f32[88,256]{1,0:T(8,128)S(1)}, u32[]{:S(2)}, u32[]{:S(2)}) collective-permute-start(f32[88,256]{1,0:T(8,128)} %param.10), channel_id=1, source_target_pairs={{0,8},{8,16},{16,24},{24,32},{32,40},{40,48},{48,56},{56,64},{64,7... | collective-permute-start | bytes 270344 | tf_op jit(solution)/shard_map/ppermute | solution.py:48
  4.8 9.6 %collective-permute-start.1 = (f32[88,256]{1,0:T(8,128)}, f32[88,256]{1,0:T(8,128)S(1)}, u32[]{:S(2)}, u32[]{:S(2)}) collective-permute-start(f32[88,256]{1,0:T(8,128)} %param.10), channel_id=1, source_target_pairs={{0,504},{8,0},{16,8},{24,16},{32,24},{40,32},{48,40},{56,48},{64,5... | collective-permute-start | bytes 270344 | tf_op jit(solution)/shard_map/ppermute | solution.py:48
  14.5 2.3 %select_reduce_fusion = f32[256,2048]{1,0:T(8,128)S(1)} fusion(f32[4,2048]{1,0:T(4,128)} %param.16, s32[4,2048]{1,0:T(4,128)} %param.15), kind=kLoop, calls=%fused_computation.4 | loop fusion | flops 5767168 | bytes 2162688 | tf_op jit(solution)/shard_map/reduce_sum | solution.py:78
  16.8 0.0 collective-permute-done
  16.8 0.0 collective-permute-done.1
  16.8 0.0 copy-done
  16.9 0.0 copy-done.5
  16.9 0.0 copy-done.4
  16.9 0.0 copy-start.1
  16.9 0.0 copy-start.2
  16.9 0.0 copy-start.8
  16.9 2.6 %fusion.14 = f32[88,256]{1,0:T(8,128)S(1)} fusion(s32[9,256]{1,0:T(8,128)S(1)} %copy-done.4, s32[1536]{0:T(1024)S(1)} %get-tuple-element.18, s32[1536]{0:T(1024)S(1)} %get-tuple-element.19, pred[1536]{0:T(1024)(128)(4,1)S(1)} %fusion.38, f32[88,9]{0,1:T(8,128)S(1)} %copy-done.5, bf16[88,512]{1,0:T(8,128)(2,1)S(1)} %get-tuple-element.12, ...), kind=kOutput, calls=%fused_computation.19 | convolution fusion | flops 631126016 | bytes 386656 | tf_op jit(solution)/shard_map/dot_general | solution.py:22
  19.6 0.0 copy-start.6
  19.6 0.0 copy-start.7
  19.6 0.0 copy-done.1
  19.6 0.0 copy-done.2
  19.6 0.0 copy-done.8
  19.6 1.4 %fusion.13 = f32[2048]{0:T(1024)S(1)} fusion(f32[256,2048]{1,0:T(8,128)S(1)} %select_reduce_fusion, f32[2048]{0:T(1024)S(1)} %copy-done.1, s32[2048]{0:T(1024)S(1)} %copy-done.2, s32[88]{0:T(128)S(1)} %get-tuple-element.17, s32[88]{0:T(128)S(1)} %get-tuple-element.16, f32[88,256]{1,0:T(8,128)S(1)} %fusion.14, f32[88]{0:T(128)S(1)} %copy-done.8), kind=kOutput, calls=%fused_computation.18 | convolution fusion | flops 554749952 | bytes 2212896 | tf_op jit(solution)/shard_map/dot_general | solution.py:85
  21.0 7.3 %psum.7 = f32[2048]{0:T(1024)S(1)} all-reduce(f32[2048]{0:T(1024)S(1)} %fusion.13), channel_id=1, replica_groups=mesh['ang'=64,'zhi'=4,'core'=2] {'core'}, use_global_device_ids=true, to_apply=%region_3.4 | all-reduce | flops 2048 | bytes 16384 | tf_op jit(solution)/shard_map/psum | solution.py:87
  28.3 7.1 %collective-permute-start.2 = (f32[2048]{0:T(1024)S(1)}, f32[2048]{0:T(1024)S(1)}, u32[]{:S(2)}, u32[]{:S(2)}) collective-permute-start(f32[2048]{0:T(1024)S(1)} %psum.7), channel_id=1, source_target_pairs={{0,6},{2,0},{4,2},{6,4},{1,7},{3,1},{5,3},{7,5},{8,14},{10,8},{12,... | collective-permute-start | bytes 24584 | tf_op jit(solution)/shard_map/ppermute | solution.py:48
  35.4 2.1 %collective-permute-start.4 = (f32[2048]{0:T(1024)S(1)}, f32[2048]{0:T(1024)S(1)}, u32[]{:S(2)}, u32[]{:S(2)}) collective-permute-start(f32[2048]{0:T(1024)S(1)} %psum.7), channel_id=1, source_target_pairs={{0,2},{2,4},{4,6},{6,0},{1,3},{3,5},{5,7},{7,1},{8,10},{10,12},{12... | collective-permute-start | bytes 24584 | tf_op jit(solution)/shard_map/ppermute | solution.py:48
  37.5 0.0 collective-permute-done.2
  37.5 7.1 %collective-permute-start.3 = (f32[2048]{0:T(1024)S(1)}, f32[2048]{0:T(1024)S(1)}, u32[]{:S(2)}, u32[]{:S(2)}) collective-permute-start(f32[2048]{0:T(1024)S(1)} %collective-permute-done.2), channel_id=1, source_target_pairs={{0,6},{2,0},{4,2},{6,4},{1,7},{3,1},{5,3},{7,5},{8,14},{10,8},{12,... | collective-permute-start | bytes 24584 | tf_op jit(solution)/shard_map/ppermute | solution.py:48
  44.6 0.0 collective-permute-done.4
  44.6 1.2 %collective-permute-done.3 = f32[2048]{0:T(1024)S(1)} collective-permute-done((f32[2048]{0:T(1024)S(1)}, f32[2048]{0:T(1024)S(1)}, u32[]{:S(2)}, u32[]{:S(2)}) %collective-permute-start.3) | collective-permute-done | bytes 8224 | tf_op jit(solution)/shard_map/ppermute | solution.py:48
  45.8 0.1 concatenate.24
  46.0 0.0 copy-done.6
  46.0 0.0 copy-done.7
  46.0 0.0 copy-start.3
  46.0 2.1 %convolution_multiply_fusion.1 = f32[88,256]{1,0:T(8,128)S(1)} fusion(f32[256,2048]{1,0:T(8,128)S(1)} %select_reduce_fusion, f32[2048]{0:T(1024)S(1)} %multiply_divide_fusion, f32[2048]{0:T(1024)S(1)} %copy-done.1, s32[2048]{0:T(1024)S(1)} %copy-done.2, s32[88]{0:T(128)S(1)} %get-tuple-element.17, s32[88]{0:T(128)S(1)} %get-tuple-element.16, ...), kind=kOutput, calls=%fused_computation.25 | convolution fusion | flops 554594304 | bytes 2303008 | tf_op jit(solution)/shard_map/dot_general | solution.py:91
  48.1 0.2 reduce-precision_convert_fusion.1
  48.3 2.8 %fusion.15 = f32[88,512]{1,0:T(8,128)S(1)} fusion(s32[27,256]{1,0:T(8,128)S(1)} %pad_add_fusion, bf16[88,9,256]{2,0,1:T(8,128)(2,1)S(1)} %get-tuple-element.15, bf16[88,9,256]{2,0,1:T(8,128)(2,1)S(1)} %get-tuple-element.14, bf16[88,9,256]{2,0,1:T(8,128)(2,1)S(1)} %get-tuple-element.13), kind=kOutput, calls=%fused_computation.24 | convolution fusion | flops 627609600 | bytes 1424384 | tf_op jit(solution)/shard_map/dot_general | solution.py:29
  51.1 0.0 copy-done.3
  51.1 1.9 %collective-permute-start.5 = (f32[88,128]{1,0:T(8,128)S(1)}, f32[88,128]{1,0:T(8,128)S(1)}, u32[]{:S(2)}, u32[]{:S(2)}) collective-permute-start(f32[88,128]{1,0:T(8,128)S(1)} %get-tuple-element.4), channel_id=1, source_target_pairs={{0,8},{8,16},{16,24},{24,32},{32,40},{40,48},{48,56},{56,64},{64,7... | collective-permute-start | bytes 135176 | tf_op jit(solution)/shard_map/ppermute | solution.py:48
  53.1 9.9 %collective-permute-start.6 = (f32[88,128]{1,0:T(8,128)S(1)}, f32[88,128]{1,0:T(8,128)S(1)}, u32[]{:S(2)}, u32[]{:S(2)}) collective-permute-start(f32[88,128]{1,0:T(8,128)S(1)} %get-tuple-element.5), channel_id=1, source_target_pairs={{0,504},{8,0},{16,8},{24,16},{32,24},{40,32},{48,40},{56,48},{64,5... | collective-permute-start | bytes 135176 | tf_op jit(solution)/shard_map/ppermute | solution.py:48
  63.0 0.0 collective-permute-done.5
  63.0 1.1 %collective-permute-done.6 = f32[88,128]{1,0:T(8,128)S(1)} collective-permute-done((f32[88,128]{1,0:T(8,128)S(1)}, f32[88,128]{1,0:T(8,128)S(1)}, u32[]{:S(2)}, u32[]{:S(2)}) %collective-permute-start.6) | collective-permute-done | bytes 45088 | tf_op jit(solution)/shard_map/ppermute | solution.py:48
  64.1 0.6 pad_maximum_fusion.1
  (11 shorter events, 0.1 us)
Async XLA Ops:
  0.6 16.2 %copy-start = (f32[88,256]{1,0:T(8,128)S(1)}, f32[88,256]{1,0:T(8,128)}, u32[]{:S(2)}) copy-start(f32[88,256]{1,0:T(8,128)} %param.10) | copy-start | bytes 270340
  0.6 16.3 %copy-start.5 = (f32[88,9]{0,1:T(8,128)S(1)}, f32[88,9]{0,1:T(8,128)}, u32[]{:S(2)}) copy-start(f32[88,9]{0,1:T(8,128)} %param.11) | copy-start | bytes 9508
  0.6 16.3 %copy-start.4 = (s32[9,256]{1,0:T(8,128)S(1)}, s32[9,256]{1,0:T(8,128)}, u32[]{:S(2)}) copy-start(s32[9,256]{1,0:T(8,128)} %param.13) | copy-start | bytes 27652
  0.7 16.1 %collective-permute-start = (f32[88,256]{1,0:T(8,128)}, f32[88,256]{1,0:T(8,128)S(1)}, u32[]{:S(2)}, u32[]{:S(2)}) collective-permute-start(f32[88,256]{1,0:T(8,128)} %param.10), channel_id=1, source_target_pairs={{0,8},{8,16},{16,24},{24,32},{32,40},{40,48},{48,56},{56,64},{64,7... | collective-permute-start | bytes 270344 | tf_op jit(solution)/shard_map/ppermute | solution.py:48
  4.8 12.0 %collective-permute-start.1 = (f32[88,256]{1,0:T(8,128)}, f32[88,256]{1,0:T(8,128)S(1)}, u32[]{:S(2)}, u32[]{:S(2)}) collective-permute-start(f32[88,256]{1,0:T(8,128)} %param.10), channel_id=1, source_target_pairs={{0,504},{8,0},{16,8},{24,16},{32,24},{40,32},{48,40},{56,48},{64,5... | collective-permute-start | bytes 270344 | tf_op jit(solution)/shard_map/ppermute | solution.py:48
  16.9 2.7 %copy-start.1 = (f32[2048]{0:T(1024)S(1)}, f32[2048]{0:T(1024)}, u32[]{:S(2)}) copy-start(f32[2048]{0:T(1024)} %param.17) | copy-start | bytes 24580
  16.9 2.7 %copy-start.2 = (s32[2048]{0:T(1024)S(1)}, s32[2048]{0:T(1024)}, u32[]{:S(2)}) copy-start(s32[2048]{0:T(1024)} %param.14) | copy-start | bytes 24580
  16.9 2.7 %copy-start.8 = (f32[88]{0:T(128)S(1)}, f32[88]{0:T(128)}, u32[]{:S(2)}) copy-start(f32[88]{0:T(128)} %param.12) | copy-start | bytes 1060
  19.6 26.4 %copy-start.6 = (f32[2048]{0:T(1024)S(1)}, f32[2048]{0:T(1024)}, u32[]{:S(2)}) copy-start(f32[2048]{0:T(1024)} %param.19) | copy-start | bytes 24580
  19.6 26.4 %copy-start.7 = (f32[2048]{0:T(1024)S(1)}, f32[2048]{0:T(1024)}, u32[]{:S(2)}) copy-start(f32[2048]{0:T(1024)} %param.18) | copy-start | bytes 24580
  28.3 9.2 %collective-permute-start.2 = (f32[2048]{0:T(1024)S(1)}, f32[2048]{0:T(1024)S(1)}, u32[]{:S(2)}, u32[]{:S(2)}) collective-permute-start(f32[2048]{0:T(1024)S(1)} %psum.7), channel_id=1, source_target_pairs={{0,6},{2,0},{4,2},{6,4},{1,7},{3,1},{5,3},{7,5},{8,14},{10,8},{12,... | collective-permute-start | bytes 24584 | tf_op jit(solution)/shard_map/ppermute | solution.py:48
  35.4 9.3 %collective-permute-start.4 = (f32[2048]{0:T(1024)S(1)}, f32[2048]{0:T(1024)S(1)}, u32[]{:S(2)}, u32[]{:S(2)}) collective-permute-start(f32[2048]{0:T(1024)S(1)} %psum.7), channel_id=1, source_target_pairs={{0,2},{2,4},{4,6},{6,0},{1,3},{3,5},{5,7},{7,1},{8,10},{10,12},{12... | collective-permute-start | bytes 24584 | tf_op jit(solution)/shard_map/ppermute | solution.py:48
  37.5 8.3 %collective-permute-start.3 = (f32[2048]{0:T(1024)S(1)}, f32[2048]{0:T(1024)S(1)}, u32[]{:S(2)}, u32[]{:S(2)}) collective-permute-start(f32[2048]{0:T(1024)S(1)} %collective-permute-done.2), channel_id=1, source_target_pairs={{0,6},{2,0},{4,2},{6,4},{1,7},{3,1},{5,3},{7,5},{8,14},{10,8},{12,... | collective-permute-start | bytes 24584 | tf_op jit(solution)/shard_map/ppermute | solution.py:48
  46.0 5.1 %copy-start.3 = (f32[2048]{0:T(1024)}, f32[2048]{0:T(1024)S(1)}, u32[]{:S(2)}) copy-start(f32[2048]{0:T(1024)S(1)} %dynamic-slice_reduce_fusion) | copy-start | bytes 24580
  51.1 11.9 %collective-permute-start.5 = (f32[88,128]{1,0:T(8,128)S(1)}, f32[88,128]{1,0:T(8,128)S(1)}, u32[]{:S(2)}, u32[]{:S(2)}) collective-permute-start(f32[88,128]{1,0:T(8,128)S(1)} %get-tuple-element.4), channel_id=1, source_target_pairs={{0,8},{8,16},{16,24},{24,32},{32,40},{40,48},{48,56},{56,64},{64,7... | collective-permute-start | bytes 135176 | tf_op jit(solution)/shard_map/ppermute | solution.py:48
  53.1 11.1 %collective-permute-start.6 = (f32[88,128]{1,0:T(8,128)S(1)}, f32[88,128]{1,0:T(8,128)S(1)}, u32[]{:S(2)}, u32[]{:S(2)}) collective-permute-start(f32[88,128]{1,0:T(8,128)S(1)} %get-tuple-element.5), channel_id=1, source_target_pairs={{0,504},{8,0},{16,8},{24,16},{32,24},{40,32},{48,40},{56,48},{64,5... | collective-permute-start | bytes 135176 | tf_op jit(solution)/shard_map/ppermute | solution.py:48

commit v15 on v13

--- a/solution.py
+++ b/solution.py
@@ -98,14 +98,16 @@
     sensitivity = adjoint_sum * weighted
 
     terms = stencil[:, :, None] * sensitivity[:, None, :]
-    framed = spread_select(terms, pick)
-    to_after, to_before = lax.optimization_barrier((framed[:, frame - COLS :], framed[:, :COLS]))
+    edge_id = lax.broadcasted_iota(jnp.int32, (2 * COLS, taps, pixels), 0)
+    edge_id = edge_id + jnp.where(edge_id >= COLS, frame - 2 * COLS, 0)
+    edges = spread_select(terms, (edge_id == neighbours[None]).astype(jnp.bfloat16))
+    to_after, to_before = lax.optimization_barrier((edges[:, COLS:], edges[:, :COLS]))
     from_before = ring(to_after, "ang", 1)
     from_after = ring(to_before, "ang", -1)
-    inner = framed[:, COLS : frame - COLS]
-    gradient = jnp.concatenate(
-        [inner[:, :COLS] + from_before, inner[:, COLS : pixels - COLS], inner[:, pixels - COLS :] + from_after],
-        axis=1,
+    own_id = COLS + lax.broadcasted_iota(jnp.int32, (pixels, taps, pixels), 0)
+    inner = spread_select(terms, (own_id == neighbours[None]).astype(jnp.bfloat16))
+    gradient = inner + jnp.pad(from_before, ((0, 0), (0, pixels - COLS))) + jnp.pad(
+        from_after, ((0, 0), (pixels - COLS, 0))
     )
     return (predicted, gradient)
 

time: 63 us -> 62.2 us (0.987)
  waiting for transfers between devices: 2.31 us -> 1.64 us
    ppermute x7, waiting for transfers between devices: 2.31 us -> 1.64 us  [ring(): lax.ppermute(value, axis, [(i, (i + step) % count) for i in range(count)])]
    add x1 -> x3, other arithmetic: 0.02 us -> 0.67 us  [the longest x1 0.66 us: on_device(): inner + jnp.pad(from_before, ((0, 0), (0, pixels - COLS)))]
    concatenate x1 -> x0, other arithmetic: 0.64 us -> none  [on_device(): jnp.concatenate([inner[:, :COLS] + from_before, inner[:, COLS:pixels - CO...]
    dot_general x1 -> x2, matrix products: 0.99 us -> 1.29 us  [spread_select(): lax.dot_general(split3(value), onehot, (((1, 2), (1, 2)), ((), ())), pref...]
  transfers between devices with their start and end apart: 7 -> 7, of which waited for: 2 -> 2; matrix products, arithmetic and copies ran while one was open for 4% -> 5% of each run, Pallas kernels for 0% -> 0%
where the time goes in v15:
time: 62.2 us; the launch traced here: 61.3 us
  starting transfers between devices  41.9 us (67%)
  blocking collectives  7.3 us (12%)
  matrix products  5.82 us (9%)
  other arithmetic  3.48 us (6%)
  waiting for transfers between devices  1.64 us (3%)
  between operations  1.02 us (2%)
    ppermute x7, starting transfers between devices, ring(): lax.ppermute(value, axis, [(i, (i + step) % count) for i in range(count)])  41.9 us
    psum x1, blocking collectives, on_device(): pair = lax.psum(partial_value, 'core')  7.3 us
    reduce_sum x1, other arithmetic, on_device(): jnp.sum(jnp.where(pixel_id[None] == star_pixels[:, None, :], star_weights...  2.28 us
    dot_general x1, matrix products, on_device(): lax.dot_general(radial * weight_back[None, :], spread, (((1,), (1,)), (()...  2.06 us
    ppermute x7, waiting for transfers between devices, ring(): lax.ppermute(value, axis, [(i, (i + step) % count) for i in range(count)])  1.64 us
    dot_general x1, matrix products, on_device(): jnp.dot(weighted, spread, precision=HIGHEST, preferred_element_type=jnp.f...  1.4 us
    dot_general x2, matrix products, spread_select(): lax.dot_general(split3(value), onehot, (((1, 2), (1, 2)), ((), ())), pref...  1.29 us
  transfers between devices with their start and end apart: 7, of which 2 were waited for; matrix products, arithmetic and copies ran while one was open for 5% of the time, Pallas kernels for 0%

profile of v15, /device:TPU:1, one launch (start us, length us, event | category | flops | bytes accessed | tf_op | source)
XLA Modules:
  0.0 61.3 jit_solution(14532549627908154814)
XLA Ops:
  0.6 0.0 copy-start
  0.6 0.0 copy-start.8
  0.7 4.2 %collective-permute-start = (f32[88,256]{1,0:T(8,128)}, f32[88,256]{1,0:T(8,128)S(1)}, u32[]{:S(2)}, u32[]{:S(2)}) collective-permute-start(f32[88,256]{1,0:T(8,128)} %param.10), channel_id=1, source_target_pairs={{0,8},{8,16},{16,24},{24,32},{32,40},{40,48},{48,56},{56,64},{64,7... | collective-permute-start | bytes 270344 | tf_op jit(solution)/shard_map/ppermute | solution.py:46
  4.8 9.6 %collective-permute-start.1 = (f32[88,256]{1,0:T(8,128)}, f32[88,256]{1,0:T(8,128)S(1)}, u32[]{:S(2)}, u32[]{:S(2)}) collective-permute-start(f32[88,256]{1,0:T(8,128)} %param.10), channel_id=1, source_target_pairs={{0,504},{8,0},{16,8},{24,16},{32,24},{40,32},{48,40},{56,48},{64,5... | collective-permute-start | bytes 270344 | tf_op jit(solution)/shard_map/ppermute | solution.py:46
  14.5 2.3 %select_reduce_fusion = f32[256,2048]{1,0:T(8,128)S(1)} fusion(f32[4,2048]{1,0:T(4,128)} %param.16, s32[4,2048]{1,0:T(4,128)} %param.15), kind=kLoop, calls=%fused_computation | loop fusion | flops 5767168 | bytes 2162688 | tf_op jit(solution)/shard_map/reduce_sum | solution.py:78
  16.7 0.0 copy-start.3
  16.8 0.0 collective-permute-done
  16.8 0.0 collective-permute-done.1
  16.8 0.0 copy-done
  16.9 0.0 copy-done.8
  16.9 0.0 copy-start.1
  16.9 0.0 copy-start.2
  16.9 0.0 copy-start.7
  16.9 1.1 %fusion = f32[264,9,256]{2,0,1:T(8,128)S(1)} fusion(s32[9,256]{1,0:T(8,128)S(1)} %copy-done.8, bf16[88,512]{1,0:T(8,128)(2,1)S(1)} %get-tuple-element.8, bf16[88,512]{1,0:T(8,128)(2,1)S(1)} %get-tuple-element.7, bf16[88,512]{1,0:T(8,128)(2,1)S(1)} %get-tuple-element.6), kind=kOutput, calls=%fused_computation.3 | convolution fusion | flops 624844800 | bytes 2712576 | tf_op jit(solution)/shard_map/dot_general | solution.py:20
  18.0 0.0 copy-done.3
  18.0 0.0 copy-start.5
  18.0 0.0 copy-start.6
  18.0 0.2 fusion.19
  18.2 0.0 copy-done.1
  18.2 0.0 copy-done.2
  18.2 0.0 copy-done.7
  18.2 1.4 %fusion.6 = f32[2048]{0:T(1024)S(1)} fusion(f32[256,2048]{1,0:T(8,128)S(1)} %select_reduce_fusion, f32[2048]{0:T(1024)S(1)} %copy-done.1, s32[2048]{0:T(1024)S(1)} %copy-done.2, s32[88]{0:T(128)S(1)} %get-tuple-element.15, s32[88]{0:T(128)S(1)} %get-tuple-element.14, f32[88,256]{1,0:T(8,128)S(1)} %fusion.19, f32[88]{0:T(128)S(1)} %copy-done.7), kind=kOutput, calls=%fused_computation.11 | convolution fusion | flops 554749952 | bytes 2212896 | tf_op jit(solution)/shard_map/dot_general | solution.py:85
  19.6 7.3 %psum.7 = f32[2048]{0:T(1024)S(1)} all-reduce(f32[2048]{0:T(1024)S(1)} %fusion.6), channel_id=1, replica_groups=mesh['ang'=64,'zhi'=4,'core'=2] {'core'}, use_global_device_ids=true, to_apply=%region_3.4 | all-reduce | flops 2048 | bytes 16384 | tf_op jit(solution)/shard_map/psum | solution.py:87
  26.9 7.1 %collective-permute-start.2 = (f32[2048]{0:T(1024)S(1)}, f32[2048]{0:T(1024)S(1)}, u32[]{:S(2)}, u32[]{:S(2)}) collective-permute-start(f32[2048]{0:T(1024)S(1)} %psum.7), channel_id=1, source_target_pairs={{0,6},{2,0},{4,2},{6,4},{1,7},{3,1},{5,3},{7,5},{8,14},{10,8},{12,... | collective-permute-start | bytes 24584 | tf_op jit(solution)/shard_map/ppermute | solution.py:46
  34.0 2.1 %collective-permute-start.4 = (f32[2048]{0:T(1024)S(1)}, f32[2048]{0:T(1024)S(1)}, u32[]{:S(2)}, u32[]{:S(2)}) collective-permute-start(f32[2048]{0:T(1024)S(1)} %psum.7), channel_id=1, source_target_pairs={{0,2},{2,4},{4,6},{6,0},{1,3},{3,5},{5,7},{7,1},{8,10},{10,12},{12... | collective-permute-start | bytes 24584 | tf_op jit(solution)/shard_map/ppermute | solution.py:46
  36.2 0.0 collective-permute-done.2
  36.2 7.1 %collective-permute-start.3 = (f32[2048]{0:T(1024)S(1)}, f32[2048]{0:T(1024)S(1)}, u32[]{:S(2)}, u32[]{:S(2)}) collective-permute-start(f32[2048]{0:T(1024)S(1)} %collective-permute-done.2), channel_id=1, source_target_pairs={{0,6},{2,0},{4,2},{6,4},{1,7},{3,1},{5,3},{7,5},{8,14},{10,8},{12,... | collective-permute-start | bytes 24584 | tf_op jit(solution)/shard_map/ppermute | solution.py:46
  43.3 0.0 collective-permute-done.4
  43.3 1.2 %collective-permute-done.3 = f32[2048]{0:T(1024)S(1)} collective-permute-done((f32[2048]{0:T(1024)S(1)}, f32[2048]{0:T(1024)S(1)}, u32[]{:S(2)}, u32[]{:S(2)}) %collective-permute-start.3) | collective-permute-done | bytes 8224 | tf_op jit(solution)/shard_map/ppermute | solution.py:46
  44.5 0.1 concatenate.19
  44.6 0.0 copy-done.5
  44.6 0.0 copy-done.6
  44.6 0.0 copy-start.4
  44.7 2.1 %convolution_multiply_fusion.1 = f32[88,256]{1,0:T(8,128)S(1)} fusion(f32[256,2048]{1,0:T(8,128)S(1)} %select_reduce_fusion, f32[2048]{0:T(1024)S(1)} %multiply_divide_fusion, f32[2048]{0:T(1024)S(1)} %copy-done.1, s32[2048]{0:T(1024)S(1)} %copy-done.2, s32[88]{0:T(128)S(1)} %get-tuple-element.15, s32[88]{0:T(128)S(1)} %get-tuple-element.14, ...), kind=kOutput, calls=%fused_computation.22 | convolution fusion | flops 554594304 | bytes 2303008 | tf_op jit(solution)/shard_map/dot_general | solution.py:91
  46.7 0.2 reduce-precision_convert_fusion.1
  47.0 0.6 %fusion.14 = f32[264,256]{1,0:T(8,128)S(1)} fusion(s32[9,256]{1,0:T(8,128)S(1)} %copy-done.8, s32[256]{0:T(256)S(1)} %fusion.38, bf16[88,9,256]{2,0,1:T(8,128)(2,1)S(1)} %get-tuple-element.11, bf16[88,9,256]{2,0,1:T(8,128)(2,1)S(1)} %get-tuple-element.10, bf16[88,9,256]{2,0,1:T(8,128)(2,1)S(1)} %get-tuple-element.9), kind=kOutput, calls=%fused_computation.17 | convolution fusion | flops 315666432 | bytes 1497088 | tf_op jit(solution)/shard_map/dot_general | solution.py:26
  47.6 0.0 copy-done.4
  47.7 1.9 %collective-permute-start.5 = (f32[88,128]{1,0:T(8,128)S(1)}, f32[88,128]{1,0:T(8,128)S(1)}, u32[]{:S(2)}, u32[]{:S(2)}) collective-permute-start(f32[88,128]{1,0:T(8,128)S(1)} %get-tuple-element.4), channel_id=1, source_target_pairs={{0,8},{8,16},{16,24},{24,32},{32,40},{40,48},{48,56},{56,64},{64,7... | collective-permute-start | bytes 135176 | tf_op jit(solution)/shard_map/ppermute | solution.py:46
  49.6 9.9 %collective-permute-start.6 = (f32[88,128]{1,0:T(8,128)S(1)}, f32[88,128]{1,0:T(8,128)S(1)}, u32[]{:S(2)}, u32[]{:S(2)}) collective-permute-start(f32[88,128]{1,0:T(8,128)S(1)} %get-tuple-element.5), channel_id=1, source_target_pairs={{0,504},{8,0},{16,8},{24,16},{32,24},{40,32},{48,40},{56,48},{64,5... | collective-permute-start | bytes 135176 | tf_op jit(solution)/shard_map/ppermute | solution.py:46
  59.6 0.6 %fusion.11 = f32[264,256]{1,0:T(8,128)S(1)} fusion(s32[9,256]{1,0:T(8,128)S(1)} %copy-done.8, s32[256]{0:T(256)S(1)} %iota_add_fusion, bf16[88,9,256]{2,0,1:T(8,128)(2,1)S(1)} %get-tuple-element.11, bf16[88,9,256]{2,0,1:T(8,128)(2,1)S(1)} %get-tuple-element.10, bf16[88,9,256]{2,0,1:T(8,128)(2,1)S(1)} %get-tuple-element.9), kind=kOutput, calls=%fused_computation.16 | convolution fusion | flops 315666432 | bytes 1497088 | tf_op jit(solution)/shard_map/dot_general | solution.py:26
  60.2 0.0 collective-permute-done.5
  60.2 0.5 collective-permute-done.6
  60.7 0.7 %fusion.36 = f32[88,256]{1,0:T(8,128)} fusion(f32[264,256]{1,0:T(8,128)S(1)} %fusion.11, f32[88,128]{1,0:T(8,128)S(1)} %collective-permute-done.6, f32[88,128]{1,0:T(8,128)S(1)} %collective-permute-done.5), kind=kLoop, calls=%fused_computation.54 | loop fusion | flops 90112 | bytes 450560 | tf_op jit(solution)/shard_map/add | solution.py:109
  (10 shorter events, 0.1 us)
Async XLA Ops:
  0.6 16.2 %copy-start = (f32[88,256]{1,0:T(8,128)S(1)}, f32[88,256]{1,0:T(8,128)}, u32[]{:S(2)}) copy-start(f32[88,256]{1,0:T(8,128)} %param.10) | copy-start | bytes 270340
  0.6 16.2 %copy-start.8 = (s32[9,256]{1,0:T(8,128)S(1)}, s32[9,256]{1,0:T(8,128)}, u32[]{:S(2)}) copy-start(s32[9,256]{1,0:T(8,128)} %param.13) | copy-start | bytes 27652
  0.7 16.1 %collective-permute-start = (f32[88,256]{1,0:T(8,128)}, f32[88,256]{1,0:T(8,128)S(1)}, u32[]{:S(2)}, u32[]{:S(2)}) collective-permute-start(f32[88,256]{1,0:T(8,128)} %param.10), channel_id=1, source_target_pairs={{0,8},{8,16},{16,24},{24,32},{32,40},{40,48},{48,56},{56,64},{64,7... | collective-permute-start | bytes 270344 | tf_op jit(solution)/shard_map/ppermute | solution.py:46
  4.8 12.0 %collective-permute-start.1 = (f32[88,256]{1,0:T(8,128)}, f32[88,256]{1,0:T(8,128)S(1)}, u32[]{:S(2)}, u32[]{:S(2)}) collective-permute-start(f32[88,256]{1,0:T(8,128)} %param.10), channel_id=1, source_target_pairs={{0,504},{8,0},{16,8},{24,16},{32,24},{40,32},{48,40},{56,48},{64,5... | collective-permute-start | bytes 270344 | tf_op jit(solution)/shard_map/ppermute | solution.py:46
  16.7 1.3 %copy-start.3 = (f32[88,9]{0,1:T(8,128)S(1)}, f32[88,9]{0,1:T(8,128)}, u32[]{:S(2)}) copy-start(f32[88,9]{0,1:T(8,128)} %param.11) | copy-start | bytes 9508
  16.9 1.3 %copy-start.1 = (f32[2048]{0:T(1024)S(1)}, f32[2048]{0:T(1024)}, u32[]{:S(2)}) copy-start(f32[2048]{0:T(1024)} %param.17) | copy-start | bytes 24580
  16.9 1.3 %copy-start.2 = (s32[2048]{0:T(1024)S(1)}, s32[2048]{0:T(1024)}, u32[]{:S(2)}) copy-start(s32[2048]{0:T(1024)} %param.14) | copy-start | bytes 24580
  16.9 1.3 %copy-start.7 = (f32[88]{0:T(128)S(1)}, f32[88]{0:T(128)}, u32[]{:S(2)}) copy-start(f32[88]{0:T(128)} %param.12) | copy-start | bytes 1060
  18.0 26.6 %copy-start.5 = (f32[2048]{0:T(1024)S(1)}, f32[2048]{0:T(1024)}, u32[]{:S(2)}) copy-start(f32[2048]{0:T(1024)} %param.19) | copy-start | bytes 24580
  18.0 26.6 %copy-start.6 = (f32[2048]{0:T(1024)S(1)}, f32[2048]{0:T(1024)}, u32[]{:S(2)}) copy-start(f32[2048]{0:T(1024)} %param.18) | copy-start | bytes 24580
  26.9 9.2 %collective-permute-start.2 = (f32[2048]{0:T(1024)S(1)}, f32[2048]{0:T(1024)S(1)}, u32[]{:S(2)}, u32[]{:S(2)}) collective-permute-start(f32[2048]{0:T(1024)S(1)} %psum.7), channel_id=1, source_target_pairs={{0,6},{2,0},{4,2},{6,4},{1,7},{3,1},{5,3},{7,5},{8,14},{10,8},{12,... | collective-permute-start | bytes 24584 | tf_op jit(solution)/shard_map/ppermute | solution.py:46
  34.0 9.2 %collective-permute-start.4 = (f32[2048]{0:T(1024)S(1)}, f32[2048]{0:T(1024)S(1)}, u32[]{:S(2)}, u32[]{:S(2)}) collective-permute-start(f32[2048]{0:T(1024)S(1)} %psum.7), channel_id=1, source_target_pairs={{0,2},{2,4},{4,6},{6,0},{1,3},{3,5},{5,7},{7,1},{8,10},{10,12},{12... | collective-permute-start | bytes 24584 | tf_op jit(solution)/shard_map/ppermute | solution.py:46
  36.2 8.3 %collective-permute-start.3 = (f32[2048]{0:T(1024)S(1)}, f32[2048]{0:T(1024)S(1)}, u32[]{:S(2)}, u32[]{:S(2)}) collective-permute-start(f32[2048]{0:T(1024)S(1)} %collective-permute-done.2), channel_id=1, source_target_pairs={{0,6},{2,0},{4,2},{6,4},{1,7},{3,1},{5,3},{7,5},{8,14},{10,8},{12,... | collective-permute-start | bytes 24584 | tf_op jit(solution)/shard_map/ppermute | solution.py:46
  44.6 3.0 %copy-start.4 = (f32[2048]{0:T(1024)}, f32[2048]{0:T(1024)S(1)}, u32[]{:S(2)}) copy-start(f32[2048]{0:T(1024)S(1)} %dynamic-slice_reduce_fusion) | copy-start | bytes 24580
  47.7 12.5 %collective-permute-start.5 = (f32[88,128]{1,0:T(8,128)S(1)}, f32[88,128]{1,0:T(8,128)S(1)}, u32[]{:S(2)}, u32[]{:S(2)}) collective-permute-start(f32[88,128]{1,0:T(8,128)S(1)} %get-tuple-element.4), channel_id=1, source_target_pairs={{0,8},{8,16},{16,24},{24,32},{32,40},{40,48},{48,56},{56,64},{64,7... | collective-permute-start | bytes 135176 | tf_op jit(solution)/shard_map/ppermute | solution.py:46
  49.6 11.1 %collective-permute-start.6 = (f32[88,128]{1,0:T(8,128)S(1)}, f32[88,128]{1,0:T(8,128)S(1)}, u32[]{:S(2)}, u32[]{:S(2)}) collective-permute-start(f32[88,128]{1,0:T(8,128)S(1)} %get-tuple-element.5), channel_id=1, source_target_pairs={{0,504},{8,0},{16,8},{24,16},{32,24},{40,32},{48,40},{56,48},{64,5... | collective-permute-start | bytes 135176 | tf_op jit(solution)/shard_map/ppermute | solution.py:46

commit v16 on v15

--- a/solution.py
+++ b/solution.py
@@ -27,18 +27,6 @@
         split3(value), onehot, (((1, 2), (1, 2)), ((), ())), preferred_element_type=jnp.float32
     )
     return product[:rows] + product[rows : 2 * rows] + product[2 * rows :]
-
-
-def chip_sum(value, axis):
-    count = lax.axis_size(axis)
-    if count != 4:
-        return jnp.sum(lax.all_gather(value, axis), axis=0)
-    from_next = ring(value, axis, -1)
-    from_prev = ring(value, axis, 1)
-    opposite = ring(from_next, axis, -1)
-    relative = jnp.stack([value, from_next, opposite, from_prev])
-    ordered = jnp.roll(relative, lax.axis_index(axis), axis=0)
-    return jnp.sum(ordered, axis=0)
 
 
 def ring(value, axis, step):
@@ -85,7 +73,7 @@
     at_stars = jnp.dot(weighted, spread, precision=HIGHEST, preferred_element_type=jnp.float32)
     partial_value = jnp.sum(radial * at_stars, axis=0)
     pair = lax.psum(partial_value, "core")
-    predicted = chip_sum(pair, "zhi")
+    predicted = jnp.sum(lax.all_gather(pair, "zhi"), axis=0)
     weight_back = (predicted - observed) / (sigma * sigma)
 
     adjoint_sum = lax.dot_general(

time: 62.2 us -> 63.2 us (1.016)
  the two profiles are of different devices: /device:TPU:1 before, /device:TPU:126 now
where the time goes in v16:
time: 63.2 us; the launch traced here: 62.9 us
  blocking collectives  22.9 us (36%)
  waiting for transfers between devices  15.7 us (25%)
  starting transfers between devices  13.9 us (22%)
  matrix products  5.81 us (9%)
  other arithmetic  3.48 us (6%)
  between operations  0.94 us (1%)
    all_gather x1, blocking collectives, on_device(): predicted = jnp.sum(lax.all_gather(pair, 'zhi'), axis=0)  20.4 us
    ppermute x4, waiting for transfers between devices, ring(): lax.ppermute(value, axis, [(i, (i + step) % count) for i in range(count)])  15.7 us
    ppermute x4, starting transfers between devices, ring(): lax.ppermute(value, axis, [(i, (i + step) % count) for i in range(count)])  13.9 us
    psum x1, blocking collectives, on_device(): pair = lax.psum(partial_value, 'core')  2.5 us
    reduce_sum x1, other arithmetic, on_device(): jnp.sum(jnp.where(pixel_id[None] == star_pixels[:, None, :], star_weights...  2.29 us
    dot_general x1, matrix products, on_device(): lax.dot_general(radial * weight_back[None, :], spread, (((1,), (1,)), (()...  2.06 us
    dot_general x1, matrix products, on_device(): jnp.dot(weighted, spread, precision=HIGHEST, preferred_element_type=jnp.f...  1.4 us
    dot_general x2, matrix products, spread_select(): lax.dot_general(split3(value), onehot, (((1, 2), (1, 2)), ((), ())), pref...  1.29 us
  transfers between devices with their start and end apart: 4, of which 2 were waited for; matrix products, arithmetic and copies ran while one was open for 5% of the time, Pallas kernels for 0%

profile of v16, /device:TPU:126, one launch (start us, length us, event | category | flops | bytes accessed | tf_op | source)
XLA Modules:
  0.0 62.9 jit_solution(13293328526380740197)
XLA Ops:
  0.6 0.0 copy-start
  0.6 0.0 copy-start.8
  0.6 6.2 %collective-permute-start = (f32[88,256]{1,0:T(8,128)}, f32[88,256]{1,0:T(8,128)S(1)}, u32[]{:S(2)}, u32[]{:S(2)}) collective-permute-start(f32[88,256]{1,0:T(8,128)} %param.10), channel_id=1, source_target_pairs={{0,8},{8,16},{16,24},{24,32},{32,40},{40,48},{48,56},{56,64},{64,7... | collective-permute-start | bytes 270344 | tf_op jit(solution)/shard_map/ppermute | solution.py:34
  6.8 1.9 %collective-permute-start.1 = (f32[88,256]{1,0:T(8,128)}, f32[88,256]{1,0:T(8,128)S(1)}, u32[]{:S(2)}, u32[]{:S(2)}) collective-permute-start(f32[88,256]{1,0:T(8,128)} %param.10), channel_id=1, source_target_pairs={{0,504},{8,0},{16,8},{24,16},{32,24},{40,32},{48,40},{56,48},{64,5... | collective-permute-start | bytes 270344 | tf_op jit(solution)/shard_map/ppermute | solution.py:34
  8.8 2.3 %select_reduce_fusion = f32[256,2048]{1,0:T(8,128)S(1)} fusion(f32[4,2048]{1,0:T(4,128)} %param.16, s32[4,2048]{1,0:T(4,128)} %param.15), kind=kLoop, calls=%fused_computation | loop fusion | flops 5767168 | bytes 2162688 | tf_op jit(solution)/shard_map/reduce_sum | solution.py:66
  11.1 0.0 copy-start.3
  11.1 0.0 collective-permute-done
  11.1 8.3 %collective-permute-done.1 = f32[88,256]{1,0:T(8,128)S(1)} collective-permute-done((f32[88,256]{1,0:T(8,128)}, f32[88,256]{1,0:T(8,128)S(1)}, u32[]{:S(2)}, u32[]{:S(2)}) %collective-permute-start.1) | collective-permute-done | bytes 90144 | tf_op jit(solution)/shard_map/ppermute | solution.py:34
  19.5 0.0 copy-done
  19.5 0.0 copy-done.8
  19.6 0.0 copy-start.1
  19.6 0.0 copy-start.2
  19.6 0.0 copy-start.7
  19.6 1.1 %fusion = f32[264,9,256]{2,0,1:T(8,128)S(1)} fusion(s32[9,256]{1,0:T(8,128)S(1)} %copy-done.8, bf16[88,512]{1,0:T(8,128)(2,1)S(1)} %get-tuple-element.8, bf16[88,512]{1,0:T(8,128)(2,1)S(1)} %get-tuple-element.7, bf16[88,512]{1,0:T(8,128)(2,1)S(1)} %get-tuple-element.6), kind=kOutput, calls=%fused_computation.3 | convolution fusion | flops 624844800 | bytes 2712576 | tf_op jit(solution)/shard_map/dot_general | solution.py:20
  20.7 0.0 copy-done.3
  20.7 0.0 copy-start.5
  20.7 0.0 copy-start.6
  20.7 0.2 fusion.19
  20.9 0.0 copy-done.1
  20.9 0.0 copy-done.2
  20.9 0.0 copy-done.7
  20.9 1.4 %fusion.6 = f32[2048]{0:T(1024)S(1)} fusion(f32[256,2048]{1,0:T(8,128)S(1)} %select_reduce_fusion, f32[2048]{0:T(1024)S(1)} %copy-done.1, s32[2048]{0:T(1024)S(1)} %copy-done.2, s32[88]{0:T(128)S(1)} %get-tuple-element.15, s32[88]{0:T(128)S(1)} %get-tuple-element.14, f32[88,256]{1,0:T(8,128)S(1)} %fusion.19, f32[88]{0:T(128)S(1)} %copy-done.7), kind=kOutput, calls=%fused_computation.11 | convolution fusion | flops 554749952 | bytes 2212896 | tf_op jit(solution)/shard_map/dot_general | solution.py:73
  22.3 2.5 %psum.7 = f32[1,2048]{1,0:T(1,128)S(1)} all-reduce(f32[1,2048]{1,0:T(1,128)S(1)} %bitcast.11), channel_id=1, replica_groups=mesh['ang'=64,'zhi'=4,'core'=2] {'core'}, use_global_device_ids=true, to_apply=%region_3.4 | all-reduce | flops 2048 | bytes 16384 | tf_op jit(solution)/shard_map/psum | solution.py:75
  24.8 20.4 %all-gather = f32[4,1,2048]{2,1,0:T(1,128)S(1)} all-gather(f32[1,1,2048]{2,1,0:T(1,128)S(1)} %bitcast.12), channel_id=1, replica_groups=mesh['ang'=64,'zhi'=4,'core'=2] {'zhi'}, dimensions={0}, use_global_device_ids=true | all-gather | bytes 40960 | tf_op jit(solution)/shard_map/all_gather | solution.py:76
  45.3 0.0 copy-done.5
  45.3 0.0 copy-done.6
  45.3 0.0 copy-start.4
  45.3 2.1 %convolution_multiply_fusion.1 = f32[88,256]{1,0:T(8,128)S(1)} fusion(f32[256,2048]{1,0:T(8,128)S(1)} %select_reduce_fusion, f32[2048]{0:T(1024)S(1)} %multiply_divide_fusion, f32[2048]{0:T(1024)S(1)} %copy-done.1, s32[2048]{0:T(1024)S(1)} %copy-done.2, s32[88]{0:T(128)S(1)} %get-tuple-element.15, s32[88]{0:T(128)S(1)} %get-tuple-element.14, ...), kind=kOutput, calls=%fused_computation.22 | convolution fusion | flops 554594304 | bytes 2303008 | tf_op jit(solution)/shard_map/dot_general | solution.py:79
  47.4 0.2 reduce-precision_convert_fusion.1
  47.6 0.6 %fusion.14 = f32[264,256]{1,0:T(8,128)S(1)} fusion(s32[9,256]{1,0:T(8,128)S(1)} %copy-done.8, s32[256]{0:T(256)S(1)} %fusion.38, bf16[88,9,256]{2,0,1:T(8,128)(2,1)S(1)} %get-tuple-element.11, bf16[88,9,256]{2,0,1:T(8,128)(2,1)S(1)} %get-tuple-element.10, bf16[88,9,256]{2,0,1:T(8,128)(2,1)S(1)} %get-tuple-element.9), kind=kOutput, calls=%fused_computation.17 | convolution fusion | flops 315666432 | bytes 1497088 | tf_op jit(solution)/shard_map/dot_general | solution.py:26
  48.3 0.0 copy-done.4
  48.3 1.9 %collective-permute-start.2 = (f32[88,128]{1,0:T(8,128)S(1)}, f32[88,128]{1,0:T(8,128)S(1)}, u32[]{:S(2)}, u32[]{:S(2)}) collective-permute-start(f32[88,128]{1,0:T(8,128)S(1)} %get-tuple-element.4), channel_id=1, source_target_pairs={{0,8},{8,16},{16,24},{24,32},{32,40},{40,48},{48,56},{56,64},{64,7... | collective-permute-start | bytes 135176 | tf_op jit(solution)/shard_map/ppermute | solution.py:34
  50.3 3.9 %collective-permute-start.3 = (f32[88,128]{1,0:T(8,128)S(1)}, f32[88,128]{1,0:T(8,128)S(1)}, u32[]{:S(2)}, u32[]{:S(2)}) collective-permute-start(f32[88,128]{1,0:T(8,128)S(1)} %get-tuple-element.5), channel_id=1, source_target_pairs={{0,504},{8,0},{16,8},{24,16},{32,24},{40,32},{48,40},{56,48},{64,5... | collective-permute-start | bytes 135176 | tf_op jit(solution)/shard_map/ppermute | solution.py:34
  54.2 0.6 %fusion.11 = f32[264,256]{1,0:T(8,128)S(1)} fusion(s32[9,256]{1,0:T(8,128)S(1)} %copy-done.8, s32[256]{0:T(256)S(1)} %iota_add_fusion, bf16[88,9,256]{2,0,1:T(8,128)(2,1)S(1)} %get-tuple-element.11, bf16[88,9,256]{2,0,1:T(8,128)(2,1)S(1)} %get-tuple-element.10, bf16[88,9,256]{2,0,1:T(8,128)(2,1)S(1)} %get-tuple-element.9), kind=kOutput, calls=%fused_computation.16 | convolution fusion | flops 315666432 | bytes 1497088 | tf_op jit(solution)/shard_map/dot_general | solution.py:26
  54.9 0.0 collective-permute-done.2
  54.9 7.4 %collective-permute-done.3 = f32[88,128]{1,0:T(8,128)S(1)} collective-permute-done((f32[88,128]{1,0:T(8,128)S(1)}, f32[88,128]{1,0:T(8,128)S(1)}, u32[]{:S(2)}, u32[]{:S(2)}) %collective-permute-start.3) | collective-permute-done | bytes 45088 | tf_op jit(solution)/shard_map/ppermute | solution.py:34
  62.2 0.7 %fusion.36 = f32[88,256]{1,0:T(8,128)} fusion(f32[264,256]{1,0:T(8,128)S(1)} %fusion.11, f32[88,128]{1,0:T(8,128)S(1)} %collective-permute-done.3, f32[88,128]{1,0:T(8,128)S(1)} %collective-permute-done.2), kind=kLoop, calls=%fused_computation.54 | loop fusion | flops 90112 | bytes 450560 | tf_op jit(solution)/shard_map/add | solution.py:97
  (10 shorter events, 0.1 us)
Async XLA Ops:
  0.6 18.9 %copy-start = (f32[88,256]{1,0:T(8,128)S(1)}, f32[88,256]{1,0:T(8,128)}, u32[]{:S(2)}) copy-start(f32[88,256]{1,0:T(8,128)} %param.10) | copy-start | bytes 270340
  0.6 18.9 %copy-start.8 = (s32[9,256]{1,0:T(8,128)S(1)}, s32[9,256]{1,0:T(8,128)}, u32[]{:S(2)}) copy-start(s32[9,256]{1,0:T(8,128)} %param.13) | copy-start | bytes 27652
  0.6 10.5 %collective-permute-start = (f32[88,256]{1,0:T(8,128)}, f32[88,256]{1,0:T(8,128)S(1)}, u32[]{:S(2)}, u32[]{:S(2)}) collective-permute-start(f32[88,256]{1,0:T(8,128)} %param.10), channel_id=1, source_target_pairs={{0,8},{8,16},{16,24},{24,32},{32,40},{40,48},{48,56},{56,64},{64,7... | collective-permute-start | bytes 270344 | tf_op jit(solution)/shard_map/ppermute | solution.py:34
  6.8 12.6 %collective-permute-start.1 = (f32[88,256]{1,0:T(8,128)}, f32[88,256]{1,0:T(8,128)S(1)}, u32[]{:S(2)}, u32[]{:S(2)}) collective-permute-start(f32[88,256]{1,0:T(8,128)} %param.10), channel_id=1, source_target_pairs={{0,504},{8,0},{16,8},{24,16},{32,24},{40,32},{48,40},{56,48},{64,5... | collective-permute-start | bytes 270344 | tf_op jit(solution)/shard_map/ppermute | solution.py:34
  11.1 9.6 %copy-start.3 = (f32[88,9]{0,1:T(8,128)S(1)}, f32[88,9]{0,1:T(8,128)}, u32[]{:S(2)}) copy-start(f32[88,9]{0,1:T(8,128)} %param.11) | copy-start | bytes 9508
  19.6 1.3 %copy-start.1 = (f32[2048]{0:T(1024)S(1)}, f32[2048]{0:T(1024)}, u32[]{:S(2)}) copy-start(f32[2048]{0:T(1024)} %param.17) | copy-start | bytes 24580
  19.6 1.3 %copy-start.2 = (s32[2048]{0:T(1024)S(1)}, s32[2048]{0:T(1024)}, u32[]{:S(2)}) copy-start(s32[2048]{0:T(1024)} %param.14) | copy-start | bytes 24580
  19.6 1.3 %copy-start.7 = (f32[88]{0:T(128)S(1)}, f32[88]{0:T(128)}, u32[]{:S(2)}) copy-start(f32[88]{0:T(128)} %param.12) | copy-start | bytes 1060
  20.7 24.6 %copy-start.5 = (f32[2048]{0:T(1024)S(1)}, f32[2048]{0:T(1024)}, u32[]{:S(2)}) copy-start(f32[2048]{0:T(1024)} %param.19) | copy-start | bytes 24580
  20.7 24.6 %copy-start.6 = (f32[2048]{0:T(1024)S(1)}, f32[2048]{0:T(1024)}, u32[]{:S(2)}) copy-start(f32[2048]{0:T(1024)} %param.18) | copy-start | bytes 24580
  45.3 3.0 %copy-start.4 = (f32[2048]{0:T(1024)}, f32[2048]{0:T(1024)S(1)}, u32[]{:S(2)}) copy-start(f32[2048]{0:T(1024)S(1)} %reduce_sum.39) | copy-start | bytes 24580
  48.3 6.5 %collective-permute-start.2 = (f32[88,128]{1,0:T(8,128)S(1)}, f32[88,128]{1,0:T(8,128)S(1)}, u32[]{:S(2)}, u32[]{:S(2)}) collective-permute-start(f32[88,128]{1,0:T(8,128)S(1)} %get-tuple-element.4), channel_id=1, source_target_pairs={{0,8},{8,16},{16,24},{24,32},{32,40},{40,48},{48,56},{56,64},{64,7... | collective-permute-start | bytes 135176 | tf_op jit(solution)/shard_map/ppermute | solution.py:34
  50.3 12.0 %collective-permute-start.3 = (f32[88,128]{1,0:T(8,128)S(1)}, f32[88,128]{1,0:T(8,128)S(1)}, u32[]{:S(2)}, u32[]{:S(2)}) collective-permute-start(f32[88,128]{1,0:T(8,128)S(1)} %get-tuple-element.5), channel_id=1, source_target_pairs={{0,504},{8,0},{16,8},{24,16},{32,24},{40,32},{48,40},{56,48},{64,5... | collective-permute-start | bytes 135176 | tf_op jit(solution)/shard_map/ppermute | solution.py:34

commit v17 on v16

--- a/solution.py
+++ b/solution.py
@@ -27,6 +27,26 @@
         split3(value), onehot, (((1, 2), (1, 2)), ((), ())), preferred_element_type=jnp.float32
     )
     return product[:rows] + product[rows : 2 * rows] + product[2 * rows :]
+
+
+def shell_sum(value):
+    chips, cores = lax.axis_size("zhi"), lax.axis_size("core")
+    if chips != 4 or cores != 2:
+        return jnp.sum(lax.all_gather(value, ("zhi", "core")), axis=0)
+    swap = [(0, 1), (1, 0)]
+    from_next = ring(value, "zhi", -1)
+    from_prev = ring(value, "zhi", 1)
+    from_core = lax.ppermute(value, "core", swap)
+    opposite = ring(from_next, "zhi", -1)
+    core_sides = lax.ppermute(jnp.stack([from_next, from_prev]), "core", swap)
+    diagonal = [(j * 2 + d, ((j - 1) % chips) * 2 + (1 - d)) for j in range(chips) for d in range(cores)]
+    core_opposite = lax.ppermute(from_next, ("zhi", "core"), diagonal)
+    chip = lax.axis_index("zhi")
+    own = jnp.roll(jnp.stack([value, from_next, opposite, from_prev]), chip, axis=0)
+    other = jnp.roll(jnp.stack([from_core, core_sides[0], core_opposite, core_sides[1]]), chip, axis=0)
+    first = lax.axis_index("core") == 0
+    ordered = jnp.stack([jnp.where(first, own, other), jnp.where(first, other, own)], axis=1)
+    return jnp.sum(ordered.reshape(chips * cores, -1), axis=0)
 
 
 def ring(value, axis, step):
@@ -72,8 +92,7 @@
 
     at_stars = jnp.dot(weighted, spread, precision=HIGHEST, preferred_element_type=jnp.float32)
     partial_value = jnp.sum(radial * at_stars, axis=0)
-    pair = lax.psum(partial_value, "core")
-    predicted = jnp.sum(lax.all_gather(pair, "zhi"), axis=0)
+    predicted = shell_sum(partial_value)
     weight_back = (predicted - observed) / (sigma * sigma)
 
     adjoint_sum = lax.dot_general(

time: 63.2 us -> 77.8 us (1.23)
  the two profiles are of different devices: /device:TPU:126 before, /device:TPU:1 now
where the time goes in v17:
time: 77.8 us; the launch traced here: 77.3 us
  starting transfers between devices  52.5 us (67%)
  waiting for transfers between devices  13.3 us (17%)
  matrix products  5.81 us (7%)
  other arithmetic  4.54 us (6%)
  between operations  1.04 us (1%)
    ppermute x7, starting transfers between devices, ring(): lax.ppermute(value, axis, [(i, (i + step) % count) for i in range(count)])  43.7 us
    ppermute x7, waiting for transfers between devices, ring(): lax.ppermute(value, axis, [(i, (i + step) % count) for i in range(count)])  7.58 us
    ppermute x1, waiting for transfers between devices, shell_sum(): core_opposite = lax.ppermute(from_next, ('zhi', 'core'), diagonal)  5.76 us
    ppermute x1, starting transfers between devices, shell_sum(): core_sides = lax.ppermute(jnp.stack([from_next, from_prev]), 'core', swap)  4.63 us
    ppermute x1, starting transfers between devices, shell_sum(): core_opposite = lax.ppermute(from_next, ('zhi', 'core'), diagonal)  2.3 us
    reduce_sum x1, other arithmetic, on_device(): jnp.sum(jnp.where(pixel_id[None] == star_pixels[:, None, :], star_weights...  2.28 us
    dot_general x1, matrix products, on_device(): lax.dot_general(radial * weight_back[None, :], spread, (((1,), (1,)), (()...  2.06 us
    ppermute x1, starting transfers between devices, shell_sum(): from_core = lax.ppermute(value, 'core', swap)  1.92 us
  transfers between devices with their start and end apart: 10, of which 4 were waited for; matrix products, arithmetic and copies ran while one was open for 4% of the time, Pallas kernels for 0%

profile of v17, /device:TPU:1, one launch (start us, length us, event | category | flops | bytes accessed | tf_op | source)
XLA Modules:
  0.0 77.3 jit_solution(6153353858680854386)
XLA Ops:
  0.6 0.0 copy-start
  0.6 0.0 copy-start.7
  0.7 4.2 %collective-permute-start = (f32[88,256]{1,0:T(8,128)}, f32[88,256]{1,0:T(8,128)S(1)}, u32[]{:S(2)}, u32[]{:S(2)}) collective-permute-start(f32[88,256]{1,0:T(8,128)} %param.12), channel_id=1, source_target_pairs={{0,8},{8,16},{16,24},{24,32},{32,40},{40,48},{48,56},{56,64},{64,7... | collective-permute-start | bytes 270344 | tf_op jit(solution)/shard_map/ppermute | solution.py:54
  4.8 9.6 %collective-permute-start.1 = (f32[88,256]{1,0:T(8,128)}, f32[88,256]{1,0:T(8,128)S(1)}, u32[]{:S(2)}, u32[]{:S(2)}) collective-permute-start(f32[88,256]{1,0:T(8,128)} %param.12), channel_id=1, source_target_pairs={{0,504},{8,0},{16,8},{24,16},{32,24},{40,32},{48,40},{56,48},{64,5... | collective-permute-start | bytes 270344 | tf_op jit(solution)/shard_map/ppermute | solution.py:54
  14.5 2.3 %select_reduce_fusion = f32[256,2048]{1,0:T(8,128)S(1)} fusion(f32[4,2048]{1,0:T(4,128)} %param.18, s32[4,2048]{1,0:T(4,128)} %param.17), kind=kLoop, calls=%fused_computation | loop fusion | flops 5767168 | bytes 2162688 | tf_op jit(solution)/shard_map/reduce_sum | solution.py:86
  16.7 0.0 copy-start.3
  16.8 0.0 collective-permute-done
  16.8 0.0 collective-permute-done.1
  16.8 0.0 copy-done
  16.9 0.0 copy-done.7
  16.9 0.0 copy-start.1
  16.9 0.0 copy-start.2
  16.9 0.0 copy-start.6
  16.9 1.1 %fusion = f32[264,9,256]{2,0,1:T(8,128)S(1)} fusion(s32[9,256]{1,0:T(8,128)S(1)} %copy-done.7, bf16[88,512]{1,0:T(8,128)(2,1)S(1)} %get-tuple-element.13, bf16[88,512]{1,0:T(8,128)(2,1)S(1)} %get-tuple-element.12, bf16[88,512]{1,0:T(8,128)(2,1)S(1)} %get-tuple-element.11), kind=kOutput, calls=%fused_computation.3 | convolution fusion | flops 624844800 | bytes 2712576 | tf_op jit(solution)/shard_map/dot_general | solution.py:20
  18.0 0.0 copy-done.3
  18.0 0.0 copy-start.4
  18.0 0.0 copy-start.5
  18.0 0.2 fusion.19
  18.2 0.0 copy-done.1
  18.2 0.0 copy-done.2
  18.2 0.0 copy-done.6
  18.2 1.4 %fusion.6 = f32[2048]{0:T(1024)S(1)} fusion(f32[256,2048]{1,0:T(8,128)S(1)} %select_reduce_fusion, f32[2048]{0:T(1024)S(1)} %copy-done.1, s32[2048]{0:T(1024)S(1)} %copy-done.2, s32[88]{0:T(128)S(1)} %get-tuple-element.22, s32[88]{0:T(128)S(1)} %get-tuple-element.21, f32[88,256]{1,0:T(8,128)S(1)} %fusion.19, f32[88]{0:T(128)S(1)} %copy-done.6), kind=kOutput, calls=%fused_computation.11 | convolution fusion | flops 554749952 | bytes 2212896 | tf_op jit(solution)/shard_map/dot_general | solution.py:93
  19.6 10.9 %collective-permute-start.2 = (f32[2048]{0:T(1024)S(1)}, f32[2048]{0:T(1024)S(1)}, u32[]{:S(2)}, u32[]{:S(2)}) collective-permute-start(f32[2048]{0:T(1024)S(1)} %fusion.6), channel_id=1, source_target_pairs={{0,6},{2,0},{4,2},{6,4},{1,7},{3,1},{5,3},{7,5},{8,14},{10,8},{12,... | collective-permute-start | bytes 24584 | tf_op jit(solution)/shard_map/ppermute | solution.py:54
  30.6 1.9 %collective-permute-start.4 = (f32[2048]{0:T(1024)S(1)}, f32[2048]{0:T(1024)S(1)}, u32[]{:S(2)}, u32[]{:S(2)}) collective-permute-start(f32[2048]{0:T(1024)S(1)} %fusion.6), channel_id=1, source_target_pairs={{0,2},{2,4},{4,6},{6,0},{1,3},{3,5},{5,7},{7,1},{8,10},{10,12},{12... | collective-permute-start | bytes 24584 | tf_op jit(solution)/shard_map/ppermute | solution.py:54
  32.5 0.0 collective-permute-done.2
  32.5 6.4 %collective-permute-done.4 = f32[2048]{0:T(1024)S(1)} collective-permute-done((f32[2048]{0:T(1024)S(1)}, f32[2048]{0:T(1024)S(1)}, u32[]{:S(2)}, u32[]{:S(2)}) %collective-permute-start.4) | collective-permute-done | bytes 8224 | tf_op jit(solution)/shard_map/ppermute | solution.py:54
  38.9 4.6 %collective-permute-start.6 = (f32[2,2048]{1,0:T(2,128)S(1)}, f32[2,2048]{1,0:T(2,128)S(1)}, u32[]{:S(2)}, u32[]{:S(2)}) collective-permute-start(f32[2,2048]{1,0:T(2,128)S(1)} %pad_maximum_fusion.4), channel_id=1, source_target_pairs={{0,1},{1,0},{2,3},{3,2},{4,5},{5,4},{6,7},{7,6},{8,9},{9,8},{10,11... | collective-permute-start | bytes 49160 | tf_op jit(solution)/shard_map/ppermute | solution.py:41
  43.6 1.9 %collective-permute-start.5 = (f32[2048]{0:T(1024)S(1)}, f32[2048]{0:T(1024)S(1)}, u32[]{:S(2)}, u32[]{:S(2)}) collective-permute-start(f32[2048]{0:T(1024)S(1)} %fusion.6), channel_id=1, source_target_pairs={{0,1},{1,0},{2,3},{3,2},{4,5},{5,4},{6,7},{7,6},{8,9},{9,8},{10,11... | collective-permute-start | bytes 24584 | tf_op jit(solution)/shard_map/ppermute | solution.py:39
  45.5 5.2 %collective-permute-start.3 = (f32[2048]{0:T(1024)S(1)}, f32[2048]{0:T(1024)S(1)}, u32[]{:S(2)}, u32[]{:S(2)}) collective-permute-start(f32[2048]{0:T(1024)S(1)} %collective-permute-done.2), channel_id=1, source_target_pairs={{0,6},{2,0},{4,2},{6,4},{1,7},{3,1},{5,3},{7,5},{8,14},{10,8},{12,... | collective-permute-start | bytes 24584 | tf_op jit(solution)/shard_map/ppermute | solution.py:54
  50.7 2.3 %collective-permute-start.7 = (f32[2048]{0:T(1024)S(1)}, f32[2048]{0:T(1024)S(1)}, u32[]{:S(2)}, u32[]{:S(2)}) collective-permute-start(f32[2048]{0:T(1024)S(1)} %collective-permute-done.2), channel_id=1, source_target_pairs={{0,7},{1,6},{2,1},{3,0},{4,3},{5,2},{6,5},{7,4},{8,15},{9,14},{10,... | collective-permute-start | bytes 24584 | tf_op jit(solution)/shard_map/ppermute | solution.py:43
  53.0 0.0 collective-permute-done.6
  53.0 0.0 collective-permute-done.5
  53.0 0.8 collective-permute-done.3
  53.8 5.8 %collective-permute-done.7 = f32[2048]{0:T(1024)S(1)} collective-permute-done((f32[2048]{0:T(1024)S(1)}, f32[2048]{0:T(1024)S(1)}, u32[]{:S(2)}, u32[]{:S(2)}) %collective-permute-start.7) | collective-permute-done | bytes 8224 | tf_op jit(solution)/shard_map/ppermute | solution.py:43
  59.6 0.5 select_reduce_fusion.1
  60.0 0.0 copy-done.4
  60.1 0.0 copy-done.5
  60.1 0.6 multiply_divide_fusion
  60.7 2.1 %convolution_multiply_fusion.1 = f32[88,256]{1,0:T(8,128)S(1)} fusion(f32[256,2048]{1,0:T(8,128)S(1)} %select_reduce_fusion, f32[2048]{0:T(1024)S(1)} %get-tuple-element.9, f32[2048]{0:T(1024)S(1)} %copy-done.1, s32[2048]{0:T(1024)S(1)} %copy-done.2, s32[88]{0:T(128)S(1)} %get-tuple-element.22, s32[88]{0:T(128)S(1)} %get-tuple-element.21, ...), kind=kOutput, calls=%fused_computation.22 | convolution fusion | flops 554594304 | bytes 2303008 | tf_op jit(solution)/shard_map/dot_general | solution.py:98
  62.7 0.2 reduce-precision_convert_fusion.1
  63.0 0.6 fusion.14
  63.7 1.9 %collective-permute-start.8 = (f32[88,128]{1,0:T(8,128)S(1)}, f32[88,128]{1,0:T(8,128)S(1)}, u32[]{:S(2)}, u32[]{:S(2)}) collective-permute-start(f32[88,128]{1,0:T(8,128)S(1)} %get-tuple-element.5), channel_id=1, source_target_pairs={{0,8},{8,16},{16,24},{24,32},{32,40},{40,48},{48,56},{56,64},{64,7... | collective-permute-start | bytes 135176 | tf_op jit(solution)/shard_map/ppermute | solution.py:54
  65.6 9.9 %collective-permute-start.9 = (f32[88,128]{1,0:T(8,128)S(1)}, f32[88,128]{1,0:T(8,128)S(1)}, u32[]{:S(2)}, u32[]{:S(2)}) collective-permute-start(f32[88,128]{1,0:T(8,128)S(1)} %get-tuple-element.6), channel_id=1, source_target_pairs={{0,504},{8,0},{16,8},{24,16},{32,24},{40,32},{48,40},{56,48},{64,5... | collective-permute-start | bytes 135176 | tf_op jit(solution)/shard_map/ppermute | solution.py:54
  75.6 0.6 fusion.11
  76.2 0.0 collective-permute-done.8
  76.2 0.5 collective-permute-done.9
  76.7 0.7 fusion.36
  (10 shorter events, 0.1 us)
Async XLA Ops:
  0.6 16.2 %copy-start = (f32[88,256]{1,0:T(8,128)S(1)}, f32[88,256]{1,0:T(8,128)}, u32[]{:S(2)}) copy-start(f32[88,256]{1,0:T(8,128)} %param.12) | copy-start | bytes 270340
  0.6 16.2 %copy-start.7 = (s32[9,256]{1,0:T(8,128)S(1)}, s32[9,256]{1,0:T(8,128)}, u32[]{:S(2)}) copy-start(s32[9,256]{1,0:T(8,128)} %param.15) | copy-start | bytes 27652
  0.7 16.1 %collective-permute-start = (f32[88,256]{1,0:T(8,128)}, f32[88,256]{1,0:T(8,128)S(1)}, u32[]{:S(2)}, u32[]{:S(2)}) collective-permute-start(f32[88,256]{1,0:T(8,128)} %param.12), channel_id=1, source_target_pairs={{0,8},{8,16},{16,24},{24,32},{32,40},{40,48},{48,56},{56,64},{64,7... | collective-permute-start | bytes 270344 | tf_op jit(solution)/shard_map/ppermute | solution.py:54
  4.8 12.0 %collective-permute-start.1 = (f32[88,256]{1,0:T(8,128)}, f32[88,256]{1,0:T(8,128)S(1)}, u32[]{:S(2)}, u32[]{:S(2)}) collective-permute-start(f32[88,256]{1,0:T(8,128)} %param.12), channel_id=1, source_target_pairs={{0,504},{8,0},{16,8},{24,16},{32,24},{40,32},{48,40},{56,48},{64,5... | collective-permute-start | bytes 270344 | tf_op jit(solution)/shard_map/ppermute | solution.py:54
  16.7 1.3 %copy-start.3 = (f32[88,9]{0,1:T(8,128)S(1)}, f32[88,9]{0,1:T(8,128)}, u32[]{:S(2)}) copy-start(f32[88,9]{0,1:T(8,128)} %param.13) | copy-start | bytes 9508
  16.9 1.3 %copy-start.1 = (f32[2048]{0:T(1024)S(1)}, f32[2048]{0:T(1024)}, u32[]{:S(2)}) copy-start(f32[2048]{0:T(1024)} %param.19) | copy-start | bytes 24580
  16.9 1.3 %copy-start.2 = (s32[2048]{0:T(1024)S(1)}, s32[2048]{0:T(1024)}, u32[]{:S(2)}) copy-start(s32[2048]{0:T(1024)} %param.16) | copy-start | bytes 24580
  16.9 1.3 %copy-start.6 = (f32[88]{0:T(128)S(1)}, f32[88]{0:T(128)}, u32[]{:S(2)}) copy-start(f32[88]{0:T(128)} %param.14) | copy-start | bytes 1060
  18.0 42.0 %copy-start.4 = (f32[2048]{0:T(1024)S(1)}, f32[2048]{0:T(1024)}, u32[]{:S(2)}) copy-start(f32[2048]{0:T(1024)} %param.21) | copy-start | bytes 24580
  18.0 42.0 %copy-start.5 = (f32[2048]{0:T(1024)S(1)}, f32[2048]{0:T(1024)}, u32[]{:S(2)}) copy-start(f32[2048]{0:T(1024)} %param.20) | copy-start | bytes 24580
  19.6 12.9 %collective-permute-start.2 = (f32[2048]{0:T(1024)S(1)}, f32[2048]{0:T(1024)S(1)}, u32[]{:S(2)}, u32[]{:S(2)}) collective-permute-start(f32[2048]{0:T(1024)S(1)} %fusion.6), channel_id=1, source_target_pairs={{0,6},{2,0},{4,2},{6,4},{1,7},{3,1},{5,3},{7,5},{8,14},{10,8},{12,... | collective-permute-start | bytes 24584 | tf_op jit(solution)/shard_map/ppermute | solution.py:54
  30.6 8.3 %collective-permute-start.4 = (f32[2048]{0:T(1024)S(1)}, f32[2048]{0:T(1024)S(1)}, u32[]{:S(2)}, u32[]{:S(2)}) collective-permute-start(f32[2048]{0:T(1024)S(1)} %fusion.6), channel_id=1, source_target_pairs={{0,2},{2,4},{4,6},{6,0},{1,3},{3,5},{5,7},{7,1},{8,10},{10,12},{12... | collective-permute-start | bytes 24584 | tf_op jit(solution)/shard_map/ppermute | solution.py:54
  38.9 14.1 %collective-permute-start.6 = (f32[2,2048]{1,0:T(2,128)S(1)}, f32[2,2048]{1,0:T(2,128)S(1)}, u32[]{:S(2)}, u32[]{:S(2)}) collective-permute-start(f32[2,2048]{1,0:T(2,128)S(1)} %pad_maximum_fusion.4), channel_id=1, source_target_pairs={{0,1},{1,0},{2,3},{3,2},{4,5},{5,4},{6,7},{7,6},{8,9},{9,8},{10,11... | collective-permute-start | bytes 49160 | tf_op jit(solution)/shard_map/ppermute | solution.py:41
  43.6 9.5 %collective-permute-start.5 = (f32[2048]{0:T(1024)S(1)}, f32[2048]{0:T(1024)S(1)}, u32[]{:S(2)}, u32[]{:S(2)}) collective-permute-start(f32[2048]{0:T(1024)S(1)} %fusion.6), channel_id=1, source_target_pairs={{0,1},{1,0},{2,3},{3,2},{4,5},{5,4},{6,7},{7,6},{8,9},{9,8},{10,11... | collective-permute-start | bytes 24584 | tf_op jit(solution)/shard_map/ppermute | solution.py:39
  45.5 8.3 %collective-permute-start.3 = (f32[2048]{0:T(1024)S(1)}, f32[2048]{0:T(1024)S(1)}, u32[]{:S(2)}, u32[]{:S(2)}) collective-permute-start(f32[2048]{0:T(1024)S(1)} %collective-permute-done.2), channel_id=1, source_target_pairs={{0,6},{2,0},{4,2},{6,4},{1,7},{3,1},{5,3},{7,5},{8,14},{10,8},{12,... | collective-permute-start | bytes 24584 | tf_op jit(solution)/shard_map/ppermute | solution.py:54
  50.7 8.9 %collective-permute-start.7 = (f32[2048]{0:T(1024)S(1)}, f32[2048]{0:T(1024)S(1)}, u32[]{:S(2)}, u32[]{:S(2)}) collective-permute-start(f32[2048]{0:T(1024)S(1)} %collective-permute-done.2), channel_id=1, source_target_pairs={{0,7},{1,6},{2,1},{3,0},{4,3},{5,2},{6,5},{7,4},{8,15},{9,14},{10,... | collective-permute-start | bytes 24584 | tf_op jit(solution)/shard_map/ppermute | solution.py:43
  63.7 12.5 %collective-permute-start.8 = (f32[88,128]{1,0:T(8,128)S(1)}, f32[88,128]{1,0:T(8,128)S(1)}, u32[]{:S(2)}, u32[]{:S(2)}) collective-permute-start(f32[88,128]{1,0:T(8,128)S(1)} %get-tuple-element.5), channel_id=1, source_target_pairs={{0,8},{8,16},{16,24},{24,32},{32,40},{40,48},{48,56},{56,64},{64,7... | collective-permute-start | bytes 135176 | tf_op jit(solution)/shard_map/ppermute | solution.py:54
  65.6 11.1 %collective-permute-start.9 = (f32[88,128]{1,0:T(8,128)S(1)}, f32[88,128]{1,0:T(8,128)S(1)}, u32[]{:S(2)}, u32[]{:S(2)}) collective-permute-start(f32[88,128]{1,0:T(8,128)S(1)} %get-tuple-element.6), channel_id=1, source_target_pairs={{0,504},{8,0},{16,8},{24,16},{32,24},{40,32},{48,40},{56,48},{64,5... | collective-permute-start | bytes 135176 | tf_op jit(solution)/shard_map/ppermute | solution.py:54

commit v18 on v15

--- a/solution.py
+++ b/solution.py
@@ -88,13 +88,16 @@
     predicted = chip_sum(pair, "zhi")
     weight_back = (predicted - observed) / (sigma * sigma)
 
-    adjoint_sum = lax.dot_general(
-        radial * weight_back[None, :],
-        spread,
+    spread_parts = lax.optimization_barrier(split3(spread))
+    spread_parts = spread_parts.reshape(3 * pixels, nstars)
+    blocks = lax.dot_general(
+        split3(radial * weight_back[None, :]),
+        spread_parts,
         (((1,), (1,)), ((), ())),
-        precision=HIGHEST,
         preferred_element_type=jnp.float32,
     )
+    part = lambda i, j: blocks[i * shells : (i + 1) * shells, j * pixels : (j + 1) * pixels]
+    adjoint_sum = ((part(2, 0) + part(0, 2)) + part(1, 1)) + (part(1, 0) + part(0, 1)) + part(0, 0)
     sensitivity = adjoint_sum * weighted
 
     terms = stencil[:, :, None] * sensitivity[:, None, :]

time: 62.2 us -> 73.7 us (1.18)
  waiting for transfers between devices: 1.64 us -> 11.5 us
  other arithmetic: 3.48 us -> 8.84 us
  blocking collectives: 7.3 us -> 4.26 us
  starting transfers between devices: 41.9 us -> 40.8 us
  matrix products: 5.82 us -> 6.73 us
    ppermute x7, waiting for transfers between devices: 1.64 us -> 11.5 us  [ring(): lax.ppermute(value, axis, [(i, (i + step) % count) for i in range(count)])]
    psum x1, blocking collectives: 7.3 us -> 4.26 us  [on_device(): pair = lax.psum(partial_value, 'core')]
    concatenate x0 -> x1, other arithmetic: none -> 3.03 us  [split3(): return jnp.concatenate([high, middle, low], axis=0).astype(jnp.bfloat16)]
    another operation x2 -> x4, other arithmetic: 0.29 us -> 2.53 us
    ppermute x7, starting transfers between devices: 41.9 us -> 40.8 us  [ring(): lax.ppermute(value, axis, [(i, (i + step) % count) for i in range(count)])]
    dot_general x1, matrix products: 2.06 us -> 2.98 us  [on_device(): lax.dot_general(split3(radial * weight_back[None, :]), spread_parts, (((1...]
  transfers between devices with their start and end apart: 7 -> 7, of which waited for: 2 -> 3; matrix products, arithmetic and copies ran while one was open for 5% -> 11% of each run, Pallas kernels for 0% -> 0%
where the time goes in v18:
time: 73.7 us; the launch traced here: 73.3 us
  starting transfers between devices  40.8 us (55%)
  waiting for transfers between devices  11.5 us (16%)
  other arithmetic  8.84 us (12%)
  matrix products  6.73 us (9%)
  blocking collectives  4.26 us (6%)
  between operations  0.98 us (1%)
    ppermute x7, starting transfers between devices, ring(): lax.ppermute(value, axis, [(i, (i + step) % count) for i in range(count)])  40.8 us
    ppermute x7, waiting for transfers between devices, ring(): lax.ppermute(value, axis, [(i, (i + step) % count) for i in range(count)])  11.5 us
    psum x1, blocking collectives, on_device(): pair = lax.psum(partial_value, 'core')  4.26 us
    concatenate x1, other arithmetic, split3(): return jnp.concatenate([high, middle, low], axis=0).astype(jnp.bfloat16)  3.03 us
    dot_general x1, matrix products, on_device(): lax.dot_general(split3(radial * weight_back[None, :]), spread_parts, (((1...  2.98 us
    another operation x4, other arithmetic  2.53 us
    reduce_sum x1, other arithmetic, on_device(): jnp.sum(jnp.where(pixel_id[None] == star_pixels[:, None, :], star_weights...  2.28 us
  transfers between devices with their start and end apart: 7, of which 3 were waited for; matrix products, arithmetic and copies ran while one was open for 11% of the time, Pallas kernels for 0%

profile of v18, /device:TPU:1, one launch (start us, length us, event | category | flops | bytes accessed | tf_op | source)
XLA Modules:
  0.0 73.3 jit_solution(6075634117873966307)
XLA Ops:
  0.6 11.7 %collective-permute-start.1 = (f32[88,256]{1,0:T(8,128)}, f32[88,256]{1,0:T(8,128)S(1)}, u32[]{:S(2)}, u32[]{:S(2)}) collective-permute-start(f32[88,256]{1,0:T(8,128)} %param.10), channel_id=1, source_target_pairs={{0,504},{8,0},{16,8},{24,16},{32,24},{40,32},{48,40},{56,48},{64,5... | collective-permute-start | bytes 270344 | tf_op jit(solution)/shard_map/ppermute | solution.py:46
  12.4 1.9 %collective-permute-start = (f32[88,256]{1,0:T(8,128)}, f32[88,256]{1,0:T(8,128)S(1)}, u32[]{:S(2)}, u32[]{:S(2)}) collective-permute-start(f32[88,256]{1,0:T(8,128)} %param.10), channel_id=1, source_target_pairs={{0,8},{8,16},{16,24},{24,32},{32,40},{40,48},{48,56},{56,64},{64,7... | collective-permute-start | bytes 270344 | tf_op jit(solution)/shard_map/ppermute | solution.py:46
  14.3 2.3 %select_reduce_fusion = f32[256,2048]{1,0:T(8,128)S(1)} fusion(f32[4,2048]{1,0:T(4,128)} %param.16, s32[4,2048]{1,0:T(4,128)} %param.15), kind=kLoop, calls=%fused_computation | loop fusion | flops 5767168 | bytes 2162688 | tf_op jit(solution)/shard_map/reduce_sum | solution.py:78
  16.6 1.9 %reduce-precision_convert_fusion.1 = (bf16[256,2048]{1,0:T(8,128)(2,1)S(1)}, bf16[256,2048]{1,0:T(8,128)(2,1)}, bf16[256,2048]{1,0:T(8,128)(2,1)}) fusion(f32[256,2048]{1,0:T(8,128)S(1)} %select_reduce_fusion), kind=kLoop, calls=%fused_computation.8 | loop fusion | flops 3670016 | bytes 5242880 | tf_op jit(solution)/shard_map/convert.3
  18.5 0.0 copy-start
  18.5 0.0 copy-start.8
  18.5 3.0 %pad_maximum_fusion = bf16[768,2048]{1,0:T(8,128)(2,1)} fusion(bf16[256,2048]{1,0:T(8,128)(2,1)} %get-tuple-element.7, bf16[256,2048]{1,0:T(8,128)(2,1)} %get-tuple-element.8, bf16[256,2048]{1,0:T(8,128)(2,1)S(1)} %get-tuple-element.6), kind=kLoop, calls=%fused_computation.4 | loop fusion | flops 9437184 | bytes 6291456 | tf_op jit(solution)/shard_map/concatenate | solution.py:15
  21.6 0.0 copy-start.3
  21.6 0.0 collective-permute-done.1
  21.6 2.3 %collective-permute-done = f32[88,256]{1,0:T(8,128)S(1)} collective-permute-done((f32[88,256]{1,0:T(8,128)}, f32[88,256]{1,0:T(8,128)S(1)}, u32[]{:S(2)}, u32[]{:S(2)}) %collective-permute-start) | collective-permute-done | bytes 90144 | tf_op jit(solution)/shard_map/ppermute | solution.py:46
  23.9 0.0 copy-done
  23.9 0.0 copy-done.8
  23.9 0.0 copy-start.1
  23.9 0.0 copy-start.2
  24.0 0.0 copy-start.7
  24.0 1.1 %fusion = f32[264,9,256]{2,0,1:T(8,128)S(1)} fusion(s32[9,256]{1,0:T(8,128)S(1)} %copy-done.8, bf16[88,512]{1,0:T(8,128)(2,1)S(1)} %get-tuple-element.11, bf16[88,512]{1,0:T(8,128)(2,1)S(1)} %get-tuple-element.10, bf16[88,512]{1,0:T(8,128)(2,1)S(1)} %get-tuple-element.9), kind=kOutput, calls=%fused_computation.3 | convolution fusion | flops 624844800 | bytes 2712576 | tf_op jit(solution)/shard_map/dot_general | solution.py:20
  25.0 0.0 copy-done.3
  25.1 0.0 copy-start.5
  25.1 0.0 copy-start.6
  25.1 0.2 fusion.26
  25.3 0.0 copy-done.1
  25.3 0.0 copy-done.2
  25.3 0.0 copy-done.7
  25.3 1.4 %fusion.7 = f32[2048]{0:T(1024)S(1)} fusion(f32[256,2048]{1,0:T(8,128)S(1)} %select_reduce_fusion, f32[2048]{0:T(1024)S(1)} %copy-done.1, s32[2048]{0:T(1024)S(1)} %copy-done.2, s32[88]{0:T(128)S(1)} %get-tuple-element.21, s32[88]{0:T(128)S(1)} %get-tuple-element.20, f32[88,256]{1,0:T(8,128)S(1)} %fusion.26, f32[88]{0:T(128)S(1)} %copy-done.7), kind=kOutput, calls=%fused_computation.17 | convolution fusion | flops 554749952 | bytes 2212896 | tf_op jit(solution)/shard_map/dot_general | solution.py:85
  26.7 4.3 %psum.7 = f32[2048]{0:T(1024)S(1)} all-reduce(f32[2048]{0:T(1024)S(1)} %fusion.7), channel_id=1, replica_groups=mesh['ang'=64,'zhi'=4,'core'=2] {'core'}, use_global_device_ids=true, to_apply=%region_3.4 | all-reduce | flops 2048 | bytes 16384 | tf_op jit(solution)/shard_map/psum | solution.py:87
  30.9 9.8 %collective-permute-start.2 = (f32[2048]{0:T(1024)S(1)}, f32[2048]{0:T(1024)S(1)}, u32[]{:S(2)}, u32[]{:S(2)}) collective-permute-start(f32[2048]{0:T(1024)S(1)} %psum.7), channel_id=1, source_target_pairs={{0,6},{2,0},{4,2},{6,4},{1,7},{3,1},{5,3},{7,5},{8,14},{10,8},{12,... | collective-permute-start | bytes 24584 | tf_op jit(solution)/shard_map/ppermute | solution.py:46
  40.7 1.9 %collective-permute-start.4 = (f32[2048]{0:T(1024)S(1)}, f32[2048]{0:T(1024)S(1)}, u32[]{:S(2)}, u32[]{:S(2)}) collective-permute-start(f32[2048]{0:T(1024)S(1)} %psum.7), channel_id=1, source_target_pairs={{0,2},{2,4},{4,6},{6,0},{1,3},{3,5},{5,7},{7,1},{8,10},{10,12},{12... | collective-permute-start | bytes 24584 | tf_op jit(solution)/shard_map/ppermute | solution.py:46
  42.6 0.0 collective-permute-done.2
  42.7 7.3 %collective-permute-start.3 = (f32[2048]{0:T(1024)S(1)}, f32[2048]{0:T(1024)S(1)}, u32[]{:S(2)}, u32[]{:S(2)}) collective-permute-start(f32[2048]{0:T(1024)S(1)} %collective-permute-done.2), channel_id=1, source_target_pairs={{0,6},{2,0},{4,2},{6,4},{1,7},{3,1},{5,3},{7,5},{8,14},{10,8},{12,... | collective-permute-start | bytes 24584 | tf_op jit(solution)/shard_map/ppermute | solution.py:46
  50.0 0.0 collective-permute-done.4
  50.0 1.0 %collective-permute-done.3 = f32[2048]{0:T(1024)S(1)} collective-permute-done((f32[2048]{0:T(1024)S(1)}, f32[2048]{0:T(1024)S(1)}, u32[]{:S(2)}, u32[]{:S(2)}) %collective-permute-start.3) | collective-permute-done | bytes 8224 | tf_op jit(solution)/shard_map/ppermute | solution.py:46
  51.0 0.1 concatenate.27
  51.1 0.0 copy-done.5
  51.1 0.0 copy-done.6
  51.1 0.0 copy-start.4
  51.2 0.3 reduce-precision_convert_fusion.5
  51.5 3.0 %fusion.18 = f32[264,768]{1,0:T(8,128)S(1)} fusion(bf16[768,2048]{1,0:T(8,128)(2,1)} %pad_maximum_fusion, bf16[88,2048]{1,0:T(8,128)(2,1)S(1)} %get-tuple-element.19, bf16[88,2048]{1,0:T(8,128)(2,1)S(1)} %get-tuple-element.18, bf16[88,2048]{1,0:T(8,128)(2,1)S(1)} %get-tuple-element.17), kind=kOutput, calls=%fused_computation.28 | convolution fusion | flops 833716224 | bytes 5038080 | tf_op jit(solution)/shard_map/dot_general | solution.py:93
  54.5 0.0 copy-done.4
  54.5 0.1 fusion.36
  54.6 0.2 reduce-precision_convert_fusion.3
  54.8 0.6 fusion.15
  55.5 6.3 %collective-permute-start.6 = (f32[88,128]{1,0:T(8,128)S(1)}, f32[88,128]{1,0:T(8,128)S(1)}, u32[]{:S(2)}, u32[]{:S(2)}) collective-permute-start(f32[88,128]{1,0:T(8,128)S(1)} %get-tuple-element.5), channel_id=1, source_target_pairs={{0,504},{8,0},{16,8},{24,16},{32,24},{40,32},{48,40},{56,48},{64,5... | collective-permute-start | bytes 135176 | tf_op jit(solution)/shard_map/ppermute | solution.py:46
  61.8 1.9 %collective-permute-start.5 = (f32[88,128]{1,0:T(8,128)S(1)}, f32[88,128]{1,0:T(8,128)S(1)}, u32[]{:S(2)}, u32[]{:S(2)}) collective-permute-start(f32[88,128]{1,0:T(8,128)S(1)} %get-tuple-element.4), channel_id=1, source_target_pairs={{0,8},{8,16},{16,24},{24,32},{32,40},{40,48},{48,56},{56,64},{64,7... | collective-permute-start | bytes 135176 | tf_op jit(solution)/shard_map/ppermute | solution.py:46
  63.7 0.6 fusion.12
  64.4 0.0 collective-permute-done.6
  64.4 8.2 %collective-permute-done.5 = f32[88,128]{1,0:T(8,128)S(1)} collective-permute-done((f32[88,128]{1,0:T(8,128)S(1)}, f32[88,128]{1,0:T(8,128)S(1)}, u32[]{:S(2)}, u32[]{:S(2)}) %collective-permute-start.5) | collective-permute-done | bytes 45088 | tf_op jit(solution)/shard_map/ppermute | solution.py:46
  72.6 0.7 fusion.35
  (10 shorter events, 0.1 us)
Async XLA Ops:
  0.6 20.9 %collective-permute-start.1 = (f32[88,256]{1,0:T(8,128)}, f32[88,256]{1,0:T(8,128)S(1)}, u32[]{:S(2)}, u32[]{:S(2)}) collective-permute-start(f32[88,256]{1,0:T(8,128)} %param.10), channel_id=1, source_target_pairs={{0,504},{8,0},{16,8},{24,16},{32,24},{40,32},{48,40},{56,48},{64,5... | collective-permute-start | bytes 270344 | tf_op jit(solution)/shard_map/ppermute | solution.py:46
  12.4 11.5 %collective-permute-start = (f32[88,256]{1,0:T(8,128)}, f32[88,256]{1,0:T(8,128)S(1)}, u32[]{:S(2)}, u32[]{:S(2)}) collective-permute-start(f32[88,256]{1,0:T(8,128)} %param.10), channel_id=1, source_target_pairs={{0,8},{8,16},{16,24},{24,32},{32,40},{40,48},{48,56},{56,64},{64,7... | collective-permute-start | bytes 270344 | tf_op jit(solution)/shard_map/ppermute | solution.py:46
  18.5 5.4 %copy-start = (f32[88,256]{1,0:T(8,128)S(1)}, f32[88,256]{1,0:T(8,128)}, u32[]{:S(2)}) copy-start(f32[88,256]{1,0:T(8,128)} %param.10) | copy-start | bytes 270340
  18.5 5.4 %copy-start.8 = (s32[9,256]{1,0:T(8,128)S(1)}, s32[9,256]{1,0:T(8,128)}, u32[]{:S(2)}) copy-start(s32[9,256]{1,0:T(8,128)} %param.13) | copy-start | bytes 27652
  21.6 3.5 %copy-start.3 = (f32[88,9]{0,1:T(8,128)S(1)}, f32[88,9]{0,1:T(8,128)}, u32[]{:S(2)}) copy-start(f32[88,9]{0,1:T(8,128)} %param.11) | copy-start | bytes 9508
  23.9 1.3 %copy-start.1 = (f32[2048]{0:T(1024)S(1)}, f32[2048]{0:T(1024)}, u32[]{:S(2)}) copy-start(f32[2048]{0:T(1024)} %param.17) | copy-start | bytes 24580
  23.9 1.3 %copy-start.2 = (s32[2048]{0:T(1024)S(1)}, s32[2048]{0:T(1024)}, u32[]{:S(2)}) copy-start(s32[2048]{0:T(1024)} %param.14) | copy-start | bytes 24580
  24.0 1.3 %copy-start.7 = (f32[88]{0:T(128)S(1)}, f32[88]{0:T(128)}, u32[]{:S(2)}) copy-start(f32[88]{0:T(128)} %param.12) | copy-start | bytes 1060
  25.1 26.1 %copy-start.5 = (f32[2048]{0:T(1024)S(1)}, f32[2048]{0:T(1024)}, u32[]{:S(2)}) copy-start(f32[2048]{0:T(1024)} %param.19) | copy-start | bytes 24580
  25.1 26.1 %copy-start.6 = (f32[2048]{0:T(1024)S(1)}, f32[2048]{0:T(1024)}, u32[]{:S(2)}) copy-start(f32[2048]{0:T(1024)} %param.18) | copy-start | bytes 24580
  30.9 11.7 %collective-permute-start.2 = (f32[2048]{0:T(1024)S(1)}, f32[2048]{0:T(1024)S(1)}, u32[]{:S(2)}, u32[]{:S(2)}) collective-permute-start(f32[2048]{0:T(1024)S(1)} %psum.7), channel_id=1, source_target_pairs={{0,6},{2,0},{4,2},{6,4},{1,7},{3,1},{5,3},{7,5},{8,14},{10,8},{12,... | collective-permute-start | bytes 24584 | tf_op jit(solution)/shard_map/ppermute | solution.py:46
  40.7 9.2 %collective-permute-start.4 = (f32[2048]{0:T(1024)S(1)}, f32[2048]{0:T(1024)S(1)}, u32[]{:S(2)}, u32[]{:S(2)}) collective-permute-start(f32[2048]{0:T(1024)S(1)} %psum.7), channel_id=1, source_target_pairs={{0,2},{2,4},{4,6},{6,0},{1,3},{3,5},{5,7},{7,1},{8,10},{10,12},{12... | collective-permute-start | bytes 24584 | tf_op jit(solution)/shard_map/ppermute | solution.py:46
  42.7 8.3 %collective-permute-start.3 = (f32[2048]{0:T(1024)S(1)}, f32[2048]{0:T(1024)S(1)}, u32[]{:S(2)}, u32[]{:S(2)}) collective-permute-start(f32[2048]{0:T(1024)S(1)} %collective-permute-done.2), channel_id=1, source_target_pairs={{0,6},{2,0},{4,2},{6,4},{1,7},{3,1},{5,3},{7,5},{8,14},{10,8},{12,... | collective-permute-start | bytes 24584 | tf_op jit(solution)/shard_map/ppermute | solution.py:46
  51.1 3.3 %copy-start.4 = (f32[2048]{0:T(1024)}, f32[2048]{0:T(1024)S(1)}, u32[]{:S(2)}) copy-start(f32[2048]{0:T(1024)S(1)} %dynamic-slice_reduce_fusion) | copy-start | bytes 24580
  55.5 8.8 %collective-permute-start.6 = (f32[88,128]{1,0:T(8,128)S(1)}, f32[88,128]{1,0:T(8,128)S(1)}, u32[]{:S(2)}, u32[]{:S(2)}) collective-permute-start(f32[88,128]{1,0:T(8,128)S(1)} %get-tuple-element.5), channel_id=1, source_target_pairs={{0,504},{8,0},{16,8},{24,16},{32,24},{40,32},{48,40},{56,48},{64,5... | collective-permute-start | bytes 135176 | tf_op jit(solution)/shard_map/ppermute | solution.py:46
  61.8 10.8 %collective-permute-start.5 = (f32[88,128]{1,0:T(8,128)S(1)}, f32[88,128]{1,0:T(8,128)S(1)}, u32[]{:S(2)}, u32[]{:S(2)}) collective-permute-start(f32[88,128]{1,0:T(8,128)S(1)} %get-tuple-element.4), channel_id=1, source_target_pairs={{0,8},{8,16},{16,24},{24,32},{32,40},{40,48},{48,56},{56,64},{64,7... | collective-permute-start | bytes 135176 | tf_op jit(solution)/shard_map/ppermute | solution.py:46

commit v19 on v15

--- a/solution.py
+++ b/solution.py
@@ -75,7 +75,10 @@
 
     nstars = star_bin.shape[0]
     pixel_id = lax.broadcasted_iota(jnp.int32, (pixels, nstars), 0)
-    spread = jnp.sum(jnp.where(pixel_id[None] == star_pixels[:, None, :], star_weights[:, None, :], 0.0), axis=0)
+    spread = jnp.zeros((pixels, nstars), jnp.float32)
+    for corner in range(star_pixels.shape[0]):
+        spread = spread + jnp.where(pixel_id == star_pixels[corner][None, :], star_weights[corner][None, :], 0.0)
+    spread = lax.optimization_barrier(spread)
 
     shell_start = (lax.axis_index("zhi") * lax.axis_size("core") + lax.axis_index("core")) * shells
     bin_id = shell_start + lax.broadcasted_iota(jnp.int32, (shells, nstars), 0)

time: 62.2 us -> 62.9 us (1.011)
  local copies, waits for them, and re-layouts: 0.18 us -> 2.56 us
  other arithmetic: 3.48 us -> 1.95 us
    reduce_sum x1 -> x0, other arithmetic: 2.28 us -> none  [on_device(): jnp.sum(jnp.where(pixel_id[None] == star_pixels[:, None, :], star_weights...]
    slice x0 -> x2, local copies, waits for them, and re-layouts: none -> 1.91 us  [the longest x1 0.96 us: on_device(): star_pixels[corner][None, :]]
    add x0 -> x1, other arithmetic: none -> 0.75 us  [on_device(): spread + jnp.where(pixel_id == star_pixels[corner][None, :], star_weights...]
where the time goes in v19:
time: 62.9 us; the launch traced here: 61.8 us
  starting transfers between devices  41.6 us (66%)
  blocking collectives  7.24 us (12%)
  matrix products  5.81 us (9%)
  local copies, waits for them, and re-layouts  2.56 us (4%)
  other arithmetic  1.95 us (3%)
  waiting for transfers between devices  1.65 us (3%)
  between operations  1.01 us (2%)
    ppermute x7, starting transfers between devices, ring(): lax.ppermute(value, axis, [(i, (i + step) % count) for i in range(count)])  41.6 us
    psum x1, blocking collectives, on_device(): pair = lax.psum(partial_value, 'core')  7.24 us
    dot_general x1, matrix products, on_device(): lax.dot_general(radial * weight_back[None, :], spread, (((1,), (1,)), (()...  2.06 us
    ppermute x7, waiting for transfers between devices, ring(): lax.ppermute(value, axis, [(i, (i + step) % count) for i in range(count)])  1.65 us
    dot_general x1, matrix products, on_device(): jnp.dot(weighted, spread, precision=HIGHEST, preferred_element_type=jnp.f...  1.4 us
    dot_general x2, matrix products, spread_select(): lax.dot_general(split3(value), onehot, (((1, 2), (1, 2)), ((), ())), pref...  1.29 us
  transfers between devices with their start and end apart: 7, of which 2 were waited for; matrix products, arithmetic and copies ran while one was open for 5% of the time, Pallas kernels for 0%

profile of v19, /device:TPU:1, one launch (start us, length us, event | category | flops | bytes accessed | tf_op | source)
XLA Modules:
  0.0 61.8 jit_solution(2946234176217269525)
XLA Ops:
  0.6 0.0 copy-start
  0.6 0.0 copy-start.8
  0.6 4.2 %collective-permute-start = (f32[88,256]{1,0:T(8,128)}, f32[88,256]{1,0:T(8,128)S(1)}, u32[]{:S(2)}, u32[]{:S(2)}) collective-permute-start(f32[88,256]{1,0:T(8,128)} %param.10), channel_id=1, source_target_pairs={{0,8},{8,16},{16,24},{24,32},{32,40},{40,48},{48,56},{56,64},{64,7... | collective-permute-start | bytes 270344 | tf_op jit(solution)/shard_map/ppermute | solution.py:46
  4.8 9.6 %collective-permute-start.1 = (f32[88,256]{1,0:T(8,128)}, f32[88,256]{1,0:T(8,128)S(1)}, u32[]{:S(2)}, u32[]{:S(2)}) collective-permute-start(f32[88,256]{1,0:T(8,128)} %param.10), channel_id=1, source_target_pairs={{0,504},{8,0},{16,8},{24,16},{32,24},{40,32},{48,40},{56,48},{64,5... | collective-permute-start | bytes 270344 | tf_op jit(solution)/shard_map/ppermute | solution.py:46
  14.4 1.0 %fusion.45 = (s32[1,2048]{1,0:T(1,128)S(1)}, s32[1,2048]{1,0:T(1,128)S(1)}, s32[1,2048]{1,0:T(1,128)S(1)}, s32[1,2048]{1,0:T(1,128)S(1)}) fusion(s32[4,2048]{1,0:T(4,128)} %param.15), kind=kLoop, calls=%fused_computation.74 | loop fusion | bytes 65536 | tf_op jit(solution)/shard_map/slice | solution.py:80
  15.4 0.9 %fusion.46 = (f32[1,2048]{1,0:T(1,128)S(1)}, f32[1,2048]{1,0:T(1,128)S(1)}, f32[1,2048]{1,0:T(1,128)S(1)}, f32[1,2048]{1,0:T(1,128)S(1)}) fusion(f32[4,2048]{1,0:T(4,128)} %param.16), kind=kLoop, calls=%fused_computation.75 | loop fusion | bytes 65536 | tf_op jit(solution)/shard_map/slice | solution.py:80
  16.4 0.8 %select_add_fusion = f32[256,2048]{1,0:T(8,128)S(1)} fusion(f32[2048]{0:T(1024)S(1)} %bitcast.29, s32[2048]{0:T(1024)S(1)} %bitcast.25, f32[2048]{0:T(1024)S(1)} %bitcast.30, s32[2048]{0:T(1024)S(1)} %bitcast.26, f32[2048]{0:T(1024)S(1)} %bitcast.28, s32[2048]{0:T(1024)S(1)} %bitcast.24, f32[2048]{0:T(1024)S(1)} %bitcast.27, s32[2048]{0:T(1024)S(1)} %bitcast.23), kind=kLoop, calls=%fused_computation.8 | loop fusion | flops 5767168 | bytes 2162688 | tf_op jit(solution)/shard_map/add | solution.py:80
  17.1 0.0 copy-start.3
  17.2 0.0 collective-permute-done
  17.2 0.0 collective-permute-done.1
  17.2 0.0 copy-done
  17.3 0.0 copy-done.8
  17.3 1.1 %fusion = f32[264,9,256]{2,0,1:T(8,128)S(1)} fusion(s32[9,256]{1,0:T(8,128)S(1)} %copy-done.8, bf16[88,512]{1,0:T(8,128)(2,1)S(1)} %get-tuple-element.8, bf16[88,512]{1,0:T(8,128)(2,1)S(1)} %get-tuple-element.7, bf16[88,512]{1,0:T(8,128)(2,1)S(1)} %get-tuple-element.6), kind=kOutput, calls=%fused_computation.1 | convolution fusion | flops 624844800 | bytes 2712576 | tf_op jit(solution)/shard_map/dot_general | solution.py:20
  18.3 0.0 copy-done.3
  18.4 0.0 copy-start.1
  18.4 0.0 copy-start.2
  18.4 0.0 copy-start.7
  18.4 0.0 copy-start.5
  18.4 0.0 copy-start.6
  18.4 0.2 fusion.19
  18.6 0.5 copy-done.1
  19.1 0.0 copy-done.2
  19.1 0.0 copy-done.7
  19.1 1.4 %fusion.6 = f32[2048]{0:T(1024)S(1)} fusion(f32[256,2048]{1,0:T(8,128)S(1)} %select_add_fusion, f32[2048]{0:T(1024)S(1)} %copy-done.1, s32[2048]{0:T(1024)S(1)} %copy-done.2, s32[88]{0:T(128)S(1)} %get-tuple-element.23, s32[88]{0:T(128)S(1)} %get-tuple-element.22, f32[88,256]{1,0:T(8,128)S(1)} %fusion.19, f32[88]{0:T(128)S(1)} %copy-done.7), kind=kOutput, calls=%fused_computation.14 | convolution fusion | flops 554749952 | bytes 2212896 | tf_op jit(solution)/shard_map/dot_general | solution.py:88
  20.5 7.2 %psum.7 = f32[2048]{0:T(1024)S(1)} all-reduce(f32[2048]{0:T(1024)S(1)} %fusion.6), channel_id=1, replica_groups=mesh['ang'=64,'zhi'=4,'core'=2] {'core'}, use_global_device_ids=true, to_apply=%region_2.3 | all-reduce | flops 2048 | bytes 16384 | tf_op jit(solution)/shard_map/psum | solution.py:90
  27.7 7.1 %collective-permute-start.2 = (f32[2048]{0:T(1024)S(1)}, f32[2048]{0:T(1024)S(1)}, u32[]{:S(2)}, u32[]{:S(2)}) collective-permute-start(f32[2048]{0:T(1024)S(1)} %psum.7), channel_id=1, source_target_pairs={{0,6},{2,0},{4,2},{6,4},{1,7},{3,1},{5,3},{7,5},{8,14},{10,8},{12,... | collective-permute-start | bytes 24584 | tf_op jit(solution)/shard_map/ppermute | solution.py:46
  34.8 2.1 %collective-permute-start.4 = (f32[2048]{0:T(1024)S(1)}, f32[2048]{0:T(1024)S(1)}, u32[]{:S(2)}, u32[]{:S(2)}) collective-permute-start(f32[2048]{0:T(1024)S(1)} %psum.7), channel_id=1, source_target_pairs={{0,2},{2,4},{4,6},{6,0},{1,3},{3,5},{5,7},{7,1},{8,10},{10,12},{12... | collective-permute-start | bytes 24584 | tf_op jit(solution)/shard_map/ppermute | solution.py:46
  36.9 0.0 collective-permute-done.2
  36.9 7.1 %collective-permute-start.3 = (f32[2048]{0:T(1024)S(1)}, f32[2048]{0:T(1024)S(1)}, u32[]{:S(2)}, u32[]{:S(2)}) collective-permute-start(f32[2048]{0:T(1024)S(1)} %collective-permute-done.2), channel_id=1, source_target_pairs={{0,6},{2,0},{4,2},{6,4},{1,7},{3,1},{5,3},{7,5},{8,14},{10,8},{12,... | collective-permute-start | bytes 24584 | tf_op jit(solution)/shard_map/ppermute | solution.py:46
  44.1 0.0 collective-permute-done.4
  44.1 1.2 %collective-permute-done.3 = f32[2048]{0:T(1024)S(1)} collective-permute-done((f32[2048]{0:T(1024)S(1)}, f32[2048]{0:T(1024)S(1)}, u32[]{:S(2)}, u32[]{:S(2)}) %collective-permute-start.3) | collective-permute-done | bytes 8224 | tf_op jit(solution)/shard_map/ppermute | solution.py:46
  45.2 0.1 concatenate.19
  45.4 0.0 copy-done.5
  45.4 0.0 copy-done.6
  45.4 0.0 copy-start.4
  45.4 2.1 %convolution_multiply_fusion.1 = f32[88,256]{1,0:T(8,128)S(1)} fusion(f32[256,2048]{1,0:T(8,128)S(1)} %select_add_fusion, f32[2048]{0:T(1024)S(1)} %multiply_divide_fusion, f32[2048]{0:T(1024)S(1)} %copy-done.1, s32[2048]{0:T(1024)S(1)} %copy-done.2, s32[88]{0:T(128)S(1)} %get-tuple-element.23, s32[88]{0:T(128)S(1)} %get-tuple-element.22, ...), kind=kOutput, calls=%fused_computation.25 | convolution fusion | flops 554594304 | bytes 2303008 | tf_op jit(solution)/shard_map/dot_general | solution.py:94
  47.5 0.2 reduce-precision_convert_fusion.1
  47.8 0.6 %fusion.14 = f32[264,256]{1,0:T(8,128)S(1)} fusion(s32[9,256]{1,0:T(8,128)S(1)} %copy-done.8, s32[256]{0:T(256)S(1)} %fusion.38, bf16[88,9,256]{2,0,1:T(8,128)(2,1)S(1)} %get-tuple-element.11, bf16[88,9,256]{2,0,1:T(8,128)(2,1)S(1)} %get-tuple-element.10, bf16[88,9,256]{2,0,1:T(8,128)(2,1)S(1)} %get-tuple-element.9), kind=kOutput, calls=%fused_computation.20 | convolution fusion | flops 315666432 | bytes 1497088 | tf_op jit(solution)/shard_map/dot_general | solution.py:26
  48.4 0.0 copy-done.4
  48.5 1.9 %collective-permute-start.5 = (f32[88,128]{1,0:T(8,128)S(1)}, f32[88,128]{1,0:T(8,128)S(1)}, u32[]{:S(2)}, u32[]{:S(2)}) collective-permute-start(f32[88,128]{1,0:T(8,128)S(1)} %get-tuple-element.4), channel_id=1, source_target_pairs={{0,8},{8,16},{16,24},{24,32},{32,40},{40,48},{48,56},{56,64},{64,7... | collective-permute-start | bytes 135176 | tf_op jit(solution)/shard_map/ppermute | solution.py:46
  50.4 9.6 %collective-permute-start.6 = (f32[88,128]{1,0:T(8,128)S(1)}, f32[88,128]{1,0:T(8,128)S(1)}, u32[]{:S(2)}, u32[]{:S(2)}) collective-permute-start(f32[88,128]{1,0:T(8,128)S(1)} %get-tuple-element.5), channel_id=1, source_target_pairs={{0,504},{8,0},{16,8},{24,16},{32,24},{40,32},{48,40},{56,48},{64,5... | collective-permute-start | bytes 135176 | tf_op jit(solution)/shard_map/ppermute | solution.py:46
  60.0 0.6 %fusion.11 = f32[264,256]{1,0:T(8,128)S(1)} fusion(s32[9,256]{1,0:T(8,128)S(1)} %copy-done.8, s32[256]{0:T(256)S(1)} %iota_add_fusion, bf16[88,9,256]{2,0,1:T(8,128)(2,1)S(1)} %get-tuple-element.11, bf16[88,9,256]{2,0,1:T(8,128)(2,1)S(1)} %get-tuple-element.10, bf16[88,9,256]{2,0,1:T(8,128)(2,1)S(1)} %get-tuple-element.9), kind=kOutput, calls=%fused_computation.19 | convolution fusion | flops 315666432 | bytes 1497088 | tf_op jit(solution)/shard_map/dot_general | solution.py:26
  60.7 0.0 collective-permute-done.5
  60.7 0.5 collective-permute-done.6
  61.1 0.7 %fusion.36 = f32[88,256]{1,0:T(8,128)} fusion(f32[264,256]{1,0:T(8,128)S(1)} %fusion.11, f32[88,128]{1,0:T(8,128)S(1)} %collective-permute-done.6, f32[88,128]{1,0:T(8,128)S(1)} %collective-permute-done.5), kind=kLoop, calls=%fused_computation.57 | loop fusion | flops 90112 | bytes 450560 | tf_op jit(solution)/shard_map/add | solution.py:112
  (10 shorter events, 0.1 us)
Async XLA Ops:
  0.6 16.6 %copy-start = (f32[88,256]{1,0:T(8,128)S(1)}, f32[88,256]{1,0:T(8,128)}, u32[]{:S(2)}) copy-start(f32[88,256]{1,0:T(8,128)} %param.10) | copy-start | bytes 270340
  0.6 16.6 %copy-start.8 = (s32[9,256]{1,0:T(8,128)S(1)}, s32[9,256]{1,0:T(8,128)}, u32[]{:S(2)}) copy-start(s32[9,256]{1,0:T(8,128)} %param.13) | copy-start | bytes 27652
  0.6 16.5 %collective-permute-start = (f32[88,256]{1,0:T(8,128)}, f32[88,256]{1,0:T(8,128)S(1)}, u32[]{:S(2)}, u32[]{:S(2)}) collective-permute-start(f32[88,256]{1,0:T(8,128)} %param.10), channel_id=1, source_target_pairs={{0,8},{8,16},{16,24},{24,32},{32,40},{40,48},{48,56},{56,64},{64,7... | collective-permute-start | bytes 270344 | tf_op jit(solution)/shard_map/ppermute | solution.py:46
  4.8 12.4 %collective-permute-start.1 = (f32[88,256]{1,0:T(8,128)}, f32[88,256]{1,0:T(8,128)S(1)}, u32[]{:S(2)}, u32[]{:S(2)}) collective-permute-start(f32[88,256]{1,0:T(8,128)} %param.10), channel_id=1, source_target_pairs={{0,504},{8,0},{16,8},{24,16},{32,24},{40,32},{48,40},{56,48},{64,5... | collective-permute-start | bytes 270344 | tf_op jit(solution)/shard_map/ppermute | solution.py:46
  17.1 1.2 %copy-start.3 = (f32[88,9]{0,1:T(8,128)S(1)}, f32[88,9]{0,1:T(8,128)}, u32[]{:S(2)}) copy-start(f32[88,9]{0,1:T(8,128)} %param.11) | copy-start | bytes 9508
  18.4 0.7 %copy-start.1 = (f32[2048]{0:T(1024)S(1)}, f32[2048]{0:T(1024)}, u32[]{:S(2)}) copy-start(f32[2048]{0:T(1024)} %param.17) | copy-start | bytes 24580
  18.4 0.7 %copy-start.2 = (s32[2048]{0:T(1024)S(1)}, s32[2048]{0:T(1024)}, u32[]{:S(2)}) copy-start(s32[2048]{0:T(1024)} %param.14) | copy-start | bytes 24580
  18.4 0.7 %copy-start.7 = (f32[88]{0:T(128)S(1)}, f32[88]{0:T(128)}, u32[]{:S(2)}) copy-start(f32[88]{0:T(128)} %param.12) | copy-start | bytes 1060
  18.4 27.0 %copy-start.5 = (f32[2048]{0:T(1024)S(1)}, f32[2048]{0:T(1024)}, u32[]{:S(2)}) copy-start(f32[2048]{0:T(1024)} %param.19) | copy-start | bytes 24580
  18.4 27.0 %copy-start.6 = (f32[2048]{0:T(1024)S(1)}, f32[2048]{0:T(1024)}, u32[]{:S(2)}) copy-start(f32[2048]{0:T(1024)} %param.18) | copy-start | bytes 24580
  27.7 9.2 %collective-permute-start.2 = (f32[2048]{0:T(1024)S(1)}, f32[2048]{0:T(1024)S(1)}, u32[]{:S(2)}, u32[]{:S(2)}) collective-permute-start(f32[2048]{0:T(1024)S(1)} %psum.7), channel_id=1, source_target_pairs={{0,6},{2,0},{4,2},{6,4},{1,7},{3,1},{5,3},{7,5},{8,14},{10,8},{12,... | collective-permute-start | bytes 24584 | tf_op jit(solution)/shard_map/ppermute | solution.py:46
  34.8 9.2 %collective-permute-start.4 = (f32[2048]{0:T(1024)S(1)}, f32[2048]{0:T(1024)S(1)}, u32[]{:S(2)}, u32[]{:S(2)}) collective-permute-start(f32[2048]{0:T(1024)S(1)} %psum.7), channel_id=1, source_target_pairs={{0,2},{2,4},{4,6},{6,0},{1,3},{3,5},{5,7},{7,1},{8,10},{10,12},{12... | collective-permute-start | bytes 24584 | tf_op jit(solution)/shard_map/ppermute | solution.py:46
  36.9 8.3 %collective-permute-start.3 = (f32[2048]{0:T(1024)S(1)}, f32[2048]{0:T(1024)S(1)}, u32[]{:S(2)}, u32[]{:S(2)}) collective-permute-start(f32[2048]{0:T(1024)S(1)} %collective-permute-done.2), channel_id=1, source_target_pairs={{0,6},{2,0},{4,2},{6,4},{1,7},{3,1},{5,3},{7,5},{8,14},{10,8},{12,... | collective-permute-start | bytes 24584 | tf_op jit(solution)/shard_map/ppermute | solution.py:46
  45.4 3.0 %copy-start.4 = (f32[2048]{0:T(1024)}, f32[2048]{0:T(1024)S(1)}, u32[]{:S(2)}) copy-start(f32[2048]{0:T(1024)S(1)} %dynamic-slice_reduce_fusion) | copy-start | bytes 24580
  48.5 12.2 %collective-permute-start.5 = (f32[88,128]{1,0:T(8,128)S(1)}, f32[88,128]{1,0:T(8,128)S(1)}, u32[]{:S(2)}, u32[]{:S(2)}) collective-permute-start(f32[88,128]{1,0:T(8,128)S(1)} %get-tuple-element.4), channel_id=1, source_target_pairs={{0,8},{8,16},{16,24},{24,32},{32,40},{40,48},{48,56},{56,64},{64,7... | collective-permute-start | bytes 135176 | tf_op jit(solution)/shard_map/ppermute | solution.py:46
  50.4 10.7 %collective-permute-start.6 = (f32[88,128]{1,0:T(8,128)S(1)}, f32[88,128]{1,0:T(8,128)S(1)}, u32[]{:S(2)}, u32[]{:S(2)}) collective-permute-start(f32[88,128]{1,0:T(8,128)S(1)} %get-tuple-element.5), channel_id=1, source_target_pairs={{0,504},{8,0},{16,8},{24,16},{32,24},{40,32},{48,40},{56,48},{64,5... | collective-permute-start | bytes 135176 | tf_op jit(solution)/shard_map/ppermute | solution.py:46

commit v20 on v15

--- a/solution.py
+++ b/solution.py
@@ -84,8 +84,7 @@
 
     at_stars = jnp.dot(weighted, spread, precision=HIGHEST, preferred_element_type=jnp.float32)
     partial_value = jnp.sum(radial * at_stars, axis=0)
-    pair = lax.psum(partial_value, "core")
-    predicted = chip_sum(pair, "zhi")
+    predicted = lax.psum(chip_sum(partial_value, "zhi"), "core")
     weight_back = (predicted - observed) / (sigma * sigma)
 
     adjoint_sum = lax.dot_general(

time: 62.2 us -> 63.4 us (1.019)
  starting transfers between devices: 41.9 us -> 45.8 us
  blocking collectives: 7.3 us -> 5.34 us
    ppermute x7, starting transfers between devices: 41.9 us -> 45.8 us  [ring(): lax.ppermute(value, axis, [(i, (i + step) % count) for i in range(count)])]
    psum x1, blocking collectives: 7.3 us -> 5.34 us  [on_device(): predicted = lax.psum(chip_sum(partial_value, 'zhi'), 'core')]
where the time goes in v20:
time: 63.4 us; the launch traced here: 63 us
  starting transfers between devices  45.8 us (72%)
  matrix products  5.82 us (9%)
  blocking collectives  5.34 us (8%)
  other arithmetic  3.48 us (5%)
  waiting for transfers between devices  1.46 us (2%)
  between operations  1 us (2%)
    ppermute x7, starting transfers between devices, ring(): lax.ppermute(value, axis, [(i, (i + step) % count) for i in range(count)])  45.8 us
    psum x1, blocking collectives, on_device(): predicted = lax.psum(chip_sum(partial_value, 'zhi'), 'core')  5.34 us
    reduce_sum x1, other arithmetic, on_device(): jnp.sum(jnp.where(pixel_id[None] == star_pixels[:, None, :], star_weights...  2.28 us
    dot_general x1, matrix products, on_device(): lax.dot_general(radial * weight_back[None, :], spread, (((1,), (1,)), (()...  2.06 us
    ppermute x7, waiting for transfers between devices, ring(): lax.ppermute(value, axis, [(i, (i + step) % count) for i in range(count)])  1.46 us
    dot_general x1, matrix products, on_device(): jnp.dot(weighted, spread, precision=HIGHEST, preferred_element_type=jnp.f...  1.4 us
    dot_general x2, matrix products, spread_select(): lax.dot_general(split3(value), onehot, (((1, 2), (1, 2)), ((), ())), pref...  1.29 us
  transfers between devices with their start and end apart: 7, of which 2 were waited for; matrix products, arithmetic and copies ran while one was open for 5% of the time, Pallas kernels for 0%

profile of v20, /device:TPU:1, one launch (start us, length us, event | category | flops | bytes accessed | tf_op | source)
XLA Modules:
  0.0 63.0 jit_solution(16191173354837919714)
XLA Ops:
  0.6 0.0 copy-start
  0.6 0.0 copy-start.8
  0.7 4.2 %collective-permute-start = (f32[88,256]{1,0:T(8,128)}, f32[88,256]{1,0:T(8,128)S(1)}, u32[]{:S(2)}, u32[]{:S(2)}) collective-permute-start(f32[88,256]{1,0:T(8,128)} %param.10), channel_id=1, source_target_pairs={{0,8},{8,16},{16,24},{24,32},{32,40},{40,48},{48,56},{56,64},{64,7... | collective-permute-start | bytes 270344 | tf_op jit(solution)/shard_map/ppermute | solution.py:46
  4.8 9.6 %collective-permute-start.1 = (f32[88,256]{1,0:T(8,128)}, f32[88,256]{1,0:T(8,128)S(1)}, u32[]{:S(2)}, u32[]{:S(2)}) collective-permute-start(f32[88,256]{1,0:T(8,128)} %param.10), channel_id=1, source_target_pairs={{0,504},{8,0},{16,8},{24,16},{32,24},{40,32},{48,40},{56,48},{64,5... | collective-permute-start | bytes 270344 | tf_op jit(solution)/shard_map/ppermute | solution.py:46
  14.5 2.3 %select_reduce_fusion = f32[256,2048]{1,0:T(8,128)S(1)} fusion(f32[4,2048]{1,0:T(4,128)} %param.16, s32[4,2048]{1,0:T(4,128)} %param.15), kind=kLoop, calls=%fused_computation | loop fusion | flops 5767168 | bytes 2162688 | tf_op jit(solution)/shard_map/reduce_sum | solution.py:78
  16.7 0.0 copy-start.3
  16.8 0.0 collective-permute-done
  16.8 0.0 collective-permute-done.1
  16.8 0.0 copy-done
  16.9 0.0 copy-done.8
  16.9 0.0 copy-start.1
  16.9 0.0 copy-start.2
  16.9 0.0 copy-start.7
  16.9 1.1 %fusion = f32[264,9,256]{2,0,1:T(8,128)S(1)} fusion(s32[9,256]{1,0:T(8,128)S(1)} %copy-done.8, bf16[88,512]{1,0:T(8,128)(2,1)S(1)} %get-tuple-element.8, bf16[88,512]{1,0:T(8,128)(2,1)S(1)} %get-tuple-element.7, bf16[88,512]{1,0:T(8,128)(2,1)S(1)} %get-tuple-element.6), kind=kOutput, calls=%fused_computation.3 | convolution fusion | flops 624844800 | bytes 2712576 | tf_op jit(solution)/shard_map/dot_general | solution.py:20
  18.0 0.0 copy-done.3
  18.0 0.0 copy-start.5
  18.0 0.0 copy-start.6
  18.0 0.2 fusion.19
  18.2 0.0 copy-done.1
  18.2 0.0 copy-done.2
  18.2 0.0 copy-done.7
  18.2 1.4 %fusion.6 = f32[2048]{0:T(1024)S(1)} fusion(f32[256,2048]{1,0:T(8,128)S(1)} %select_reduce_fusion, f32[2048]{0:T(1024)S(1)} %copy-done.1, s32[2048]{0:T(1024)S(1)} %copy-done.2, s32[88]{0:T(128)S(1)} %get-tuple-element.15, s32[88]{0:T(128)S(1)} %get-tuple-element.14, f32[88,256]{1,0:T(8,128)S(1)} %fusion.19, f32[88]{0:T(128)S(1)} %copy-done.7), kind=kOutput, calls=%fused_computation.11 | convolution fusion | flops 554749952 | bytes 2212896 | tf_op jit(solution)/shard_map/dot_general | solution.py:85
  19.6 10.9 %collective-permute-start.2 = (f32[2048]{0:T(1024)S(1)}, f32[2048]{0:T(1024)S(1)}, u32[]{:S(2)}, u32[]{:S(2)}) collective-permute-start(f32[2048]{0:T(1024)S(1)} %fusion.6), channel_id=1, source_target_pairs={{0,6},{2,0},{4,2},{6,4},{1,7},{3,1},{5,3},{7,5},{8,14},{10,8},{12,... | collective-permute-start | bytes 24584 | tf_op jit(solution)/shard_map/ppermute | solution.py:46
  30.6 1.9 %collective-permute-start.4 = (f32[2048]{0:T(1024)S(1)}, f32[2048]{0:T(1024)S(1)}, u32[]{:S(2)}, u32[]{:S(2)}) collective-permute-start(f32[2048]{0:T(1024)S(1)} %fusion.6), channel_id=1, source_target_pairs={{0,2},{2,4},{4,6},{6,0},{1,3},{3,5},{5,7},{7,1},{8,10},{10,12},{12... | collective-permute-start | bytes 24584 | tf_op jit(solution)/shard_map/ppermute | solution.py:46
  32.5 0.0 collective-permute-done.2
  32.5 7.3 %collective-permute-start.3 = (f32[2048]{0:T(1024)S(1)}, f32[2048]{0:T(1024)S(1)}, u32[]{:S(2)}, u32[]{:S(2)}) collective-permute-start(f32[2048]{0:T(1024)S(1)} %collective-permute-done.2), channel_id=1, source_target_pairs={{0,6},{2,0},{4,2},{6,4},{1,7},{3,1},{5,3},{7,5},{8,14},{10,8},{12,... | collective-permute-start | bytes 24584 | tf_op jit(solution)/shard_map/ppermute | solution.py:46
  39.8 0.0 collective-permute-done.4
  39.9 1.0 %collective-permute-done.3 = f32[2048]{0:T(1024)S(1)} collective-permute-done((f32[2048]{0:T(1024)S(1)}, f32[2048]{0:T(1024)S(1)}, u32[]{:S(2)}, u32[]{:S(2)}) %collective-permute-start.3) | collective-permute-done | bytes 8224 | tf_op jit(solution)/shard_map/ppermute | solution.py:46
  40.8 0.1 concatenate.19
  41.0 5.3 %psum.7 = f32[2048]{0:T(1024)S(1)} all-reduce(f32[2048]{0:T(1024)S(1)} %dynamic-slice_reduce_fusion), channel_id=1, replica_groups=mesh['ang'=64,'zhi'=4,'core'=2] {'core'}, use_global_device_ids=true, to_apply=%region_4.5 | all-reduce | flops 2048 | bytes 16384 | tf_op jit(solution)/shard_map/psum | solution.py:87
  46.3 0.0 copy-done.5
  46.3 0.0 copy-done.6
  46.3 0.0 copy-start.4
  46.4 2.1 %convolution_multiply_fusion.1 = f32[88,256]{1,0:T(8,128)S(1)} fusion(f32[256,2048]{1,0:T(8,128)S(1)} %select_reduce_fusion, f32[2048]{0:T(1024)S(1)} %multiply_divide_fusion, f32[2048]{0:T(1024)S(1)} %copy-done.1, s32[2048]{0:T(1024)S(1)} %copy-done.2, s32[88]{0:T(128)S(1)} %get-tuple-element.15, s32[88]{0:T(128)S(1)} %get-tuple-element.14, ...), kind=kOutput, calls=%fused_computation.22 | convolution fusion | flops 554594304 | bytes 2303008 | tf_op jit(solution)/shard_map/dot_general | solution.py:90
  48.4 0.2 reduce-precision_convert_fusion.1
  48.7 0.6 %fusion.14 = f32[264,256]{1,0:T(8,128)S(1)} fusion(s32[9,256]{1,0:T(8,128)S(1)} %copy-done.8, s32[256]{0:T(256)S(1)} %fusion.38, bf16[88,9,256]{2,0,1:T(8,128)(2,1)S(1)} %get-tuple-element.11, bf16[88,9,256]{2,0,1:T(8,128)(2,1)S(1)} %get-tuple-element.10, bf16[88,9,256]{2,0,1:T(8,128)(2,1)S(1)} %get-tuple-element.9), kind=kOutput, calls=%fused_computation.17 | convolution fusion | flops 315666432 | bytes 1497088 | tf_op jit(solution)/shard_map/dot_general | solution.py:26
  49.3 0.0 copy-done.4
  49.4 1.9 %collective-permute-start.5 = (f32[88,128]{1,0:T(8,128)S(1)}, f32[88,128]{1,0:T(8,128)S(1)}, u32[]{:S(2)}, u32[]{:S(2)}) collective-permute-start(f32[88,128]{1,0:T(8,128)S(1)} %get-tuple-element.4), channel_id=1, source_target_pairs={{0,8},{8,16},{16,24},{24,32},{32,40},{40,48},{48,56},{56,64},{64,7... | collective-permute-start | bytes 135176 | tf_op jit(solution)/shard_map/ppermute | solution.py:46
  51.3 9.9 %collective-permute-start.6 = (f32[88,128]{1,0:T(8,128)S(1)}, f32[88,128]{1,0:T(8,128)S(1)}, u32[]{:S(2)}, u32[]{:S(2)}) collective-permute-start(f32[88,128]{1,0:T(8,128)S(1)} %get-tuple-element.5), channel_id=1, source_target_pairs={{0,504},{8,0},{16,8},{24,16},{32,24},{40,32},{48,40},{56,48},{64,5... | collective-permute-start | bytes 135176 | tf_op jit(solution)/shard_map/ppermute | solution.py:46
  61.3 0.6 %fusion.11 = f32[264,256]{1,0:T(8,128)S(1)} fusion(s32[9,256]{1,0:T(8,128)S(1)} %copy-done.8, s32[256]{0:T(256)S(1)} %iota_add_fusion, bf16[88,9,256]{2,0,1:T(8,128)(2,1)S(1)} %get-tuple-element.11, bf16[88,9,256]{2,0,1:T(8,128)(2,1)S(1)} %get-tuple-element.10, bf16[88,9,256]{2,0,1:T(8,128)(2,1)S(1)} %get-tuple-element.9), kind=kOutput, calls=%fused_computation.16 | convolution fusion | flops 315666432 | bytes 1497088 | tf_op jit(solution)/shard_map/dot_general | solution.py:26
  61.9 0.0 collective-permute-done.5
  61.9 0.5 collective-permute-done.6
  62.4 0.7 %fusion.36 = f32[88,256]{1,0:T(8,128)} fusion(f32[264,256]{1,0:T(8,128)S(1)} %fusion.11, f32[88,128]{1,0:T(8,128)S(1)} %collective-permute-done.6, f32[88,128]{1,0:T(8,128)S(1)} %collective-permute-done.5), kind=kLoop, calls=%fused_computation.54 | loop fusion | flops 90112 | bytes 450560 | tf_op jit(solution)/shard_map/add | solution.py:108
  (10 shorter events, 0.1 us)
Async XLA Ops:
  0.6 16.2 %copy-start = (f32[88,256]{1,0:T(8,128)S(1)}, f32[88,256]{1,0:T(8,128)}, u32[]{:S(2)}) copy-start(f32[88,256]{1,0:T(8,128)} %param.10) | copy-start | bytes 270340
  0.6 16.2 %copy-start.8 = (s32[9,256]{1,0:T(8,128)S(1)}, s32[9,256]{1,0:T(8,128)}, u32[]{:S(2)}) copy-start(s32[9,256]{1,0:T(8,128)} %param.13) | copy-start | bytes 27652
  0.7 16.1 %collective-permute-start = (f32[88,256]{1,0:T(8,128)}, f32[88,256]{1,0:T(8,128)S(1)}, u32[]{:S(2)}, u32[]{:S(2)}) collective-permute-start(f32[88,256]{1,0:T(8,128)} %param.10), channel_id=1, source_target_pairs={{0,8},{8,16},{16,24},{24,32},{32,40},{40,48},{48,56},{56,64},{64,7... | collective-permute-start | bytes 270344 | tf_op jit(solution)/shard_map/ppermute | solution.py:46
  4.8 12.0 %collective-permute-start.1 = (f32[88,256]{1,0:T(8,128)}, f32[88,256]{1,0:T(8,128)S(1)}, u32[]{:S(2)}, u32[]{:S(2)}) collective-permute-start(f32[88,256]{1,0:T(8,128)} %param.10), channel_id=1, source_target_pairs={{0,504},{8,0},{16,8},{24,16},{32,24},{40,32},{48,40},{56,48},{64,5... | collective-permute-start | bytes 270344 | tf_op jit(solution)/shard_map/ppermute | solution.py:46
  16.7 1.3 %copy-start.3 = (f32[88,9]{0,1:T(8,128)S(1)}, f32[88,9]{0,1:T(8,128)}, u32[]{:S(2)}) copy-start(f32[88,9]{0,1:T(8,128)} %param.11) | copy-start | bytes 9508
  16.9 1.3 %copy-start.1 = (f32[2048]{0:T(1024)S(1)}, f32[2048]{0:T(1024)}, u32[]{:S(2)}) copy-start(f32[2048]{0:T(1024)} %param.17) | copy-start | bytes 24580
  16.9 1.3 %copy-start.2 = (s32[2048]{0:T(1024)S(1)}, s32[2048]{0:T(1024)}, u32[]{:S(2)}) copy-start(s32[2048]{0:T(1024)} %param.14) | copy-start | bytes 24580
  16.9 1.3 %copy-start.7 = (f32[88]{0:T(128)S(1)}, f32[88]{0:T(128)}, u32[]{:S(2)}) copy-start(f32[88]{0:T(128)} %param.12) | copy-start | bytes 1060
  18.0 28.3 %copy-start.5 = (f32[2048]{0:T(1024)S(1)}, f32[2048]{0:T(1024)}, u32[]{:S(2)}) copy-start(f32[2048]{0:T(1024)} %param.19) | copy-start | bytes 24580
  18.0 28.3 %copy-start.6 = (f32[2048]{0:T(1024)S(1)}, f32[2048]{0:T(1024)}, u32[]{:S(2)}) copy-start(f32[2048]{0:T(1024)} %param.18) | copy-start | bytes 24580
  19.6 12.9 %collective-permute-start.2 = (f32[2048]{0:T(1024)S(1)}, f32[2048]{0:T(1024)S(1)}, u32[]{:S(2)}, u32[]{:S(2)}) collective-permute-start(f32[2048]{0:T(1024)S(1)} %fusion.6), channel_id=1, source_target_pairs={{0,6},{2,0},{4,2},{6,4},{1,7},{3,1},{5,3},{7,5},{8,14},{10,8},{12,... | collective-permute-start | bytes 24584 | tf_op jit(solution)/shard_map/ppermute | solution.py:46
  30.6 9.2 %collective-permute-start.4 = (f32[2048]{0:T(1024)S(1)}, f32[2048]{0:T(1024)S(1)}, u32[]{:S(2)}, u32[]{:S(2)}) collective-permute-start(f32[2048]{0:T(1024)S(1)} %fusion.6), channel_id=1, source_target_pairs={{0,2},{2,4},{4,6},{6,0},{1,3},{3,5},{5,7},{7,1},{8,10},{10,12},{12... | collective-permute-start | bytes 24584 | tf_op jit(solution)/shard_map/ppermute | solution.py:46
  32.5 8.3 %collective-permute-start.3 = (f32[2048]{0:T(1024)S(1)}, f32[2048]{0:T(1024)S(1)}, u32[]{:S(2)}, u32[]{:S(2)}) collective-permute-start(f32[2048]{0:T(1024)S(1)} %collective-permute-done.2), channel_id=1, source_target_pairs={{0,6},{2,0},{4,2},{6,4},{1,7},{3,1},{5,3},{7,5},{8,14},{10,8},{12,... | collective-permute-start | bytes 24584 | tf_op jit(solution)/shard_map/ppermute | solution.py:46
  46.3 3.0 %copy-start.4 = (f32[2048]{0:T(1024)}, f32[2048]{0:T(1024)S(1)}, u32[]{:S(2)}) copy-start(f32[2048]{0:T(1024)S(1)} %psum.7) | copy-start | bytes 24580
  49.4 12.5 %collective-permute-start.5 = (f32[88,128]{1,0:T(8,128)S(1)}, f32[88,128]{1,0:T(8,128)S(1)}, u32[]{:S(2)}, u32[]{:S(2)}) collective-permute-start(f32[88,128]{1,0:T(8,128)S(1)} %get-tuple-element.4), channel_id=1, source_target_pairs={{0,8},{8,16},{16,24},{24,32},{32,40},{40,48},{48,56},{56,64},{64,7... | collective-permute-start | bytes 135176 | tf_op jit(solution)/shard_map/ppermute | solution.py:46
  51.3 11.1 %collective-permute-start.6 = (f32[88,128]{1,0:T(8,128)S(1)}, f32[88,128]{1,0:T(8,128)S(1)}, u32[]{:S(2)}, u32[]{:S(2)}) collective-permute-start(f32[88,128]{1,0:T(8,128)S(1)} %get-tuple-element.5), channel_id=1, source_target_pairs={{0,504},{8,0},{16,8},{24,16},{32,24},{40,32},{48,40},{56,48},{64,5... | collective-permute-start | bytes 135176 | tf_op jit(solution)/shard_map/ppermute | solution.py:46
